TPU v7x, 32 devices: a whole 2x2x4 slice. The times are simulated.
32 devices in a mesh: chan: 2 (over core), sky: 16 (over z, y, x).
Axes of the slice: x: 2, y: 2, z: 4, core: 2. Of those that a mesh axis runs over, the one named last changes fastest.
Arguments:
- dirty: bfloat16 [4, 256, 2048], P('chan', None, 'sky'), may hold values from -6 to 6
- model: float32 [4, 256, 2048], P(None, 'chan', 'sky'), may hold values from -3 to 3
- spectral: float32 [4, 4], replicated, may hold values from 0.25 to 1.5
- psf_rows: float32 [4, 4, 129], replicated, may hold values from -0.5 to 0.5
- psf_cols: float32 [4, 4, 129], replicated, may hold values from -0.5 to 0.5
- strip_width: int32 [16], replicated, may hold values from 128 to 128, as said below
Outputs:
- residual: bfloat16 [4, 256, 2048], P('chan', None, 'sky')
- model_new: float32 [4, 256, 2048], P(None, 'chan', 'sky')
Inputs may be any that keep to these rules, and one draw needn't show every extreme that they name: `strip_width`: every strip has between 128 and 128 live columns, left-aligned in its slot; some strip has exactly 128 and some strip exactly 128.
All inputs are finite; a program needn't handle non-finite values.
Results may differ from a plain program's by a relative error of at most 0.0064.
Values may be sent and summed in bfloat16 or wider, within the bound.
No kernel may reach another device: no remote copies, remote signals or barrier semaphores. Data moves between devices by JAX's collectives and lax.ppermute only.
A program may use at most 64 MiB of HBM per device.

v0:
```python
import jax
import jax.numpy as jnp
from jax import lax
from jax.sharding import PartitionSpec as P

TAPS = 129


def from_behind(value, axis, steps):
    count = lax.axis_size(axis)
    first, last = (max(0, -steps), min(count, count - steps))
    return lax.ppermute(value, axis, [(source, source + steps) for source in range(first, last)])


def toeplitz(tap_table, count_a, count_b, offset):
    rank_count = tap_table.shape[0]
    padded_taps = jnp.pad(tap_table, ((0, 0), (count_a, count_a + count_b)))
    center = offset + count_a
    ahead = padded_taps[:, center : center + count_b]
    behind = padded_taps[:, center - count_a + 1 : center]
    spacer = jnp.zeros((rank_count, 1), tap_table.dtype)
    cyclic = jnp.concatenate([ahead, spacer, behind], axis=1)
    tiled = jnp.tile(cyclic, (1, count_a))
    skewed = tiled[:, : count_a * (count_a + count_b - 1)].reshape(
        rank_count, count_a, count_a + count_b - 1
    )
    return skewed[:, :, :count_b]


def with_rims(masked, live_count):
    half_reach = (TAPS - 1) // 2
    chan_count, row_count, slot_width = masked.shape
    tail_cols = lax.dynamic_slice_in_dim(masked, live_count - half_reach, half_reach, 2)
    left_rim = from_behind(tail_cols, "sky", 1)
    right_rim = from_behind(masked[:, :, :half_reach], "sky", -1)
    padded = jnp.concatenate(
        [left_rim, masked, jnp.zeros((chan_count, row_count, 2 * half_reach), masked.dtype)], axis=2
    )
    padded = lax.dynamic_update_slice_in_dim(padded, right_rim, half_reach + live_count, 2)
    return padded[:, :, : slot_width + 2 * half_reach]


def apply_psf(extended, row_band, col_band):
    col_pass = jnp.einsum(
        "yk,rjk->ryj", extended, col_band, preferred_element_type=jnp.float32
    ).astype(jnp.bfloat16)
    return jnp.einsum("ryk,rkj->yj", row_band, col_pass, preferred_element_type=jnp.float32)


def body(dirty, model, spectral, psf_rows, psf_cols, strip_width):
    local_chans, row_count, slot_width = dirty.shape
    half_reach = (TAPS - 1) // 2
    live_count = strip_width[lax.axis_index("sky")]
    live_cols = jnp.arange(slot_width) < live_count
    first_chan = lax.axis_index("chan") * local_chans
    spec_local = lax.dynamic_slice_in_dim(spectral, first_chan, local_chans, 0)
    rows_local = lax.dynamic_slice_in_dim(psf_rows, first_chan, local_chans, 0).astype(jnp.bfloat16)
    cols_local = lax.dynamic_slice_in_dim(psf_cols, first_chan, local_chans, 0).astype(jnp.bfloat16)
    model_piece = lax.all_gather(model, "chan", axis=1, tiled=True)
    sky_image = spec_local[:, 0][:, None, None] * model_piece[0][None]
    for basis_idx in range(1, model_piece.shape[0]):
        sky_image = (
            sky_image + spec_local[:, basis_idx][:, None, None] * model_piece[basis_idx][None]
        )
    sky_image = sky_image.astype(jnp.bfloat16)
    masked = jnp.where(live_cols[None, None, :], sky_image, jnp.zeros((), jnp.bfloat16))
    extended = with_rims(masked, live_count)
    predicted = []
    for chan_idx in range(local_chans):
        row_band = toeplitz(rows_local[chan_idx], row_count, row_count, half_reach)
        col_band = toeplitz(cols_local[chan_idx], slot_width, slot_width + 2 * half_reach, 0)
        predicted.append(apply_psf(extended[chan_idx], row_band, col_band))
    predicted = jnp.stack(predicted, axis=0)
    residual = jnp.where(
        live_cols[None, None, :], dirty.astype(jnp.float32) - predicted, 0.0
    ).astype(jnp.bfloat16)
    extended_res = with_rims(residual, live_count)
    partial_value = jnp.zeros((spectral.shape[1], row_count, slot_width), jnp.float32)
    for chan_idx in range(local_chans):
        row_band = toeplitz(rows_local[chan_idx][:, ::-1], row_count, row_count, half_reach)
        col_band = toeplitz(
            cols_local[chan_idx][:, ::-1], slot_width, slot_width + 2 * half_reach, 0
        )
        grad_chan = apply_psf(extended_res[chan_idx], row_band, col_band)
        grad_chan = jnp.where(live_cols[None, :], grad_chan, 0.0)
        partial_value = partial_value + spec_local[chan_idx][:, None, None] * grad_chan[None, :, :]
    grad_share = lax.psum_scatter(partial_value, "chan", scatter_dimension=1, tiled=True)
    gram_rows = jnp.einsum("crt,cst->crs", psf_rows, psf_rows, precision=lax.Precision.HIGHEST)
    gram_cols = jnp.einsum("crt,cst->crs", psf_cols, psf_cols, precision=lax.Precision.HIGHEST)
    energy = jnp.sum(gram_rows * gram_cols, axis=(1, 2))
    curvature = jnp.sum(spectral * spectral * energy[:, None], axis=0)
    model_new = jnp.where(
        live_cols[None, None, :], model + grad_share / curvature[:, None, None], 0.0
    )
    return (residual, model_new)


def solution(mesh):
    placed = (P("chan", None, "sky"), P(None, "chan", "sky"), P(), P(), P(), P())
    return jax.shard_map(
        body,
        mesh=mesh,
        in_specs=placed,
        out_specs=(P("chan", None, "sky"), P(None, "chan", "sky")),
        check_vma=False,
    )
```

profile of v0, /device:TPU:0, one launch (start us, length us, event | category | flops | bytes accessed | tf_op | source)
XLA Modules:
  0.0 99.4 jit_solution(13053449529080827944)
XLA Ops:
  10.4 2.5 %all_gather.3 = f32[4,256,128]{2,1,0:T(8,128)S(1)} all-gather(f32[4,128,128]{2,1,0:T(8,128)} %param.7), channel_id=1, replica_groups=mesh['chan'=2,'sky'=16] {'chan'}, dimensions={1}, use_global_device_ids=true | all-gather | bytes 786432 | tf_op jit(solution)/shard_map/all_gather | solution.py:59
  15.3 5.4 %collective-permute-start = (bf16[2,256,64]{1,2,0:T(8,128)(2,1)}, bf16[2,256,64]{1,2,0:T(8,128)(2,1)}, u32[]{:S(2)}, u32[]{:S(2)}) collective-permute-start(bf16[2,256,64]{1,2,0:T(8,128)(2,1)} %get-tuple-element.17), channel_id=1, source_target_pairs={{0,1},{1,2},{2,3},{3,4},{4,5},{5,6},{6,7},{7,8},{8,9},{9,10},{10,1... | collective-permute-start | bytes 196616 | tf_op jit(solution)/shard_map/ppermute | solution.py:12
  20.7 1.3 %collective-permute-start.1 = (bf16[2,256,64]{1,2,0:T(8,128)(2,1)}, bf16[2,256,64]{1,2,0:T(8,128)(2,1)}, u32[]{:S(2)}, u32[]{:S(2)}) collective-permute-start(bf16[2,256,64]{1,2,0:T(8,128)(2,1)} %get-tuple-element.16), channel_id=1, source_target_pairs={{1,0},{2,1},{3,2},{4,3},{5,4},{6,5},{7,6},{8,7},{9,8},{10,9},{11,1... | collective-permute-start | bytes 196616 | tf_op jit(solution)/shard_map/ppermute | solution.py:12
  25.6 1.1 %broadcast_bitcast_fusion.2 = bf16[1,4,256,512]{3,2,1,0:T(8,128)(2,1)} fusion(bf16[4,512]{1,0:T(4,128)(2,1)S(1)} %get-tuple-element.29), kind=kLoop, calls=%fused_computation.27 | loop fusion | bytes 1052672
  29.0 0.8 copy.20
  30.2 2.8 %reshape.78 = bf16[4,256,511]{2,1,0:T(8,128)(2,1)} reshape(bf16[4,130816]{1,0:T(4,128)(2,1)S(1)} %slice.210) | data formatting | bytes 2093056 | tf_op jit(solution)/shard_map/reshape | solution.py:24
  32.9 1.4 %copy.21 = bf16[1,4,128,384]{3,1,2,0:T(4,128)(2,1)S(1)} copy(bf16[1,4,128,384]{3,2,1,0:T(8,128)(2,1)} %broadcast_bitcast_fusion.7) | data formatting | bytes 786432
  34.3 0.9 slice.213
  35.2 2.7 %reshape.79 = bf16[4,128,383]{2,1,0:T(8,128)(2,1)} reshape(bf16[4,49024]{1,0:T(4,128)(2,1)} %slice.213) | data formatting | bytes 784384 | tf_op jit(solution)/shard_map/reshape | solution.py:24
  37.8 0.8 copy.22
  39.0 2.8 %reshape.80 = bf16[4,256,511]{2,1,0:T(8,128)(2,1)} reshape(bf16[4,130816]{1,0:T(4,128)(2,1)S(1)} %slice.222) | data formatting | bytes 2093056 | tf_op jit(solution)/shard_map/reshape | solution.py:24
  41.8 1.3 %copy.23 = bf16[1,4,128,384]{3,1,2,0:T(4,128)(2,1)S(1)} copy(bf16[1,4,128,384]{3,2,1,0:T(8,128)(2,1)} %broadcast_bitcast_fusion.6) | data formatting | bytes 786432
  43.3 1.6 %reshape.81 = bf16[4,128,383]{2,1,0:T(8,128)(2,1)} reshape(bf16[4,49024]{1,0:T(4,128)(2,1)S(1)} %slice.225) | data formatting | bytes 784384 | tf_op jit(solution)/shard_map/reshape | solution.py:24
  45.1 0.9 copy-done.3
  45.9 1.6 %pad_maximum_fusion.1 = bf16[2,256,320]{1,2,0:T(8,128)(2,1)} fusion(bf16[2,256,128]{1,2,0:T(8,128)(2,1)S(1)} %broadcast_in_dim.60, bf16[2,256,128]{1,2,0:T(8,128)(2,1)S(1)} %copy-done.3, bf16[2,256,64]{1,2,0:T(8,128)(2,1)} %collective-permute-done), kind=kLoop, calls=%fused_computation.30 | loop fusion | flops 983040 | bytes 655360 | tf_op jit(solution)/shard_map/concatenate | solution.py:36
  47.6 1.6 %dynamic_update_slice.6 = bf16[2,256,320]{1,2,0:T(8,128)(2,1)} dynamic-update-slice(bf16[2,256,320]{1,2,0:T(8,128)(2,1)} %pad_maximum_fusion.1, bf16[2,256,64]{1,2,0:T(8,128)(2,1)} %collective-permute-done.1, s32[]{:T(128)} %constant.13.clone.1, s32[]{:T(128)} %constant.13.clone.1, s32[]{:T(128)S(6)} %select_n.39) | dynamic-update-slice | bytes 131076 | tf_op jit(solution)/shard_map/dynamic_update_slice | solution.py:39
  49.2 1.5 %fusion.11 = f32[1,256,128]{1,2,0:T(8,128)S(1)} fusion(bf16[4,256,511]{2,1,0:T(8,128)(2,1)} %reshape.78, bf16[4,128,383]{2,1,0:T(8,128)(2,1)S(1)} %copy-done.6, bf16[2,256,320]{1,2,0:T(8,128)(2,1)} %dynamic_update_slice.6), kind=kOutput, calls=%fused_computation.15 | convolution fusion | flops 134348800 | bytes 1048576 | tf_op jit(solution)/shard_map/ryk,rkj->yj/dot_general | solution.py:47
  50.7 1.6 %fusion.10 = f32[1,256,128]{1,2,0:T(8,128)S(1)} fusion(bf16[4,256,511]{2,1,0:T(8,128)(2,1)} %reshape.80, bf16[4,128,383]{2,1,0:T(8,128)(2,1)} %reshape.81, bf16[2,256,320]{1,2,0:T(8,128)(2,1)} %dynamic_update_slice.6), kind=kOutput, calls=%fused_computation.14 | convolution fusion | flops 134348800 | bytes 1048576 | tf_op jit(solution)/shard_map/ryk,rkj->yj/dot_general | solution.py:47
  53.1 5.3 %collective-permute-start.2 = (bf16[2,256,64]{1,2,0:T(8,128)(2,1)}, bf16[2,256,64]{1,2,0:T(8,128)(2,1)}, u32[]{:S(2)}, u32[]{:S(2)}) collective-permute-start(bf16[2,256,64]{1,2,0:T(8,128)(2,1)} %get-tuple-element.15), channel_id=1, source_target_pairs={{0,1},{1,2},{2,3},{3,4},{4,5},{5,6},{6,7},{7,8},{8,9},{9,10},{10,1... | collective-permute-start | bytes 196616 | tf_op jit(solution)/shard_map/ppermute | solution.py:12
  59.0 0.8 copy.24
  60.2 2.8 %reshape.82 = bf16[4,256,511]{2,1,0:T(8,128)(2,1)} reshape(bf16[4,130816]{1,0:T(4,128)(2,1)S(1)} %slice.228) | data formatting | bytes 2093056 | tf_op jit(solution)/shard_map/reshape | solution.py:24
  63.4 0.9 reshape.83
  64.3 0.8 copy.26
  65.5 2.8 %reshape.84 = bf16[4,256,511]{2,1,0:T(8,128)(2,1)} reshape(bf16[4,130816]{1,0:T(4,128)(2,1)S(1)} %slice.234) | data formatting | bytes 2093056 | tf_op jit(solution)/shard_map/reshape | solution.py:24
  68.7 0.9 reshape.85
  69.6 1.3 %collective-permute-start.3 = (bf16[2,256,64]{1,2,0:T(8,128)(2,1)S(1)}, bf16[2,256,64]{1,2,0:T(8,128)(2,1)S(1)}, u32[]{:S(2)}, u32[]{:S(2)}) collective-permute-start(bf16[2,256,64]{1,2,0:T(8,128)(2,1)S(1)} %copy-done.10), channel_id=1, source_target_pairs={{1,0},{2,1},{3,2},{4,3},{5,4},{6,5},{7,6},{8,7},{9,8},{10,9},{11,1... | collective-permute-start | bytes 196616 | tf_op jit(solution)/shard_map/ppermute | solution.py:12
  70.9 0.9 pad_maximum_fusion
  71.8 4.0 %collective-permute-done.3 = bf16[2,256,64]{1,2,0:T(8,128)(2,1)S(1)} collective-permute-done((bf16[2,256,64]{1,2,0:T(8,128)(2,1)S(1)}, bf16[2,256,64]{1,2,0:T(8,128)(2,1)S(1)}, u32[]{:S(2)}, u32[]{:S(2)}) %collective-permute-start.3) | collective-permute-done | bytes 65568 | tf_op jit(solution)/shard_map/ppermute | solution.py:12
  76.7 1.6 %fusion.13 = f32[256,128]{1,0:T(8,128)S(1)} fusion(bf16[4,256,511]{2,1,0:T(8,128)(2,1)} %reshape.84, bf16[4,128,383]{2,1,0:T(8,128)(2,1)S(1)} %reshape.85, bf16[2,256,320]{1,2,0:T(8,128)(2,1)S(1)} %dynamic_update_slice.7, pred[128]{0:T(512)(128)(4,1)S(1)} %copy-done.17), kind=kOutput, calls=%fused_computation.17 | convolution fusion | flops 134381568 | bytes 1049088 | tf_op jit(solution)/shard_map/ryk,rkj->yj/dot_general | solution.py:47
  78.9 0.9 multiply_add_fusion
  81.7 9.1 %reduce-scatter.2.cloned.1.call-done = f32[4,128,128]{2,1,0:T(8,128)} async-done(((f32[4,256,128]{2,1,0:T(8,128)}), f32[4,128,128]{2,1,0:T(8,128)}) %reduce-scatter.2.cloned.1.call-update) | async-done | bytes 262160 | tf_op jit(solution)/shard_map/reduce_scatter | solution.py:87
  90.8 1.8 %add_select_fusion = f32[4,128,128]{2,1,0:T(8,128)} fusion(f32[4,128,128]{2,1,0:T(8,128)S(1)} %copy-done.5, f32[4,128,128]{2,1,0:T(8,128)} %reduce-scatter.2.cloned.1.call-done, f32[4]{0:T(128)S(1)} %multiply_reduce_fusion, pred[128]{0:T(512)(128)(4,1)S(1)} %copy-done.17), kind=kLoop, calls=%fused_computation.38 | loop fusion | flops 196608 | bytes 786576 | tf_op jit(solution)/shard_map/jit(_where)/select_n | solution.py:92
  (112 shorter events, 17.0 us)
Async XLA Ops:
  7.2 83.6 %reduce-scatter.2.cloned.1.call-start = ((), (), s32[]{:S(2)}) async-start(), calls=%async_computation.1 | async-start | bytes 786432 | tf_op jit(solution)/shard_map/reduce_scatter | solution.py:87
  7.2 0.7 copy-start.20
  9.0 5.5 %copy-start.15 = (pred[128]{0:T(512)(128)(4,1)}, pred[128]{0:T(512)(128)(4,1)S(1)}, u32[]{:S(2)}) copy-start(pred[128]{0:T(512)(128)(4,1)S(1)} %iota_compare_fusion) | copy-start | bytes 388
  9.0 0.7 copy-start.13
  9.7 0.5 copy-start.11
  14.6 0.7 copy-start.2
  14.6 7.4 %copy-start.8 = (f32[4,4,129]{2,1,0:T(4,128)S(1)}, f32[4,4,129]{2,1,0:T(4,128)}, u32[]{:S(2)}) copy-start(f32[4,4,129]{2,1,0:T(4,128)} %param.9) | copy-start | bytes 24772
  15.3 29.7 %collective-permute-start = (bf16[2,256,64]{1,2,0:T(8,128)(2,1)}, bf16[2,256,64]{1,2,0:T(8,128)(2,1)}, u32[]{:S(2)}, u32[]{:S(2)}) collective-permute-start(bf16[2,256,64]{1,2,0:T(8,128)(2,1)} %get-tuple-element.17), channel_id=1, source_target_pairs={{0,1},{1,2},{2,3},{3,4},{4,5},{5,6},{6,7},{7,8},{8,9},{9,10},{10,1... | collective-permute-start | bytes 196616 | tf_op jit(solution)/shard_map/ppermute | solution.py:12
  20.7 26.9 %collective-permute-start.1 = (bf16[2,256,64]{1,2,0:T(8,128)(2,1)}, bf16[2,256,64]{1,2,0:T(8,128)(2,1)}, u32[]{:S(2)}, u32[]{:S(2)}) collective-permute-start(bf16[2,256,64]{1,2,0:T(8,128)(2,1)} %get-tuple-element.16), channel_id=1, source_target_pairs={{1,0},{2,1},{3,2},{4,3},{5,4},{6,5},{7,6},{8,7},{9,8},{10,9},{11,1... | collective-permute-start | bytes 196616 | tf_op jit(solution)/shard_map/ppermute | solution.py:12
  32.9 4.9 %copy-start = (bf16[1,4,256,512]{3,2,1,0:T(8,128)(2,1)S(1)}, bf16[1,4,256,512]{3,2,1,0:T(8,128)(2,1)}, u32[]{:S(2)}) copy-start(bf16[1,4,256,512]{3,2,1,0:T(8,128)(2,1)} %broadcast_bitcast_fusion.2) | copy-start | bytes 3145732
  43.2 1.7 %copy-start.7 = (bf16[2,256,128]{2,1,0:T(8,128)(2,1)S(1)}, bf16[2,256,128]{2,1,0:T(8,128)(2,1)}, u32[]{:S(2)}) copy-start(bf16[2,256,128]{2,1,0:T(8,128)(2,1)} %param.6) | copy-start | bytes 393220
  45.0 0.9 copy-start.3
  45.9 3.3 %copy-start.6 = (bf16[4,128,383]{2,1,0:T(8,128)(2,1)S(1)}, bf16[4,128,383]{2,1,0:T(8,128)(2,1)}, u32[]{:S(2)}) copy-start(bf16[4,128,383]{2,1,0:T(8,128)(2,1)} %reshape.79) | copy-start | bytes 1176580
  50.7 1.6 %copy-start.16 = (pred[128]{0:T(512)(128)(4,1)S(1)}, pred[128]{0:T(512)(128)(4,1)}, u32[]{:S(2)}) copy-start(pred[128]{0:T(512)(128)(4,1)} %copy-done.15) | copy-start | bytes 388
  53.1 5.3 %copy-start.12 = (f32[2,4]{1,0:T(2,128)S(1)}, f32[2,4]{1,0:T(2,128)}, u32[]{:S(2)}) copy-start(f32[2,4]{1,0:T(2,128)} %copy-done.11) | copy-start | bytes 100
  53.1 17.8 %collective-permute-start.2 = (bf16[2,256,64]{1,2,0:T(8,128)(2,1)}, bf16[2,256,64]{1,2,0:T(8,128)(2,1)}, u32[]{:S(2)}, u32[]{:S(2)}) collective-permute-start(bf16[2,256,64]{1,2,0:T(8,128)(2,1)} %get-tuple-element.15), channel_id=1, source_target_pairs={{0,1},{1,2},{2,3},{3,4},{4,5},{5,6},{6,7},{7,8},{8,9},{9,10},{10,1... | collective-permute-start | bytes 196616 | tf_op jit(solution)/shard_map/ppermute | solution.py:12
  60.1 2.8 %copy-start.1 = (bf16[1,4,128,384]{3,2,1,0:T(8,128)(2,1)S(1)}, bf16[1,4,128,384]{3,2,1,0:T(8,128)(2,1)}, u32[]{:S(2)}) copy-start(bf16[1,4,128,384]{3,2,1,0:T(8,128)(2,1)} %broadcast_bitcast_fusion.5) | copy-start | bytes 1179652
  68.5 7.6 %copy-start.4 = (bf16[4,256,511]{2,1,0:T(8,128)(2,1)S(1)}, bf16[4,256,511]{2,1,0:T(8,128)(2,1)}, u32[]{:S(2)}) copy-start(bf16[4,256,511]{2,1,0:T(8,128)(2,1)} %reshape.82) | copy-start | bytes 3139588
  68.7 0.9 copy-start.10
  69.6 6.2 %collective-permute-start.3 = (bf16[2,256,64]{1,2,0:T(8,128)(2,1)S(1)}, bf16[2,256,64]{1,2,0:T(8,128)(2,1)S(1)}, u32[]{:S(2)}, u32[]{:S(2)}) collective-permute-start(bf16[2,256,64]{1,2,0:T(8,128)(2,1)S(1)} %copy-done.10), channel_id=1, source_target_pairs={{1,0},{2,1},{3,2},{4,3},{5,4},{6,5},{7,6},{8,7},{9,8},{10,9},{11,1... | collective-permute-start | bytes 196616 | tf_op jit(solution)/shard_map/ppermute | solution.py:12
  71.8 4.4 %copy-start.17 = (pred[128]{0:T(512)(128)(4,1)S(1)}, pred[128]{0:T(512)(128)(4,1)}, u32[]{:S(2)}) copy-start(pred[128]{0:T(512)(128)(4,1)} %copy-done.15) | copy-start | bytes 388
  78.3 0.6 copy-start.18
  78.3 0.6 copy-start.19
  79.8 0.7 copy-start.9
  79.8 1.0 copy-start.14
  79.9 10.9 %copy-start.5 = (f32[4,128,128]{2,1,0:T(8,128)S(1)}, f32[4,128,128]{2,1,0:T(8,128)}, u32[]{:S(2)}) copy-start(f32[4,128,128]{2,1,0:T(8,128)} %param.7) | copy-start | bytes 786436
Sparse Core Ops, SparseCore 0:
  80.0 10.7 reduce-scatter.1
where the time goes:
time: 100 us; the launch traced here: 99.4 us
  local copies, waits for them, and re-layouts  42.5 us (42%)
  between operations  16.2 us (16%)
  starting transfers between devices  13.3 us (13%)
  waiting for transfers between devices  13.1 us (13%)
  other arithmetic  6.13 us (6%)
  matrix products  5.69 us (6%)
  blocking collectives  2.47 us (2%)
    reshape x8, local copies, waits for them, and re-layouts, toeplitz(): tiled[:, :count_a * (count_a + count_b - 1)]  17.1 us
    unnamed x68, local copies, waits for them, and re-layouts  16.2 us
    ppermute x4, starting transfers between devices, from_behind(): lax.ppermute(value, axis, [(source, source + steps) for source in range(f...  13.2 us
    reduce_scatter x1, waiting for transfers between devices, body(): lax.psum_scatter(partial_value, 'chan', scatter_dimension=1, tiled=True)  9.09 us
    dot_general x4, matrix products, apply_psf(): jnp.einsum('ryk,rkj->yj', row_band, col_pass, preferred_element_type=jnp....  5.27 us
    ppermute x4, waiting for transfers between devices, from_behind(): lax.ppermute(value, axis, [(source, source + steps) for source in range(f...  3.98 us
    slice x8, local copies, waits for them, and re-layouts, toeplitz(): tiled[:, :count_a * (count_a + count_b - 1)]  2.73 us
    concatenate x2, other arithmetic, with_rims(): jnp.concatenate([left_rim, masked, jnp.zeros((chan_count, row_count, 2 *...  2.5 us
  transfers between devices with their start and end apart: 5, of which 2 were waited for; matrix products, arithmetic and copies ran while one was open for 37% of the time, Pallas kernels for 0%

commit v1 on v0

v1 whole, which is shorter than its diff:
```python
import functools

import jax
import jax.numpy as jnp
from jax import lax
from jax.experimental import pallas as pl
from jax.experimental.pallas import tpu as pltpu
from jax.sharding import PartitionSpec as P

TAPS = 129
HALF = (TAPS - 1) // 2
LANES = 512


def from_behind(value, axis, steps):
    count = lax.axis_size(axis)
    first, last = (max(0, -steps), min(count, count - steps))
    return lax.ppermute(value, axis, [(source, source + steps) for source in range(first, last)])


def tap_table(psf_rows, psf_cols, first_chan, local_chans):
    rows = lax.dynamic_slice_in_dim(psf_rows, first_chan, local_chans, 0)
    cols = lax.dynamic_slice_in_dim(psf_cols, first_chan, local_chans, 0)
    rows = rows.astype(jnp.bfloat16).astype(jnp.float32)
    cols = cols.astype(jnp.bfloat16).astype(jnp.float32)
    kinds = jnp.stack([cols[..., ::-1], cols, rows, rows[..., ::-1]], axis=1)
    kinds = jnp.pad(kinds, ((0, 0), (0, 0), (0, 0), (0, LANES - TAPS)))
    return kinds.reshape(local_chans, -1, LANES)


def col_band(w, slot):
    ext = slot + 2 * HALF
    spread = jnp.broadcast_to(w[:, :ext], (ext, ext))
    return pltpu.roll(spread, ext - 2 * HALF, 1, stride=1, stride_axis=0)[:, :slot]


def row_band(w, rows):
    spread = jnp.broadcast_to(w, (rows, LANES))
    return pltpu.roll(spread, LANES - HALF, 1, stride=1, stride_axis=0)[:, :rows]


def psf_pass(tab, base, left, centre, right, rank_count):
    rows, slot = centre.shape
    bands = [
        col_band(tab[base + r : base + r + 1, :], slot).astype(jnp.bfloat16)
        for r in range(rank_count)
    ]
    band = jnp.concatenate(bands, axis=1)
    col_pass = (
        jnp.dot(left, band[:HALF], preferred_element_type=jnp.float32)
        + jnp.dot(centre, band[HALF : HALF + slot], preferred_element_type=jnp.float32)
        + jnp.dot(right, band[HALF + slot :], preferred_element_type=jnp.float32)
    ).astype(jnp.bfloat16)
    total = None
    for r in range(rank_count):
        rb = row_band(tab[base + 2 * rank_count + r : base + 2 * rank_count + r + 1, :], rows)
        part = jnp.dot(
            rb.astype(jnp.bfloat16),
            col_pass[:, r * slot : (r + 1) * slot],
            preferred_element_type=jnp.float32,
        )
        total = part if total is None else total + part
    return total


def forward_kernel(rank_count, tab_ref, xl_ref, xc_ref, xr_ref, dirty_ref, res_ref):
    for c in range(xc_ref.shape[0]):
        tab = tab_ref[c]
        pred = psf_pass(tab, 0, xl_ref[c], xc_ref[c], xr_ref[c], rank_count)
        res_ref[c] = (dirty_ref[c].astype(jnp.float32) - pred).astype(res_ref.dtype)


def adjoint_kernel(rank_count, spec_ref, tab_ref, rl_ref, rc_ref, rr_ref, out_ref):
    basis = out_ref.shape[0]
    for c in range(rc_ref.shape[0]):
        tab = tab_ref[c]
        grad_chan = psf_pass(tab, rank_count, rl_ref[c], rc_ref[c], rr_ref[c], rank_count)
        for b in range(basis):
            term = spec_ref[c, b] * grad_chan
            if c == 0:
                out_ref[b] = term
            else:
                out_ref[b] = out_ref[b] + term


def vmem_spec():
    return pl.BlockSpec(memory_space=pltpu.VMEM)


def body(dirty, model, spectral, psf_rows, psf_cols, strip_width):
    local_chans, row_count, slot_width = dirty.shape
    basis = model.shape[0]
    rank_count = psf_rows.shape[1]
    chan_count = lax.axis_size("chan")
    first_chan = lax.axis_index("chan") * local_chans

    image_rows = spectral[:, 0][:, None, None] * model[0][None]
    for basis_idx in range(1, basis):
        image_rows = image_rows + spectral[:, basis_idx][:, None, None] * model[basis_idx][None]
    image_rows = image_rows.astype(jnp.bfloat16)
    image = lax.all_to_all(image_rows, "chan", 0, 1, tiled=True)

    tab = tap_table(psf_rows, psf_cols, first_chan, local_chans)
    spec_local = lax.dynamic_slice_in_dim(spectral, first_chan, local_chans, 0)

    xl = from_behind(image[:, :, slot_width - HALF :], "sky", 1)
    xr = from_behind(image[:, :, :HALF], "sky", -1)
    residual = pl.pallas_call(
        functools.partial(forward_kernel, rank_count),
        out_shape=jax.ShapeDtypeStruct(dirty.shape, jnp.bfloat16),
        in_specs=[vmem_spec()] * 5,
        out_specs=vmem_spec(),
    )(tab, xl, image, xr, dirty)

    rl = from_behind(residual[:, :, slot_width - HALF :], "sky", 1)
    rr = from_behind(residual[:, :, :HALF], "sky", -1)
    partial_value = pl.pallas_call(
        functools.partial(adjoint_kernel, rank_count),
        out_shape=jax.ShapeDtypeStruct((basis, row_count, slot_width), jnp.float32),
        in_specs=[pl.BlockSpec(memory_space=pltpu.SMEM)] + [vmem_spec()] * 4,
        out_specs=vmem_spec(),
    )(spec_local, tab, rl, residual, rr)

    pieces = lax.all_to_all(partial_value, "chan", 1, 0, tiled=True)
    grad_share = pieces.reshape(chan_count, basis, row_count // chan_count, slot_width).sum(0)

    gram_rows = jnp.einsum("crt,cst->crs", psf_rows, psf_rows, precision=lax.Precision.HIGHEST)
    gram_cols = jnp.einsum("crt,cst->crs", psf_cols, psf_cols, precision=lax.Precision.HIGHEST)
    energy = jnp.sum(gram_rows * gram_cols, axis=(1, 2))
    curvature = jnp.sum(spectral * spectral * energy[:, None], axis=0)
    model_new = model + grad_share / curvature[:, None, None]
    return (residual, model_new)


def solution(mesh):
    placed = (P("chan", None, "sky"), P(None, "chan", "sky"), P(), P(), P(), P())
    return jax.shard_map(
        body,
        mesh=mesh,
        in_specs=placed,
        out_specs=(P("chan", None, "sky"), P(None, "chan", "sky")),
        check_vma=False,
    )
```

time: 100 us -> 46.6 us (0.47)
  the two profiles are of different devices: /device:TPU:0 before, /device:TPU:7 now
where the time goes in v1:
time: 46.6 us; the launch traced here: 46.1 us
  starting transfers between devices  10.7 us (23%)
  blocking collectives  10.4 us (22%)
  local copies, waits for them, and re-layouts  9.36 us (20%)
  waiting for transfers between devices  7.75 us (17%)
  Pallas kernels  6.07 us (13%)
  between operations  0.79 us (2%)
  other arithmetic  0.66 us (1%)
    ppermute x4, starting transfers between devices, from_behind(): lax.ppermute(value, axis, [(source, source + steps) for source in range(f...  10.7 us
    ppermute x4, waiting for transfers between devices, from_behind(): lax.ppermute(value, axis, [(source, source + steps) for source in range(f...  7.75 us
    all_to_all x1, blocking collectives, body(): pieces = lax.all_to_all(partial_value, 'chan', 1, 0, tiled=True)  6.2 us
    unnamed x22, local copies, waits for them, and re-layouts  4.25 us
    all_to_all x1, blocking collectives, body(): image = lax.all_to_all(image_rows, 'chan', 0, 1, tiled=True)  4.16 us
    pallas_call x1, Pallas kernels, body(): pl.pallas_call(functools.partial(adjoint_kernel, rank_count), out_shape=j...  3.08 us
    pallas_call x1, Pallas kernels, body(): pl.pallas_call(functools.partial(forward_kernel, rank_count), out_shape=j...  2.99 us
    pallas_call x1, local copies, waits for them, and re-layouts, body(): pl.pallas_call(functools.partial(adjoint_kernel, rank_count), out_shape=j...  1.38 us
  transfers between devices with their start and end apart: 4, of which 2 were waited for; matrix products, arithmetic and copies ran while one was open for 5% of the time, Pallas kernels for 0%

profile of v1, /device:TPU:7, one launch (start us, length us, event | category | flops | bytes accessed | tf_op | source)
XLA Modules:
  0.0 46.1 jit_solution(7344539566480257913)
XLA Ops:
  0.6 1.0 %slice_bitcast_fusion.3 = (f32[128,128]{1,0:T(8,128)S(1)}, f32[128,128]{1,0:T(8,128)S(1)}, f32[128,128]{1,0:T(8,128)S(1)}, f32[128,128]{1,0:T(8,128)S(1)}) fusion(f32[4,128,128]{2,1,0:T(8,128)} %param.7), kind=kLoop, calls=%fused_computation.7 | loop fusion | bytes 524288 | tf_op jit(solution)/shard_map/mul | solution.py:97
  1.6 0.2 slice_reduce_fusion.3
  1.8 0.2 add_convert_fusion
  2.0 4.2 %all_to_all.30 = bf16[4,128,128]{2,1,0:T(8,128)(2,1)S(1)} all-to-all(bf16[4,128,128]{2,1,0:T(8,128)(2,1)S(1)} %add_convert_fusion), channel_id=1, replica_groups=mesh['chan'=2,'sky'=16] {'chan'}, dimensions={0} | all-to-all | bytes 262144 | tf_op jit(solution)/shard_map/all_to_all | solution.py:101
  6.2 0.1 fusion.4
  6.3 0.5 %copy-done = bf16[2,2,128,128]{3,2,1,0:T(8,128)(2,1)} copy-done((bf16[2,2,128,128]{3,2,1,0:T(8,128)(2,1)}, bf16[2,2,128,128]{3,2,1,0:T(8,128)(2,1)S(1)}, u32[]{:S(2)}) %copy-start) | copy-done | bytes 131096
  6.8 3.2 %collective-permute-start = (bf16[2,256,64]{2,1,0:T(8,128)(2,1)S(1)}, bf16[2,256,64]{2,1,0:T(8,128)(2,1)S(1)}, u32[]{:S(2)}, u32[]{:S(2)}) collective-permute-start(bf16[2,256,64]{2,1,0:T(8,128)(2,1)S(1)} %get-tuple-element.15), channel_id=1, source_target_pairs={{0,1},{1,2},{2,3},{3,4},{4,5},{5,6},{6,7},{7,8},{8,9},{9,10},{10,1... | collective-permute-start | bytes 196616 | tf_op jit(solution)/shard_map/ppermute | solution.py:18
  10.1 2.2 %collective-permute-start.1 = (bf16[2,256,64]{2,1,0:T(8,128)(2,1)S(1)}, bf16[2,256,64]{2,1,0:T(8,128)(2,1)S(1)}, u32[]{:S(2)}, u32[]{:S(2)}) collective-permute-start(bf16[2,256,64]{2,1,0:T(8,128)(2,1)S(1)} %get-tuple-element.14), channel_id=1, source_target_pairs={{1,0},{2,1},{3,2},{4,3},{5,4},{6,5},{7,6},{8,7},{9,8},{10,9},{11,1... | collective-permute-start | bytes 196616 | tf_op jit(solution)/shard_map/ppermute | solution.py:18
  12.3 0.2 fusion.5
  12.4 0.6 %copy-done.7 = f32[4,4,129]{2,1,0:T(4,128)S(1)} copy-done((f32[4,4,129]{2,1,0:T(4,128)S(1)}, f32[4,4,129]{2,1,0:T(4,128)}, u32[]{:S(2)}) %copy-start.7) | copy-done | bytes 8280
  13.0 0.2 reverse.1
  13.1 0.1 slice_bitcast_fusion.4
  13.2 0.2 reverse
  13.5 0.6 %reshape.15.tab_ref = f32[2,16,512]{2,1,0:T(8,128)} reshape(f32[2,4,4,512]{3,2,1,0:T(4,128)S(1)} %pad.4.clone) | data formatting | bytes 131072 | tf_op jit(solution)/shard_map/reshape | solution.py:28
  14.2 0.3 fusion
  14.4 0.1 multiply_reduce_fusion
  14.5 3.6 %collective-permute-done.1.xr_ref = bf16[2,256,64]{2,1,0:T(8,128)(2,1)S(1)} collective-permute-done((bf16[2,256,64]{2,1,0:T(8,128)(2,1)S(1)}, bf16[2,256,64]{2,1,0:T(8,128)(2,1)S(1)}, u32[]{:S(2)}, u32[]{:S(2)}) %collective-permute-start.1) | collective-permute-done | bytes 65568 | tf_op jit(solution)/shard_map/ppermute | solution.py:18
  18.2 0.7 %copy-done.5 = bf16[2,256,64]{2,1,0:T(8,128)(2,1)} copy-done((bf16[2,256,64]{2,1,0:T(8,128)(2,1)}, bf16[2,256,64]{2,1,0:T(8,128)(2,1)S(1)}, u32[]{:S(2)}) %copy-start.5) | copy-done | bytes 65560
  18.8 3.0 %shard_map.68.rc_ref = bf16[2,256,128]{2,1,0:T(8,128)(2,1)} custom-call(f32[2,16,512]{2,1,0:T(8,128)} %reshape.15.tab_ref, bf16[2,256,64]{2,1,0:T(8,128)(2,1)} %copy-done.4, bf16[2,256,128]{2,1,0:T(8,128)(2,1)} %bitcast.27, bf16[2,256,64]{2,1,0:T(8,128)(2,1)} %copy-done.5, bf16[2,256,128]{2,1,0:T(8,128)(2,1)} %dirty_ref.1), custom_call_target="tpu_custom_call" | custom-call | tf_op jit(solution)/shard_map/pallas_call | solution.py:108
  21.8 1.1 %fusion.3 = (bf16[2,256,64]{2,1,0:T(8,128)(2,1)S(1)}, bf16[2,256,64]{2,1,0:T(8,128)(2,1)S(1)}) fusion(bf16[2,256,128]{2,1,0:T(8,128)(2,1)} %shard_map.68.rc_ref), kind=kLoop, calls=%fused_computation.19 | loop fusion | bytes 262144 | tf_op jit(solution)/shard_map/slice | solution.py:116
  22.9 2.5 %collective-permute-start.2 = (bf16[2,256,64]{2,1,0:T(8,128)(2,1)S(1)}, bf16[2,256,64]{2,1,0:T(8,128)(2,1)S(1)}, u32[]{:S(2)}, u32[]{:S(2)}) collective-permute-start(bf16[2,256,64]{2,1,0:T(8,128)(2,1)S(1)} %get-tuple-element.13), channel_id=1, source_target_pairs={{0,1},{1,2},{2,3},{3,4},{4,5},{5,6},{6,7},{7,8},{8,9},{9,10},{10,1... | collective-permute-start | bytes 196616 | tf_op jit(solution)/shard_map/ppermute | solution.py:18
  25.4 2.8 %collective-permute-start.3 = (bf16[2,256,64]{2,1,0:T(8,128)(2,1)S(1)}, bf16[2,256,64]{2,1,0:T(8,128)(2,1)S(1)}, u32[]{:S(2)}, u32[]{:S(2)}) collective-permute-start(bf16[2,256,64]{2,1,0:T(8,128)(2,1)S(1)} %get-tuple-element.12), channel_id=1, source_target_pairs={{1,0},{2,1},{3,2},{4,3},{5,4},{6,5},{7,6},{8,7},{9,8},{10,9},{11,1... | collective-permute-start | bytes 196616 | tf_op jit(solution)/shard_map/ppermute | solution.py:18
  28.2 0.6 %constant_dynamic-slice_fusion.spec_ref = f32[2,4]{1,0:T(2,128)} fusion(f32[4,4]{1,0:T(4,128)S(1)} %copy-done.8, s32[]{:T(128)S(6)} %select_n.2), kind=kLoop, calls=%fused_computation.18 | loop fusion | bytes 68 | tf_op jit(solution)/shard_map/dynamic_slice | solution.py:104
  28.8 4.1 %collective-permute-done.3.rr_ref = bf16[2,256,64]{2,1,0:T(8,128)(2,1)S(1)} collective-permute-done((bf16[2,256,64]{2,1,0:T(8,128)(2,1)S(1)}, bf16[2,256,64]{2,1,0:T(8,128)(2,1)S(1)}, u32[]{:S(2)}, u32[]{:S(2)}) %collective-permute-start.3) | collective-permute-done | bytes 65568 | tf_op jit(solution)/shard_map/ppermute | solution.py:18
  32.9 0.7 %copy-done.3 = bf16[2,256,64]{2,1,0:T(8,128)(2,1)} copy-done((bf16[2,256,64]{2,1,0:T(8,128)(2,1)}, bf16[2,256,64]{2,1,0:T(8,128)(2,1)S(1)}, u32[]{:S(2)}) %copy-start.3) | copy-done | bytes 65560
  33.5 3.1 %shard_map.69 = f32[4,256,128]{2,1,0:T(8,128)} custom-call(f32[2,4]{1,0:T(2,128)} %constant_dynamic-slice_fusion.spec_ref, f32[2,16,512]{2,1,0:T(8,128)} %reshape.15.tab_ref, bf16[2,256,64]{2,1,0:T(8,128)(2,1)} %copy-done.2, bf16[2,256,128]{2,1,0:T(8,128)(2,1)} %shard_map.68.rc_ref, bf16[2,256,64]{2,1,0:T(8,128)(2,1)} %copy-done.3), custom_call_target="tpu_custom_call" | custom-call | tf_op jit(solution)/shard_map/pallas_call | solution.py:117
  36.6 1.4 %copy.15 = f32[4,256,128]{2,0,1:T(4,128)S(1)} copy(f32[4,256,128]{2,1,0:T(8,128)} %shard_map.69) | data formatting | bytes 1048576 | tf_op jit(solution)/shard_map/pallas_call | solution.py:117
  38.0 6.2 %all_to_all.31 = f32[4,256,128]{2,0,1:T(4,128)S(1)} all-to-all(f32[4,256,128]{2,0,1:T(4,128)S(1)} %copy.15), channel_id=1, replica_groups=mesh['chan'=2,'sky'=16] {'chan'}, dimensions={1} | all-to-all | bytes 1048576 | tf_op jit(solution)/shard_map/all_to_all | solution.py:124
  44.2 0.2 reduce_sum.27
  44.4 0.8 %copy-done.1 = f32[4,128,128]{2,1,0:T(8,128)S(1)} copy-done((f32[4,128,128]{2,1,0:T(8,128)S(1)}, f32[4,128,128]{2,1,0:T(8,128)}, u32[]{:S(2)}) %copy-start.1) | copy-done | bytes 262168
  45.1 0.2 divide_add_fusion
  45.4 0.7 %copy.17 = f32[4,128,128]{2,1,0:T(8,128)} copy(f32[4,128,128]{2,0,1:T(4,128)S(1)} %divide_add_fusion) | data formatting | bytes 524288
  (21 shorter events, 0.2 us)
Async XLA Ops:
  0.6 1.0 %copy-start.8 = (f32[4,4]{1,0:T(4,128)S(1)}, f32[4,4]{1,0:T(4,128)}, u32[]{:S(2)}) copy-start(f32[4,4]{1,0:T(4,128)} %param.8) | copy-start | bytes 196
  6.2 0.6 %copy-start = (bf16[2,2,128,128]{3,2,1,0:T(8,128)(2,1)}, bf16[2,2,128,128]{3,2,1,0:T(8,128)(2,1)S(1)}, u32[]{:S(2)}) copy-start(bf16[2,2,128,128]{3,2,1,0:T(8,128)(2,1)S(1)} %copy.14) | copy-start | bytes 393220
  6.8 5.4 %copy-start.6 = (f32[4,4,129]{2,1,0:T(4,128)S(1)}, f32[4,4,129]{2,1,0:T(4,128)}, u32[]{:S(2)}) copy-start(f32[4,4,129]{2,1,0:T(4,128)} %param.9) | copy-start | bytes 24772
  6.8 7.7 %collective-permute-start = (bf16[2,256,64]{2,1,0:T(8,128)(2,1)S(1)}, bf16[2,256,64]{2,1,0:T(8,128)(2,1)S(1)}, u32[]{:S(2)}, u32[]{:S(2)}) collective-permute-start(bf16[2,256,64]{2,1,0:T(8,128)(2,1)S(1)} %get-tuple-element.15), channel_id=1, source_target_pairs={{0,1},{1,2},{2,3},{3,4},{4,5},{5,6},{6,7},{7,8},{8,9},{9,10},{10,1... | collective-permute-start | bytes 196616 | tf_op jit(solution)/shard_map/ppermute | solution.py:18
  10.1 8.1 %collective-permute-start.1 = (bf16[2,256,64]{2,1,0:T(8,128)(2,1)S(1)}, bf16[2,256,64]{2,1,0:T(8,128)(2,1)S(1)}, u32[]{:S(2)}, u32[]{:S(2)}) collective-permute-start(bf16[2,256,64]{2,1,0:T(8,128)(2,1)S(1)} %get-tuple-element.14), channel_id=1, source_target_pairs={{1,0},{2,1},{3,2},{4,3},{5,4},{6,5},{7,6},{8,7},{9,8},{10,9},{11,1... | collective-permute-start | bytes 196616 | tf_op jit(solution)/shard_map/ppermute | solution.py:18
  12.2 0.7 %copy-start.7 = (f32[4,4,129]{2,1,0:T(4,128)S(1)}, f32[4,4,129]{2,1,0:T(4,128)}, u32[]{:S(2)}) copy-start(f32[4,4,129]{2,1,0:T(4,128)} %param.10) | copy-start | bytes 24772
  14.5 3.6 %copy-start.4 = (bf16[2,256,64]{2,1,0:T(8,128)(2,1)}, bf16[2,256,64]{2,1,0:T(8,128)(2,1)S(1)}, u32[]{:S(2)}) copy-start(bf16[2,256,64]{2,1,0:T(8,128)(2,1)S(1)} %collective-permute-done.xl_ref) | copy-start | bytes 196612
  18.2 0.7 %copy-start.5 = (bf16[2,256,64]{2,1,0:T(8,128)(2,1)}, bf16[2,256,64]{2,1,0:T(8,128)(2,1)S(1)}, u32[]{:S(2)}) copy-start(bf16[2,256,64]{2,1,0:T(8,128)(2,1)S(1)} %collective-permute-done.1.xr_ref) | copy-start | bytes 196612
  22.9 5.9 %collective-permute-start.2 = (bf16[2,256,64]{2,1,0:T(8,128)(2,1)S(1)}, bf16[2,256,64]{2,1,0:T(8,128)(2,1)S(1)}, u32[]{:S(2)}, u32[]{:S(2)}) collective-permute-start(bf16[2,256,64]{2,1,0:T(8,128)(2,1)S(1)} %get-tuple-element.13), channel_id=1, source_target_pairs={{0,1},{1,2},{2,3},{3,4},{4,5},{5,6},{6,7},{7,8},{8,9},{9,10},{10,1... | collective-permute-start | bytes 196616 | tf_op jit(solution)/shard_map/ppermute | solution.py:18
  25.4 7.5 %collective-permute-start.3 = (bf16[2,256,64]{2,1,0:T(8,128)(2,1)S(1)}, bf16[2,256,64]{2,1,0:T(8,128)(2,1)S(1)}, u32[]{:S(2)}, u32[]{:S(2)}) collective-permute-start(bf16[2,256,64]{2,1,0:T(8,128)(2,1)S(1)} %get-tuple-element.12), channel_id=1, source_target_pairs={{1,0},{2,1},{3,2},{4,3},{5,4},{6,5},{7,6},{8,7},{9,8},{10,9},{11,1... | collective-permute-start | bytes 196616 | tf_op jit(solution)/shard_map/ppermute | solution.py:18
  28.7 4.1 %copy-start.2 = (bf16[2,256,64]{2,1,0:T(8,128)(2,1)}, bf16[2,256,64]{2,1,0:T(8,128)(2,1)S(1)}, u32[]{:S(2)}) copy-start(bf16[2,256,64]{2,1,0:T(8,128)(2,1)S(1)} %collective-permute-done.2.rl_ref) | copy-start | bytes 196612
  32.9 0.7 %copy-start.3 = (bf16[2,256,64]{2,1,0:T(8,128)(2,1)}, bf16[2,256,64]{2,1,0:T(8,128)(2,1)S(1)}, u32[]{:S(2)}) copy-start(bf16[2,256,64]{2,1,0:T(8,128)(2,1)S(1)} %collective-permute-done.3.rr_ref) | copy-start | bytes 196612
  44.2 0.9 %copy-start.1 = (f32[4,128,128]{2,1,0:T(8,128)S(1)}, f32[4,128,128]{2,1,0:T(8,128)}, u32[]{:S(2)}) copy-start(f32[4,128,128]{2,1,0:T(8,128)} %param.7) | copy-start | bytes 786436

commit v2 on v1

v2 whole, which is shorter than its diff:
```python
import functools

import jax
import jax.numpy as jnp
from jax import lax
from jax.experimental import pallas as pl
from jax.experimental.pallas import tpu as pltpu
from jax.sharding import PartitionSpec as P

TAPS = 129
HALF = (TAPS - 1) // 2
LANES = 512


def from_behind(value, axis, steps):
    count = lax.axis_size(axis)
    first, last = (max(0, -steps), min(count, count - steps))
    return lax.ppermute(value, axis, [(source, source + steps) for source in range(first, last)])


def tap_table(psf_rows, psf_cols, first_chan, local_chans):
    rows = lax.dynamic_slice_in_dim(psf_rows, first_chan, local_chans, 0)
    cols = lax.dynamic_slice_in_dim(psf_cols, first_chan, local_chans, 0)
    rows = rows.astype(jnp.bfloat16).astype(jnp.float32)
    cols = cols.astype(jnp.bfloat16).astype(jnp.float32)
    kinds = jnp.stack([cols[..., ::-1], cols, rows, rows[..., ::-1]], axis=1)
    kinds = jnp.pad(kinds, ((0, 0), (0, 0), (0, 0), (0, LANES - TAPS)))
    return kinds.reshape(local_chans, -1, LANES)


def col_band(w, slot):
    ext = slot + 2 * HALF
    spread = jnp.broadcast_to(w[:, :ext], (ext, ext))
    return pltpu.roll(spread, ext - 2 * HALF, 1, stride=1, stride_axis=0)[:, :slot]


def row_band(w, rows):
    spread = jnp.broadcast_to(w, (rows, LANES))
    return pltpu.roll(spread, LANES - HALF, 1, stride=1, stride_axis=0)[:, :rows]


def band_kernel(rank_count, slot, tab_ref, colf_ref, rowf_ref, cola_ref, rowa_ref):
    rows = rowf_ref.shape[-1]
    for c in range(tab_ref.shape[0]):
        tab = tab_ref[c]
        for kind, col_ref, row_ref in ((0, colf_ref, rowf_ref), (1, cola_ref, rowa_ref)):
            for r in range(rank_count):
                w = tab[kind * rank_count + r : kind * rank_count + r + 1, :]
                col_ref[c, :, r * slot : (r + 1) * slot] = col_band(w, slot).astype(jnp.bfloat16)
                w = tab[(kind + 2) * rank_count + r : (kind + 2) * rank_count + r + 1, :]
                row_ref[c, r] = row_band(w, rows).astype(jnp.bfloat16)


def row_pass(row_ref, c, col_pass, rank_count, slot):
    total = None
    for r in range(rank_count):
        part = jnp.dot(
            row_ref[c, r], col_pass[:, r * slot : (r + 1) * slot], preferred_element_type=jnp.float32
        )
        total = part if total is None else total + part
    return total


def main_kernel(
    rank_count, spec_ref, edge_ref, colf_ref, rowf_ref, cola_ref, rowa_ref,
    xl_ref, xc_ref, xr_ref, dirty_ref, dl_ref, dr_ref, res_ref, part_ref,
):
    slot = xc_ref.shape[-1]
    pieces, basis, piece_rows, _ = part_ref.shape
    lane = lax.broadcasted_iota(jnp.int32, (xc_ref.shape[1], slot), 1)
    for c in range(xc_ref.shape[0]):
        band = colf_ref[c]
        xl, xc, xr = xl_ref[c], xc_ref[c], xr_ref[c]
        low = (
            jnp.dot(xl, band[:slot], preferred_element_type=jnp.float32)
            + jnp.dot(xc, band[slot:], preferred_element_type=jnp.float32)
        ).astype(jnp.bfloat16)
        high = (
            jnp.dot(xc, band[:slot], preferred_element_type=jnp.float32)
            + jnp.dot(xr, band[slot:], preferred_element_type=jnp.float32)
        ).astype(jnp.bfloat16)
        pred_low = row_pass(rowf_ref, c, low, rank_count, slot)
        pred_high = row_pass(rowf_ref, c, high, rank_count, slot)
        pred_own = pltpu.roll(jnp.where(lane < HALF, pred_high, pred_low), HALF, 1)
        res_own = (dirty_ref[c].astype(jnp.float32) - pred_own).astype(jnp.bfloat16)
        res_ref[c] = res_own
        halo_l = jnp.where(edge_ref[0] > 0, dl_ref[c].astype(jnp.float32) - pred_low[:, :HALF], 0.0)
        pred_right = pltpu.roll(pred_high, slot - HALF, 1)[:, :HALF]
        halo_r = jnp.where(edge_ref[1] > 0, dr_ref[c].astype(jnp.float32) - pred_right, 0.0)
        adj = cola_ref[c]
        col_pass = (
            jnp.dot(halo_l.astype(jnp.bfloat16), adj[:HALF], preferred_element_type=jnp.float32)
            + jnp.dot(res_own, adj[HALF : HALF + slot], preferred_element_type=jnp.float32)
            + jnp.dot(halo_r.astype(jnp.bfloat16), adj[HALF + slot :], preferred_element_type=jnp.float32)
        ).astype(jnp.bfloat16)
        grad_chan = row_pass(rowa_ref, c, col_pass, rank_count, slot)
        for j in range(pieces):
            block = grad_chan[j * piece_rows : (j + 1) * piece_rows]
            for b in range(basis):
                term = spec_ref[c, b] * block
                if c == 0:
                    part_ref[j, b] = term
                else:
                    part_ref[j, b] = part_ref[j, b] + term


def vmem_spec():
    return pl.BlockSpec(memory_space=pltpu.VMEM)


def smem_spec():
    return pl.BlockSpec(memory_space=pltpu.SMEM)


def body(dirty, model, spectral, psf_rows, psf_cols, strip_width):
    local_chans, row_count, slot_width = dirty.shape
    basis = model.shape[0]
    rank_count = psf_rows.shape[1]
    chan_count = lax.axis_size("chan")
    sky_count = lax.axis_size("sky")
    sky_index = lax.axis_index("sky")
    first_chan = lax.axis_index("chan") * local_chans

    dl = from_behind(dirty[:, :, slot_width - HALF :], "sky", 1)
    dr = from_behind(dirty[:, :, :HALF], "sky", -1)

    image_rows = spectral[:, 0][:, None, None] * model[0][None]
    for basis_idx in range(1, basis):
        image_rows = image_rows + spectral[:, basis_idx][:, None, None] * model[basis_idx][None]
    image_rows = image_rows.astype(jnp.bfloat16)
    image = lax.all_to_all(image_rows, "chan", 0, 1, tiled=True)
    xl = from_behind(image, "sky", 1)
    xr = from_behind(image, "sky", -1)

    tab = tap_table(psf_rows, psf_cols, first_chan, local_chans)
    band_shapes = (
        jax.ShapeDtypeStruct((local_chans, slot_width + 2 * HALF, rank_count * slot_width), jnp.bfloat16),
        jax.ShapeDtypeStruct((local_chans, rank_count, row_count, row_count), jnp.bfloat16),
    )
    colf, rowf, cola, rowa = pl.pallas_call(
        functools.partial(band_kernel, rank_count, slot_width),
        out_shape=band_shapes * 2,
        in_specs=[vmem_spec()],
        out_specs=[vmem_spec()] * 4,
    )(tab)

    spec_local = lax.dynamic_slice_in_dim(spectral, first_chan, local_chans, 0)
    edges = jnp.stack([sky_index > 0, sky_index < sky_count - 1]).astype(jnp.int32)
    piece_rows = row_count // chan_count
    residual, partial_value = pl.pallas_call(
        functools.partial(main_kernel, rank_count),
        out_shape=(
            jax.ShapeDtypeStruct(dirty.shape, jnp.bfloat16),
            jax.ShapeDtypeStruct((chan_count, basis, piece_rows, slot_width), jnp.float32),
        ),
        in_specs=[smem_spec()] * 2 + [vmem_spec()] * 10,
        out_specs=[vmem_spec()] * 2,
    )(spec_local, edges, colf, rowf, cola, rowa, xl, image, xr, dirty, dl, dr)

    pieces = lax.all_to_all(partial_value, "chan", 0, 0, tiled=True)
    grad_share = pieces.sum(0)

    gram_rows = jnp.einsum("crt,cst->crs", psf_rows, psf_rows, precision=lax.Precision.HIGHEST)
    gram_cols = jnp.einsum("crt,cst->crs", psf_cols, psf_cols, precision=lax.Precision.HIGHEST)
    energy = jnp.sum(gram_rows * gram_cols, axis=(1, 2))
    curvature = jnp.sum(spectral * spectral * energy[:, None], axis=0)
    model_new = model + grad_share / curvature[:, None, None]
    return (residual, model_new)


def solution(mesh):
    placed = (P("chan", None, "sky"), P(None, "chan", "sky"), P(), P(), P(), P())
    return jax.shard_map(
        body,
        mesh=mesh,
        in_specs=placed,
        out_specs=(P("chan", None, "sky"), P(None, "chan", "sky")),
        check_vma=False,
    )
```

time: 46.6 us -> 42 us (0.901)
  the two profiles are of different devices: /device:TPU:7 before, /device:TPU:25 now
where the time goes in v2:
time: 42 us; the launch traced here: 41.5 us
  starting transfers between devices  14.3 us (34%)
  blocking collectives  10.5 us (25%)
  Pallas kernels  8.49 us (20%)
  local copies, waits for them, and re-layouts  5.27 us (13%)
  other arithmetic  1.7 us (4%)
  between operations  0.82 us (2%)
  matrix products  0.43 us (1%)
    ppermute x4, starting transfers between devices, from_behind(): lax.ppermute(value, axis, [(source, source + steps) for source in range(f...  14.3 us
    all_to_all x1, blocking collectives, body(): pieces = lax.all_to_all(partial_value, 'chan', 0, 0, tiled=True)  6.32 us
    pallas_call x1, Pallas kernels, body(): pl.pallas_call(functools.partial(main_kernel, rank_count), out_shape=(jax...  5.32 us
    all_to_all x1, blocking collectives, body(): image = lax.all_to_all(image_rows, 'chan', 0, 1, tiled=True)  4.16 us
    pallas_call x1, Pallas kernels, body(): pl.pallas_call(functools.partial(band_kernel, rank_count, slot_width), ou...  3.16 us
    unnamed x23, local copies, waits for them, and re-layouts  2.58 us
    mul x1, local copies, waits for them, and re-layouts, body(): image_rows = spectral[:, 0][:, None, None] * model[0][None]  0.96 us
  transfers between devices with their start and end apart: 4, of which 0 were waited for; matrix products, arithmetic and copies ran while one was open for 7% of the time, Pallas kernels for 8%

profile of v2, /device:TPU:25, one launch (start us, length us, event | category | flops | bytes accessed | tf_op | source)
XLA Modules:
  0.0 41.5 jit_solution(3484911906663947061)
XLA Ops:
  0.6 1.0 %slice_bitcast_fusion.3 = (f32[128,128]{1,0:T(8,128)S(1)}, f32[128,128]{1,0:T(8,128)S(1)}, f32[128,128]{1,0:T(8,128)S(1)}, f32[128,128]{1,0:T(8,128)S(1)}) fusion(f32[4,128,128]{2,1,0:T(8,128)} %param.7), kind=kLoop, calls=%fused_computation.7 | loop fusion | bytes 524288 | tf_op jit(solution)/shard_map/mul | solution.py:127
  1.6 0.2 slice_reduce_fusion.3
  1.8 0.2 add_convert_fusion
  2.0 4.2 %all_to_all.23 = bf16[4,128,128]{2,1,0:T(8,128)(2,1)S(1)} all-to-all(bf16[4,128,128]{2,1,0:T(8,128)(2,1)S(1)} %add_convert_fusion), channel_id=1, replica_groups=mesh['chan'=2,'sky'=16] {'chan'}, dimensions={0} | all-to-all | bytes 262144 | tf_op jit(solution)/shard_map/all_to_all | solution.py:131
  6.2 3.3 %collective-permute-start = (bf16[2,256,128]{2,1,0:T(8,128)(2,1)S(1)}, bf16[2,256,128]{2,1,0:T(8,128)(2,1)S(1)}, u32[]{:S(2)}, u32[]{:S(2)}) collective-permute-start(bf16[2,256,128]{2,1,0:T(8,128)(2,1)S(1)} %bitcast.26), channel_id=1, source_target_pairs={{0,1},{1,2},{2,3},{3,4},{4,5},{5,6},{6,7},{7,8},{8,9},{9,10},{10,1... | collective-permute-start | bytes 393224 | tf_op jit(solution)/shard_map/ppermute | solution.py:18
  9.4 4.0 %collective-permute-start.1 = (bf16[2,256,128]{2,1,0:T(8,128)(2,1)S(1)}, bf16[2,256,128]{2,1,0:T(8,128)(2,1)S(1)}, u32[]{:S(2)}, u32[]{:S(2)}) collective-permute-start(bf16[2,256,128]{2,1,0:T(8,128)(2,1)S(1)} %bitcast.27), channel_id=1, source_target_pairs={{1,0},{2,1},{3,2},{4,3},{5,4},{6,5},{7,6},{8,7},{9,8},{10,9},{11,1... | collective-permute-start | bytes 393224 | tf_op jit(solution)/shard_map/ppermute | solution.py:18
  13.4 0.1 fusion.3
  13.5 0.0 copy-start.7
  13.6 1.9 %collective-permute-start.2 = (bf16[2,256,64]{2,1,0:T(8,128)(2,1)S(1)}, bf16[2,256,64]{2,1,0:T(8,128)(2,1)S(1)}, u32[]{:S(2)}, u32[]{:S(2)}) collective-permute-start(bf16[2,256,64]{2,1,0:T(8,128)(2,1)S(1)} %get-tuple-element.23), channel_id=1, source_target_pairs={{0,1},{1,2},{2,3},{3,4},{4,5},{5,6},{6,7},{7,8},{8,9},{9,10},{10,1... | collective-permute-start | bytes 196616 | tf_op jit(solution)/shard_map/ppermute | solution.py:18
  15.5 5.2 %collective-permute-start.3 = (bf16[2,256,64]{2,1,0:T(8,128)(2,1)S(1)}, bf16[2,256,64]{2,1,0:T(8,128)(2,1)S(1)}, u32[]{:S(2)}, u32[]{:S(2)}) collective-permute-start(bf16[2,256,64]{2,1,0:T(8,128)(2,1)S(1)} %get-tuple-element.22), channel_id=1, source_target_pairs={{1,0},{2,1},{3,2},{4,3},{5,4},{6,5},{7,6},{8,7},{9,8},{10,9},{11,1... | collective-permute-start | bytes 196616 | tf_op jit(solution)/shard_map/ppermute | solution.py:18
  20.7 0.0 copy-start.8
  20.7 0.2 fusion.4
  20.8 0.6 %copy-done.8 = f32[4,4,129]{2,1,0:T(4,128)S(1)} copy-done((f32[4,4,129]{2,1,0:T(4,128)S(1)}, f32[4,4,129]{2,1,0:T(4,128)}, u32[]{:S(2)}) %copy-start.8) | copy-done | bytes 8280
  21.4 0.2 reverse.1
  21.6 0.1 slice_bitcast_fusion.4
  21.6 0.2 reverse
  21.8 0.1 slice_bitcast_fusion.5
  21.9 0.3 fusion
  22.2 0.1 multiply_reduce_fusion
  22.3 0.6 %constant_dynamic-slice_fusion.spec_ref = f32[2,4]{1,0:T(2,128)} fusion(f32[4,4]{1,0:T(4,128)S(1)} %copy-done.9, s32[]{:T(128)S(6)} %select_n.2), kind=kLoop, calls=%fused_computation.19 | loop fusion | bytes 68 | tf_op jit(solution)/shard_map/dynamic_slice | solution.py:147
  22.9 0.7 %reshape.13.tab_ref = f32[2,16,512]{2,1,0:T(8,128)} reshape(f32[2,4,4,512]{3,2,1,0:T(4,128)S(1)} %pad.4.clone) | data formatting | bytes 131072 | tf_op jit(solution)/shard_map/reshape | solution.py:28
  23.5 3.2 %shard_map.68 = (bf16[2,256,512]{2,1,0:T(8,128)(2,1)}, bf16[2,4,256,256]{3,2,1,0:T(8,128)(2,1)}, bf16[2,256,512]{2,1,0:T(8,128)(2,1)}, bf16[2,4,256,256]{3,2,1,0:T(8,128)(2,1)}) custom-call(f32[2,16,512]{2,1,0:T(8,128)} %reshape.13.tab_ref), custom_call_target="tpu_custom_call" | custom-call | tf_op jit(solution)/shard_map/pallas_call | solution.py:140
  26.7 0.6 %add_convert_fusion.1.edge_ref = s32[2]{0:T(128)} fusion(pred[1]{0:T(512)(128)(4,1)} %bitcast.1, pred[1]{0:T(512)(128)(4,1)} %bitcast), kind=kLoop, calls=%fused_computation.18 | loop fusion | flops 4 | bytes 10 | tf_op jit(solution)/shard_map/convert_element_type | solution.py:148
  27.4 0.0 copy-start.3
  27.4 0.6 %copy-done.5 = bf16[2,256,64]{2,1,0:T(8,128)(2,1)} copy-done((bf16[2,256,64]{2,1,0:T(8,128)(2,1)}, bf16[2,256,64]{2,1,0:T(8,128)(2,1)S(1)}, u32[]{:S(2)}) %copy-start.5) | copy-done | bytes 65560
  28.0 0.1 copy-done.6
  28.0 0.0 copy-done.3
  28.1 0.0 copy-done.4
  28.1 5.3 %shard_map.69 = (bf16[2,256,128]{2,1,0:T(8,128)(2,1)}, f32[2,4,128,128]{3,2,1,0:T(8,128)}) custom-call(f32[2,4]{1,0:T(2,128)} %constant_dynamic-slice_fusion.spec_ref, s32[2]{0:T(128)} %add_convert_fusion.1.edge_ref, bf16[2,256,512]{2,1,0:T(8,128)(2,1)} %get-tuple-element.8.colf_ref, bf16[2,4,256,256]{3,2,1,0:T(8,128)(2,1)} %get-tuple-element.9.rowf_ref, ...), custom_call_target="tpu_custom_call" | custom-call | tf_op jit(solution)/shard_map/pallas_call | solution.py:150
  33.4 6.3 %all_to_all.24 = f32[2,4,128,128]{3,2,1,0:T(8,128)S(1)} all-to-all(f32[2,4,128,128]{3,2,1,0:T(8,128)} %get-tuple-element.13), channel_id=1, replica_groups=mesh['chan'=2,'sky'=16] {'chan'}, dimensions={0} | all-to-all | bytes 1048576 | tf_op jit(solution)/shard_map/all_to_all | solution.py:160
  39.8 0.9 %copy-done.1 = f32[4,128,128]{2,1,0:T(8,128)S(1)} copy-done((f32[4,128,128]{2,1,0:T(8,128)S(1)}, f32[4,128,128]{2,1,0:T(8,128)}, u32[]{:S(2)}) %copy-start.1) | copy-done | bytes 262168
  40.7 0.8 %divide_add_fusion = f32[4,128,128]{2,1,0:T(8,128)} fusion(f32[4,128,128]{2,1,0:T(8,128)S(1)} %copy-done.1, f32[4,128,128]{2,1,0:T(8,128)S(1)} %reduce_sum.27, f32[4]{0:T(128)S(1)} %multiply_reduce_fusion), kind=kLoop, calls=%fused_computation.2 | loop fusion | flops 131072 | bytes 786448 | tf_op jit(solution)/shard_map/add | solution.py:167
  (21 shorter events, 0.1 us)
Async XLA Ops:
  0.6 1.0 %copy-start.9 = (f32[4,4]{1,0:T(4,128)S(1)}, f32[4,4]{1,0:T(4,128)}, u32[]{:S(2)}) copy-start(f32[4,4]{1,0:T(4,128)} %param.8) | copy-start | bytes 196
  6.2 7.3 %copy-start = (bf16[2,256,128]{2,1,0:T(8,128)(2,1)S(1)}, bf16[2,256,128]{2,1,0:T(8,128)(2,1)}, u32[]{:S(2)}) copy-start(bf16[2,256,128]{2,1,0:T(8,128)(2,1)} %dirty_ref.1) | copy-start | bytes 393220
  6.2 7.4 %copy-start.2 = (bf16[2,2,128,128]{3,2,1,0:T(8,128)(2,1)}, bf16[2,2,128,128]{3,2,1,0:T(8,128)(2,1)S(1)}, u32[]{:S(2)}) copy-start(bf16[2,2,128,128]{3,2,1,0:T(8,128)(2,1)S(1)} %copy.9) | copy-start | bytes 393220
  6.2 21.2 %collective-permute-start = (bf16[2,256,128]{2,1,0:T(8,128)(2,1)S(1)}, bf16[2,256,128]{2,1,0:T(8,128)(2,1)S(1)}, u32[]{:S(2)}, u32[]{:S(2)}) collective-permute-start(bf16[2,256,128]{2,1,0:T(8,128)(2,1)S(1)} %bitcast.26), channel_id=1, source_target_pairs={{0,1},{1,2},{2,3},{3,4},{4,5},{5,6},{6,7},{7,8},{8,9},{9,10},{10,1... | collective-permute-start | bytes 393224 | tf_op jit(solution)/shard_map/ppermute | solution.py:18
  9.4 17.9 %collective-permute-start.1 = (bf16[2,256,128]{2,1,0:T(8,128)(2,1)S(1)}, bf16[2,256,128]{2,1,0:T(8,128)(2,1)S(1)}, u32[]{:S(2)}, u32[]{:S(2)}) collective-permute-start(bf16[2,256,128]{2,1,0:T(8,128)(2,1)S(1)} %bitcast.27), channel_id=1, source_target_pairs={{1,0},{2,1},{3,2},{4,3},{5,4},{6,5},{7,6},{8,7},{9,8},{10,9},{11,1... | collective-permute-start | bytes 393224 | tf_op jit(solution)/shard_map/ppermute | solution.py:18
  13.5 7.1 %copy-start.7 = (f32[4,4,129]{2,1,0:T(4,128)S(1)}, f32[4,4,129]{2,1,0:T(4,128)}, u32[]{:S(2)}) copy-start(f32[4,4,129]{2,1,0:T(4,128)} %param.9) | copy-start | bytes 24772
  13.6 13.8 %collective-permute-start.2 = (bf16[2,256,64]{2,1,0:T(8,128)(2,1)S(1)}, bf16[2,256,64]{2,1,0:T(8,128)(2,1)S(1)}, u32[]{:S(2)}, u32[]{:S(2)}) collective-permute-start(bf16[2,256,64]{2,1,0:T(8,128)(2,1)S(1)} %get-tuple-element.23), channel_id=1, source_target_pairs={{0,1},{1,2},{2,3},{3,4},{4,5},{5,6},{6,7},{7,8},{8,9},{9,10},{10,1... | collective-permute-start | bytes 196616 | tf_op jit(solution)/shard_map/ppermute | solution.py:18
  15.5 11.9 %collective-permute-start.3 = (bf16[2,256,64]{2,1,0:T(8,128)(2,1)S(1)}, bf16[2,256,64]{2,1,0:T(8,128)(2,1)S(1)}, u32[]{:S(2)}, u32[]{:S(2)}) collective-permute-start(bf16[2,256,64]{2,1,0:T(8,128)(2,1)S(1)} %get-tuple-element.22), channel_id=1, source_target_pairs={{1,0},{2,1},{3,2},{4,3},{5,4},{6,5},{7,6},{8,7},{9,8},{10,9},{11,1... | collective-permute-start | bytes 196616 | tf_op jit(solution)/shard_map/ppermute | solution.py:18
  20.7 0.7 %copy-start.8 = (f32[4,4,129]{2,1,0:T(4,128)S(1)}, f32[4,4,129]{2,1,0:T(4,128)}, u32[]{:S(2)}) copy-start(f32[4,4,129]{2,1,0:T(4,128)} %param.10) | copy-start | bytes 24772
  27.3 0.6 %copy-start.5 = (bf16[2,256,64]{2,1,0:T(8,128)(2,1)}, bf16[2,256,64]{2,1,0:T(8,128)(2,1)S(1)}, u32[]{:S(2)}) copy-start(bf16[2,256,64]{2,1,0:T(8,128)(2,1)S(1)} %collective-permute-done.2.dl_ref) | copy-start | bytes 196612
  27.3 0.7 %copy-start.6 = (bf16[2,256,64]{2,1,0:T(8,128)(2,1)}, bf16[2,256,64]{2,1,0:T(8,128)(2,1)S(1)}, u32[]{:S(2)}) copy-start(bf16[2,256,64]{2,1,0:T(8,128)(2,1)S(1)} %collective-permute-done.3.dr_ref) | copy-start | bytes 196612
  27.4 0.7 %copy-start.3 = (bf16[2,256,128]{2,1,0:T(8,128)(2,1)}, bf16[2,256,128]{2,1,0:T(8,128)(2,1)S(1)}, u32[]{:S(2)}) copy-start(bf16[2,256,128]{2,1,0:T(8,128)(2,1)S(1)} %collective-permute-done.xl_ref) | copy-start | bytes 393220
  27.4 0.7 %copy-start.4 = (bf16[2,256,128]{2,1,0:T(8,128)(2,1)}, bf16[2,256,128]{2,1,0:T(8,128)(2,1)S(1)}, u32[]{:S(2)}) copy-start(bf16[2,256,128]{2,1,0:T(8,128)(2,1)S(1)} %collective-permute-done.1.xr_ref) | copy-start | bytes 393220
  39.7 0.9 %copy-start.1 = (f32[4,128,128]{2,1,0:T(8,128)S(1)}, f32[4,128,128]{2,1,0:T(8,128)}, u32[]{:S(2)}) copy-start(f32[4,128,128]{2,1,0:T(8,128)} %param.7) | copy-start | bytes 786436

commit v3 on v2

v3 whole, which is shorter than its diff:
```python
import functools

import jax
import jax.numpy as jnp
from jax import lax
from jax.experimental import pallas as pl
from jax.experimental.pallas import tpu as pltpu
from jax.sharding import PartitionSpec as P

TAPS = 129
HALF = (TAPS - 1) // 2
LANES = 512


def from_behind(value, axis, steps):
    count = lax.axis_size(axis)
    first, last = (max(0, -steps), min(count, count - steps))
    return lax.ppermute(value, axis, [(source, source + steps) for source in range(first, last)])


def col_band(w, slot):
    ext = slot + 2 * HALF
    spread = jnp.broadcast_to(w[:, :ext], (ext, ext))
    return pltpu.roll(spread, ext - 2 * HALF, 1, stride=1, stride_axis=0)[:, :slot]


def row_band(w, rows):
    spread = jnp.broadcast_to(w, (rows, LANES))
    return pltpu.roll(spread, LANES - HALF, 1, stride=1, stride_axis=0)[:, :rows]


def row_pass(row_ref, col_pass, rank_count, slot):
    total = None
    for r in range(rank_count):
        part = jnp.dot(
            row_ref[r], col_pass[:, r * slot : (r + 1) * slot], preferred_element_type=jnp.float32
        )
        total = part if total is None else total + part
    return total


def main_kernel(
    rank_count, local_chans, sky_count, spec_ref, taps_ref, left_ref, xc_ref, right_ref, dirty_ref,
    res_ref, part_ref, colf_ref, rowf_ref, cola_ref, rowa_ref,
):
    slot = xc_ref.shape[-1]
    rows = xc_ref.shape[1]
    pieces, basis, piece_rows, _ = part_ref.shape
    first_chan = lax.axis_index("chan") * local_chans
    sky_index = lax.axis_index("sky")
    lane = lax.broadcasted_iota(jnp.int32, (rows, slot), 1)
    flip = (
        lax.broadcasted_iota(jnp.int32, (LANES // 2, LANES), 0)
        + lax.broadcasted_iota(jnp.int32, (LANES // 2, LANES), 1)
        == TAPS - 1
    ).astype(jnp.bfloat16)
    for c in range(local_chans):
        taps = taps_ref[first_chan + c].astype(jnp.bfloat16)
        rev = jnp.dot(taps[:, : LANES // 2], flip, preferred_element_type=jnp.float32)
        taps = taps.astype(jnp.float32)
        for r in range(rank_count):
            u, v = taps[r : r + 1], taps[rank_count + r : rank_count + r + 1]
            u_rev, v_rev = rev[r : r + 1], rev[rank_count + r : rank_count + r + 1]
            colf_ref[:, r * slot : (r + 1) * slot] = col_band(v_rev, slot).astype(jnp.bfloat16)
            cola_ref[:, r * slot : (r + 1) * slot] = col_band(v, slot).astype(jnp.bfloat16)
            rowf_ref[r] = row_band(u, rows).astype(jnp.bfloat16)
            rowa_ref[r] = row_band(u_rev, rows).astype(jnp.bfloat16)
        band = colf_ref[...]
        xl, xc, xr = left_ref[c, :, :slot], xc_ref[c], right_ref[c, :, :slot]
        low = (
            jnp.dot(xl, band[:slot], preferred_element_type=jnp.float32)
            + jnp.dot(xc, band[slot:], preferred_element_type=jnp.float32)
        ).astype(jnp.bfloat16)
        high = (
            jnp.dot(xc, band[:slot], preferred_element_type=jnp.float32)
            + jnp.dot(xr, band[slot:], preferred_element_type=jnp.float32)
        ).astype(jnp.bfloat16)
        pred_low = row_pass(rowf_ref, low, rank_count, slot)
        pred_high = row_pass(rowf_ref, high, rank_count, slot)
        pred_own = pltpu.roll(jnp.where(lane < HALF, pred_high, pred_low), HALF, 1)
        res_own = (dirty_ref[c].astype(jnp.float32) - pred_own).astype(jnp.bfloat16)
        res_ref[c] = res_own
        dl = left_ref[c, :, slot : slot + HALF].astype(jnp.float32)
        dr = right_ref[c, :, slot : slot + HALF].astype(jnp.float32)
        halo_l = jnp.where(sky_index > 0, dl - pred_low[:, :HALF], 0.0)
        pred_right = pltpu.roll(pred_high, slot - HALF, 1)[:, :HALF]
        halo_r = jnp.where(sky_index < sky_count - 1, dr - pred_right, 0.0)
        adj = cola_ref[...]
        col_pass = (
            jnp.dot(halo_l.astype(jnp.bfloat16), adj[:HALF], preferred_element_type=jnp.float32)
            + jnp.dot(res_own, adj[HALF : HALF + slot], preferred_element_type=jnp.float32)
            + jnp.dot(halo_r.astype(jnp.bfloat16), adj[HALF + slot :], preferred_element_type=jnp.float32)
        ).astype(jnp.bfloat16)
        grad_chan = row_pass(rowa_ref, col_pass, rank_count, slot)
        for j in range(pieces):
            block = grad_chan[j * piece_rows : (j + 1) * piece_rows]
            for b in range(basis):
                term = spec_ref[first_chan + c, b] * block
                if c == 0:
                    part_ref[j, b] = term
                else:
                    part_ref[j, b] = part_ref[j, b] + term


def vmem_spec():
    return pl.BlockSpec(memory_space=pltpu.VMEM)


def smem_spec():
    return pl.BlockSpec(memory_space=pltpu.SMEM)


def body(dirty, model, spectral, psf_rows, psf_cols, strip_width):
    local_chans, row_count, slot_width = dirty.shape
    basis = model.shape[0]
    rank_count = psf_rows.shape[1]
    chan_count = lax.axis_size("chan")
    sky_count = lax.axis_size("sky")

    image_rows = spectral[:, 0][:, None, None] * model[0][None]
    for basis_idx in range(1, basis):
        image_rows = image_rows + spectral[:, basis_idx][:, None, None] * model[basis_idx][None]
    image_rows = image_rows.astype(jnp.bfloat16)
    image = lax.all_to_all(image_rows, "chan", 0, 1, tiled=True)
    to_right = jnp.concatenate([image, dirty[:, :, slot_width - HALF :]], axis=2)
    to_left = jnp.concatenate([image, dirty[:, :, :HALF]], axis=2)
    left = from_behind(to_right, "sky", 1)
    right = from_behind(to_left, "sky", -1)

    taps = jnp.concatenate([psf_rows, psf_cols], axis=1)
    taps = jnp.pad(taps, ((0, 0), (0, 0), (0, LANES - TAPS)))
    piece_rows = row_count // chan_count
    ext = slot_width + 2 * HALF
    residual, partial_value = pl.pallas_call(
        functools.partial(main_kernel, rank_count, local_chans, sky_count),
        out_shape=(
            jax.ShapeDtypeStruct(dirty.shape, jnp.bfloat16),
            jax.ShapeDtypeStruct((chan_count, basis, piece_rows, slot_width), jnp.float32),
        ),
        in_specs=[smem_spec()] + [vmem_spec()] * 5,
        out_specs=[vmem_spec()] * 2,
        scratch_shapes=[
            pltpu.VMEM((ext, rank_count * slot_width), jnp.bfloat16),
            pltpu.VMEM((rank_count, row_count, row_count), jnp.bfloat16),
            pltpu.VMEM((ext, rank_count * slot_width), jnp.bfloat16),
            pltpu.VMEM((rank_count, row_count, row_count), jnp.bfloat16),
        ],
    )(spectral, taps, left, image, right, dirty)

    pieces = lax.all_to_all(partial_value, "chan", 0, 0, tiled=True)
    grad_share = pieces.sum(0)

    gram_rows = jnp.einsum("crt,cst->crs", psf_rows, psf_rows, precision=lax.Precision.HIGHEST)
    gram_cols = jnp.einsum("crt,cst->crs", psf_cols, psf_cols, precision=lax.Precision.HIGHEST)
    energy = jnp.sum(gram_rows * gram_cols, axis=(1, 2))
    curvature = jnp.sum(spectral * spectral * energy[:, None], axis=0)
    model_new = model + grad_share / curvature[:, None, None]
    return (residual, model_new)


def solution(mesh):
    placed = (P("chan", None, "sky"), P(None, "chan", "sky"), P(), P(), P(), P())
    return jax.shard_map(
        body,
        mesh=mesh,
        in_specs=placed,
        out_specs=(P("chan", None, "sky"), P(None, "chan", "sky")),
        check_vma=False,
    )
```

time: 42 us -> 39 us (0.929)
  the two profiles are of different devices: /device:TPU:25 before, /device:TPU:0 now
where the time goes in v3:
time: 39 us; the launch traced here: 38.5 us
  waiting for transfers between devices  10.9 us (28%)
  blocking collectives  9.05 us (23%)
  starting transfers between devices  6.15 us (16%)
  Pallas kernels  5.07 us (13%)
  local copies, waits for them, and re-layouts  4.36 us (11%)
  other arithmetic  1.81 us (5%)
  between operations  0.71 us (2%)
  matrix products  0.44 us (1%)
    ppermute x2, waiting for transfers between devices, from_behind(): lax.ppermute(value, axis, [(source, source + steps) for source in range(f...  10.9 us
    ppermute x2, starting transfers between devices, from_behind(): lax.ppermute(value, axis, [(source, source + steps) for source in range(f...  6.15 us
    all_to_all x1, blocking collectives, body(): pieces = lax.all_to_all(partial_value, 'chan', 0, 0, tiled=True)  5.21 us
    pallas_call x1, Pallas kernels, body(): pl.pallas_call(functools.partial(main_kernel, rank_count, local_chans, sk...  5.07 us
    all_to_all x1, blocking collectives, body(): image = lax.all_to_all(image_rows, 'chan', 0, 1, tiled=True)  3.84 us
    unnamed x16, local copies, waits for them, and re-layouts  3.07 us
    mul x1, local copies, waits for them, and re-layouts, body(): image_rows = spectral[:, 0][:, None, None] * model[0][None]  0.96 us
    add x1, other arithmetic, body(): model_new = model + grad_share / curvature[:, None, None]  0.8 us
  transfers between devices with their start and end apart: 2, of which 2 were waited for; matrix products, arithmetic and copies ran while one was open for 3% of the time, Pallas kernels for 0%

profile of v3, /device:TPU:0, one launch (start us, length us, event | category | flops | bytes accessed | tf_op | source)
XLA Modules:
  0.0 38.5 jit_solution(15846389184131986174)
XLA Ops:
  0.6 0.0 copy-start.7
  0.6 1.0 %slice_bitcast_fusion.3 = (f32[128,128]{1,0:T(8,128)S(1)}, f32[128,128]{1,0:T(8,128)S(1)}, f32[128,128]{1,0:T(8,128)S(1)}, f32[128,128]{1,0:T(8,128)S(1)}) fusion(f32[4,128,128]{2,1,0:T(8,128)} %param.7), kind=kLoop, calls=%fused_computation.11 | loop fusion | bytes 524288 | tf_op jit(solution)/shard_map/mul | solution.py:120
  1.6 0.0 copy-done.7
  1.6 0.2 slice_reduce_fusion.3
  1.8 0.2 add_convert_fusion
  2.0 3.8 %all_to_all.23 = bf16[4,128,128]{2,1,0:T(8,128)(2,1)S(1)} all-to-all(bf16[4,128,128]{2,1,0:T(8,128)(2,1)S(1)} %add_convert_fusion), channel_id=1, replica_groups=mesh['chan'=2,'sky'=16] {'chan'}, dimensions={0} | all-to-all | bytes 262144 | tf_op jit(solution)/shard_map/all_to_all | solution.py:124
  5.8 0.0 copy-start.1
  5.8 0.9 %copy-done.1 = bf16[2,256,128]{2,1,0:T(8,128)(2,1)S(1)} copy-done((bf16[2,256,128]{2,1,0:T(8,128)(2,1)S(1)}, bf16[2,256,128]{2,1,0:T(8,128)(2,1)}, u32[]{:S(2)}) %copy-start.1) | copy-done | bytes 131096
  6.7 0.0 copy-start
  6.7 0.1 fusion.1
  6.9 0.5 %copy-done = bf16[2,2,128,128]{3,2,1,0:T(8,128)(2,1)} copy-done((bf16[2,2,128,128]{3,2,1,0:T(8,128)(2,1)}, bf16[2,2,128,128]{3,2,1,0:T(8,128)(2,1)S(1)}, u32[]{:S(2)}) %copy-start) | copy-done | bytes 131096
  7.4 0.0 copy-start.5
  7.4 0.1 pad_maximum_fusion
  7.5 4.9 %collective-permute-start = (bf16[2,256,192]{2,1,0:T(8,128)(2,1)S(1)}, bf16[2,256,192]{2,1,0:T(8,128)(2,1)S(1)}, u32[]{:S(2)}, u32[]{:S(2)}) collective-permute-start(bf16[2,256,192]{2,1,0:T(8,128)(2,1)S(1)} %get-tuple-element.15), channel_id=1, source_target_pairs={{0,1},{1,2},{2,3},{3,4},{4,5},{5,6},{6,7},{7,8},{8,9},{9,10},{10,1... | collective-permute-start | bytes 589832 | tf_op jit(solution)/shard_map/ppermute | solution.py:18
  12.3 0.0 copy-start.6
  12.4 1.3 %collective-permute-start.1 = (bf16[2,256,192]{2,1,0:T(8,128)(2,1)S(1)}, bf16[2,256,192]{2,1,0:T(8,128)(2,1)S(1)}, u32[]{:S(2)}, u32[]{:S(2)}) collective-permute-start(bf16[2,256,192]{2,1,0:T(8,128)(2,1)S(1)} %get-tuple-element.14), channel_id=1, source_target_pairs={{1,0},{2,1},{3,2},{4,3},{5,4},{6,5},{7,6},{8,7},{9,8},{10,9},{11,1... | collective-permute-start | bytes 589832 | tf_op jit(solution)/shard_map/ppermute | solution.py:18
  13.7 0.0 copy-done.5
  13.7 0.2 fusion.2
  13.8 0.0 copy-done.6
  13.8 0.3 fusion
  14.1 0.1 multiply_reduce_fusion
  14.2 0.6 %select_maximum_fusion.taps_ref = f32[4,8,512]{2,1,0:T(8,128)} fusion(f32[4,4,129]{2,1,0:T(4,128)S(1)} %copy-done.6, f32[4,4,129]{2,1,0:T(4,128)S(1)} %copy-done.5), kind=kLoop, calls=%fused_computation.6 | loop fusion | flops 65536 | bytes 82048 | tf_op jit(solution)/shard_map/concatenate | solution.py:130
  14.8 9.0 %collective-permute-done.left_ref = bf16[2,256,192]{2,1,0:T(8,128)(2,1)S(1)} collective-permute-done((bf16[2,256,192]{2,1,0:T(8,128)(2,1)S(1)}, bf16[2,256,192]{2,1,0:T(8,128)(2,1)S(1)}, u32[]{:S(2)}, u32[]{:S(2)}) %collective-permute-start) | collective-permute-done | bytes 196640 | tf_op jit(solution)/shard_map/ppermute | solution.py:18
  23.9 0.0 copy-start.3
  23.9 1.9 %collective-permute-done.1.right_ref = bf16[2,256,192]{2,1,0:T(8,128)(2,1)S(1)} collective-permute-done((bf16[2,256,192]{2,1,0:T(8,128)(2,1)S(1)}, bf16[2,256,192]{2,1,0:T(8,128)(2,1)S(1)}, u32[]{:S(2)}, u32[]{:S(2)}) %collective-permute-start.1) | collective-permute-done | bytes 196640 | tf_op jit(solution)/shard_map/ppermute | solution.py:18
  25.8 0.0 copy-done.3
  25.8 0.7 %copy-done.4 = bf16[2,256,192]{2,1,0:T(8,128)(2,1)} copy-done((bf16[2,256,192]{2,1,0:T(8,128)(2,1)}, bf16[2,256,192]{2,1,0:T(8,128)(2,1)S(1)}, u32[]{:S(2)}) %copy-start.4) | copy-done | bytes 196632
  26.5 5.1 %shard_map.68 = (bf16[2,256,128]{2,1,0:T(8,128)(2,1)}, f32[2,4,128,128]{3,2,1,0:T(8,128)}) custom-call(f32[4,4]{1,0:T(4,128)} %spec_ref.1, f32[4,8,512]{2,1,0:T(8,128)} %select_maximum_fusion.taps_ref, bf16[2,256,192]{2,1,0:T(8,128)(2,1)} %copy-done.3, bf16[2,256,128]{2,1,0:T(8,128)(2,1)} %bitcast.17, bf16[2,256,192]{2,1,0:T(8,128)(2,1)} %copy-done.4, ...), custom_call_target="tpu_custom_call" | custom-call | tf_op jit(solution)/shard_map/pallas_call | solution.py:134
  31.5 5.2 %all_to_all.24 = f32[2,4,128,128]{3,2,1,0:T(8,128)S(1)} all-to-all(f32[2,4,128,128]{3,2,1,0:T(8,128)} %get-tuple-element.5), channel_id=1, replica_groups=mesh['chan'=2,'sky'=16] {'chan'}, dimensions={0} | all-to-all | bytes 1048576 | tf_op jit(solution)/shard_map/all_to_all | solution.py:150
  36.8 0.0 copy-start.2
  36.8 0.9 %copy-done.2 = f32[4,128,128]{2,1,0:T(8,128)S(1)} copy-done((f32[4,128,128]{2,1,0:T(8,128)S(1)}, f32[4,128,128]{2,1,0:T(8,128)}, u32[]{:S(2)}) %copy-start.2) | copy-done | bytes 262168
  37.7 0.8 %divide_add_fusion = f32[4,128,128]{2,1,0:T(8,128)} fusion(f32[4,128,128]{2,1,0:T(8,128)S(1)} %copy-done.2, f32[4,128,128]{2,1,0:T(8,128)S(1)} %reduce_sum.27, f32[4]{0:T(128)S(1)} %multiply_reduce_fusion), kind=kLoop, calls=%fused_computation.4 | loop fusion | flops 131072 | bytes 786448 | tf_op jit(solution)/shard_map/add | solution.py:157
  (3 shorter events, 0.0 us)
Async XLA Ops:
  0.6 1.0 %copy-start.7 = (f32[4,4]{1,0:T(4,128)S(1)}, f32[4,4]{1,0:T(4,128)}, u32[]{:S(2)}) copy-start(f32[4,4]{1,0:T(4,128)} %spec_ref.1) | copy-start | bytes 196
  5.8 0.9 %copy-start.1 = (bf16[2,256,128]{2,1,0:T(8,128)(2,1)S(1)}, bf16[2,256,128]{2,1,0:T(8,128)(2,1)}, u32[]{:S(2)}) copy-start(bf16[2,256,128]{2,1,0:T(8,128)(2,1)} %dirty_ref.1) | copy-start | bytes 393220
  6.7 0.6 %copy-start = (bf16[2,2,128,128]{3,2,1,0:T(8,128)(2,1)}, bf16[2,2,128,128]{3,2,1,0:T(8,128)(2,1)S(1)}, u32[]{:S(2)}) copy-start(bf16[2,2,128,128]{3,2,1,0:T(8,128)(2,1)S(1)} %copy.7) | copy-start | bytes 393220
  7.4 6.3 %copy-start.5 = (f32[4,4,129]{2,1,0:T(4,128)S(1)}, f32[4,4,129]{2,1,0:T(4,128)}, u32[]{:S(2)}) copy-start(f32[4,4,129]{2,1,0:T(4,128)} %param.9) | copy-start | bytes 24772
  7.5 16.4 %collective-permute-start = (bf16[2,256,192]{2,1,0:T(8,128)(2,1)S(1)}, bf16[2,256,192]{2,1,0:T(8,128)(2,1)S(1)}, u32[]{:S(2)}, u32[]{:S(2)}) collective-permute-start(bf16[2,256,192]{2,1,0:T(8,128)(2,1)S(1)} %get-tuple-element.15), channel_id=1, source_target_pairs={{0,1},{1,2},{2,3},{3,4},{4,5},{5,6},{6,7},{7,8},{8,9},{9,10},{10,1... | collective-permute-start | bytes 589832 | tf_op jit(solution)/shard_map/ppermute | solution.py:18
  12.3 1.5 %copy-start.6 = (f32[4,4,129]{2,1,0:T(4,128)S(1)}, f32[4,4,129]{2,1,0:T(4,128)}, u32[]{:S(2)}) copy-start(f32[4,4,129]{2,1,0:T(4,128)} %param.10) | copy-start | bytes 24772
  12.4 13.4 %collective-permute-start.1 = (bf16[2,256,192]{2,1,0:T(8,128)(2,1)S(1)}, bf16[2,256,192]{2,1,0:T(8,128)(2,1)S(1)}, u32[]{:S(2)}, u32[]{:S(2)}) collective-permute-start(bf16[2,256,192]{2,1,0:T(8,128)(2,1)S(1)} %get-tuple-element.14), channel_id=1, source_target_pairs={{1,0},{2,1},{3,2},{4,3},{5,4},{6,5},{7,6},{8,7},{9,8},{10,9},{11,1... | collective-permute-start | bytes 589832 | tf_op jit(solution)/shard_map/ppermute | solution.py:18
  23.9 1.9 %copy-start.3 = (bf16[2,256,192]{2,1,0:T(8,128)(2,1)}, bf16[2,256,192]{2,1,0:T(8,128)(2,1)S(1)}, u32[]{:S(2)}) copy-start(bf16[2,256,192]{2,1,0:T(8,128)(2,1)S(1)} %collective-permute-done.left_ref) | copy-start | bytes 589828
  25.8 0.7 %copy-start.4 = (bf16[2,256,192]{2,1,0:T(8,128)(2,1)}, bf16[2,256,192]{2,1,0:T(8,128)(2,1)S(1)}, u32[]{:S(2)}) copy-start(bf16[2,256,192]{2,1,0:T(8,128)(2,1)S(1)} %collective-permute-done.1.right_ref) | copy-start | bytes 589828
  36.8 1.0 %copy-start.2 = (f32[4,128,128]{2,1,0:T(8,128)S(1)}, f32[4,128,128]{2,1,0:T(8,128)}, u32[]{:S(2)}) copy-start(f32[4,128,128]{2,1,0:T(8,128)} %param.7) | copy-start | bytes 786436

commit v4 on v3

--- a/solution.py
+++ b/solution.py
@@ -39,6 +39,10 @@
     return total
 
 
+def unpack_cols(packed):
+    return jnp.concatenate([packed[:, :HALF], pltpu.roll(packed, HALF, 1)[:, :HALF]], axis=0)
+
+
 def main_kernel(
     rank_count, local_chans, sky_count, spec_ref, taps_ref, left_ref, xc_ref, right_ref, dirty_ref,
     res_ref, part_ref, colf_ref, rowf_ref, cola_ref, rowa_ref,
@@ -66,7 +70,7 @@
             rowf_ref[r] = row_band(u, rows).astype(jnp.bfloat16)
             rowa_ref[r] = row_band(u_rev, rows).astype(jnp.bfloat16)
         band = colf_ref[...]
-        xl, xc, xr = left_ref[c, :, :slot], xc_ref[c], right_ref[c, :, :slot]
+        xl, xc, xr = left_ref[c, :rows], xc_ref[c], right_ref[c, :rows]
         low = (
             jnp.dot(xl, band[:slot], preferred_element_type=jnp.float32)
             + jnp.dot(xc, band[slot:], preferred_element_type=jnp.float32)
@@ -80,8 +84,8 @@
         pred_own = pltpu.roll(jnp.where(lane < HALF, pred_high, pred_low), HALF, 1)
         res_own = (dirty_ref[c].astype(jnp.float32) - pred_own).astype(jnp.bfloat16)
         res_ref[c] = res_own
-        dl = left_ref[c, :, slot : slot + HALF].astype(jnp.float32)
-        dr = right_ref[c, :, slot : slot + HALF].astype(jnp.float32)
+        dl = unpack_cols(left_ref[c, rows:]).astype(jnp.float32)
+        dr = unpack_cols(right_ref[c, rows:]).astype(jnp.float32)
         halo_l = jnp.where(sky_index > 0, dl - pred_low[:, :HALF], 0.0)
         pred_right = pltpu.roll(pred_high, slot - HALF, 1)[:, :HALF]
         halo_r = jnp.where(sky_index < sky_count - 1, dr - pred_right, 0.0)
@@ -122,8 +126,11 @@
         image_rows = image_rows + spectral[:, basis_idx][:, None, None] * model[basis_idx][None]
     image_rows = image_rows.astype(jnp.bfloat16)
     image = lax.all_to_all(image_rows, "chan", 0, 1, tiled=True)
-    to_right = jnp.concatenate([image, dirty[:, :, slot_width - HALF :]], axis=2)
-    to_left = jnp.concatenate([image, dirty[:, :, :HALF]], axis=2)
+    def with_dirty(cols):
+        return jnp.concatenate([image, jnp.concatenate([cols[:, : row_count // 2], cols[:, row_count // 2 :]], axis=2)], axis=1)
+
+    to_right = with_dirty(dirty[:, :, slot_width - HALF :])
+    to_left = with_dirty(dirty[:, :, :HALF])
     left = from_behind(to_right, "sky", 1)
     right = from_behind(to_left, "sky", -1)
 

time: 39 us -> 36.2 us (0.928)
  waiting for transfers between devices: 10.9 us -> 8.12 us
    ppermute x2, waiting for transfers between devices: 10.9 us -> 8.12 us  [from_behind(): lax.ppermute(value, axis, [(source, source + steps) for source in range(f...]
where the time goes in v4:
time: 36.2 us; the launch traced here: 35.7 us
  blocking collectives  9.05 us (25%)
  waiting for transfers between devices  8.12 us (22%)
  starting transfers between devices  6.15 us (17%)
  Pallas kernels  5.13 us (14%)
  local copies, waits for them, and re-layouts  4.32 us (12%)
  other arithmetic  1.82 us (5%)
  between operations  0.71 us (2%)
  matrix products  0.44 us (1%)
    ppermute x2, waiting for transfers between devices, from_behind(): lax.ppermute(value, axis, [(source, source + steps) for source in range(f...  8.12 us
    ppermute x2, starting transfers between devices, from_behind(): lax.ppermute(value, axis, [(source, source + steps) for source in range(f...  6.15 us
    all_to_all x1, blocking collectives, body(): pieces = lax.all_to_all(partial_value, 'chan', 0, 0, tiled=True)  5.21 us
    pallas_call x1, Pallas kernels, body(): pl.pallas_call(functools.partial(main_kernel, rank_count, local_chans, sk...  5.13 us
    all_to_all x1, blocking collectives, body(): image = lax.all_to_all(image_rows, 'chan', 0, 1, tiled=True)  3.84 us
    unnamed x16, local copies, waits for them, and re-layouts  3.03 us
    mul x1, local copies, waits for them, and re-layouts, body(): image_rows = spectral[:, 0][:, None, None] * model[0][None]  0.96 us
    add x1, other arithmetic, body(): model_new = model + grad_share / curvature[:, None, None]  0.8 us
  transfers between devices with their start and end apart: 2, of which 2 were waited for; matrix products, arithmetic and copies ran while one was open for 3% of the time, Pallas kernels for 0%

profile of v4, /device:TPU:0, one launch (start us, length us, event | category | flops | bytes accessed | tf_op | source)
XLA Modules:
  0.0 35.7 jit_solution(13407869350130030620)
XLA Ops:
  0.6 0.0 copy-start.7
  0.6 1.0 %slice_bitcast_fusion.3 = (f32[128,128]{1,0:T(8,128)S(1)}, f32[128,128]{1,0:T(8,128)S(1)}, f32[128,128]{1,0:T(8,128)S(1)}, f32[128,128]{1,0:T(8,128)S(1)}) fusion(f32[4,128,128]{2,1,0:T(8,128)} %param.7), kind=kLoop, calls=%fused_computation.11 | loop fusion | bytes 524288 | tf_op jit(solution)/shard_map/mul | solution.py:124
  1.6 0.0 copy-done.7
  1.6 0.2 slice_reduce_fusion.3
  1.8 0.2 add_convert_fusion
  2.0 3.8 %all_to_all.23 = bf16[4,128,128]{2,1,0:T(8,128)(2,1)S(1)} all-to-all(bf16[4,128,128]{2,1,0:T(8,128)(2,1)S(1)} %add_convert_fusion), channel_id=1, replica_groups=mesh['chan'=2,'sky'=16] {'chan'}, dimensions={0} | all-to-all | bytes 262144 | tf_op jit(solution)/shard_map/all_to_all | solution.py:128
  5.8 0.0 copy-start
  5.8 0.9 %copy-done = bf16[2,256,128]{2,1,0:T(8,128)(2,1)S(1)} copy-done((bf16[2,256,128]{2,1,0:T(8,128)(2,1)S(1)}, bf16[2,256,128]{2,1,0:T(8,128)(2,1)}, u32[]{:S(2)}) %copy-start) | copy-done | bytes 131096
  6.7 0.0 copy-start.1
  6.7 0.1 fusion.1
  6.9 0.5 %copy-done.1 = bf16[2,2,128,128]{3,2,1,0:T(8,128)(2,1)} copy-done((bf16[2,2,128,128]{3,2,1,0:T(8,128)(2,1)}, bf16[2,2,128,128]{3,2,1,0:T(8,128)(2,1)S(1)}, u32[]{:S(2)}) %copy-start.1) | copy-done | bytes 131096
  7.4 0.0 copy-start.5
  7.4 0.1 pad_maximum_fusion
  7.5 4.9 %collective-permute-start = (bf16[2,384,128]{2,1,0:T(8,128)(2,1)S(1)}, bf16[2,384,128]{2,1,0:T(8,128)(2,1)S(1)}, u32[]{:S(2)}, u32[]{:S(2)}) collective-permute-start(bf16[2,384,128]{2,1,0:T(8,128)(2,1)S(1)} %get-tuple-element.15), channel_id=1, source_target_pairs={{0,1},{1,2},{2,3},{3,4},{4,5},{5,6},{6,7},{7,8},{8,9},{9,10},{10,1... | collective-permute-start | bytes 589832 | tf_op jit(solution)/shard_map/ppermute | solution.py:18
  12.4 0.0 copy-start.6
  12.4 1.3 %collective-permute-start.1 = (bf16[2,384,128]{2,1,0:T(8,128)(2,1)S(1)}, bf16[2,384,128]{2,1,0:T(8,128)(2,1)S(1)}, u32[]{:S(2)}, u32[]{:S(2)}) collective-permute-start(bf16[2,384,128]{2,1,0:T(8,128)(2,1)S(1)} %get-tuple-element.14), channel_id=1, source_target_pairs={{1,0},{2,1},{3,2},{4,3},{5,4},{6,5},{7,6},{8,7},{9,8},{10,9},{11,1... | collective-permute-start | bytes 589832 | tf_op jit(solution)/shard_map/ppermute | solution.py:18
  13.7 0.0 copy-done.5
  13.7 0.2 fusion.2
  13.8 0.0 copy-done.6
  13.8 0.3 fusion
  14.1 0.1 multiply_reduce_fusion
  14.2 0.6 %select_maximum_fusion.taps_ref = f32[4,8,512]{2,1,0:T(8,128)} fusion(f32[4,4,129]{2,1,0:T(4,128)S(1)} %copy-done.6, f32[4,4,129]{2,1,0:T(4,128)S(1)} %copy-done.5), kind=kLoop, calls=%fused_computation.6 | loop fusion | flops 65536 | bytes 82048 | tf_op jit(solution)/shard_map/concatenate | solution.py:137
  14.8 2.0 %collective-permute-done.left_ref = bf16[2,384,128]{2,1,0:T(8,128)(2,1)S(1)} collective-permute-done((bf16[2,384,128]{2,1,0:T(8,128)(2,1)S(1)}, bf16[2,384,128]{2,1,0:T(8,128)(2,1)S(1)}, u32[]{:S(2)}, u32[]{:S(2)}) %collective-permute-start) | collective-permute-done | bytes 196640 | tf_op jit(solution)/shard_map/ppermute | solution.py:18
  16.8 0.0 copy-start.3
  16.8 6.2 %collective-permute-done.1.right_ref = bf16[2,384,128]{2,1,0:T(8,128)(2,1)S(1)} collective-permute-done((bf16[2,384,128]{2,1,0:T(8,128)(2,1)S(1)}, bf16[2,384,128]{2,1,0:T(8,128)(2,1)S(1)}, u32[]{:S(2)}, u32[]{:S(2)}) %collective-permute-start.1) | collective-permute-done | bytes 196640 | tf_op jit(solution)/shard_map/ppermute | solution.py:18
  23.0 0.0 copy-done.3
  23.0 0.0 copy-start.4
  23.0 0.7 %copy-done.4 = bf16[2,384,128]{2,1,0:T(8,128)(2,1)} copy-done((bf16[2,384,128]{2,1,0:T(8,128)(2,1)}, bf16[2,384,128]{2,1,0:T(8,128)(2,1)S(1)}, u32[]{:S(2)}) %copy-start.4) | copy-done | bytes 196632
  23.6 5.1 %shard_map.68 = (bf16[2,256,128]{2,1,0:T(8,128)(2,1)}, f32[2,4,128,128]{3,2,1,0:T(8,128)}) custom-call(f32[4,4]{1,0:T(4,128)} %spec_ref.1, f32[4,8,512]{2,1,0:T(8,128)} %select_maximum_fusion.taps_ref, bf16[2,384,128]{2,1,0:T(8,128)(2,1)} %copy-done.3, bf16[2,256,128]{2,1,0:T(8,128)(2,1)} %bitcast.17, bf16[2,384,128]{2,1,0:T(8,128)(2,1)} %copy-done.4, ...), custom_call_target="tpu_custom_call" | custom-call | tf_op jit(solution)/shard_map/pallas_call | solution.py:141
  28.8 5.2 %all_to_all.24 = f32[2,4,128,128]{3,2,1,0:T(8,128)S(1)} all-to-all(f32[2,4,128,128]{3,2,1,0:T(8,128)} %get-tuple-element.5), channel_id=1, replica_groups=mesh['chan'=2,'sky'=16] {'chan'}, dimensions={0} | all-to-all | bytes 1048576 | tf_op jit(solution)/shard_map/all_to_all | solution.py:157
  34.0 0.9 %copy-done.2 = f32[4,128,128]{2,1,0:T(8,128)S(1)} copy-done((f32[4,128,128]{2,1,0:T(8,128)S(1)}, f32[4,128,128]{2,1,0:T(8,128)}, u32[]{:S(2)}) %copy-start.2) | copy-done | bytes 262168
  34.9 0.8 %divide_add_fusion = f32[4,128,128]{2,1,0:T(8,128)} fusion(f32[4,128,128]{2,1,0:T(8,128)S(1)} %copy-done.2, f32[4,128,128]{2,1,0:T(8,128)S(1)} %reduce_sum.27, f32[4]{0:T(128)S(1)} %multiply_reduce_fusion), kind=kLoop, calls=%fused_computation.2 | loop fusion | flops 131072 | bytes 786448 | tf_op jit(solution)/shard_map/add | solution.py:164
  (3 shorter events, 0.0 us)
Async XLA Ops:
  0.6 1.0 %copy-start.7 = (f32[4,4]{1,0:T(4,128)S(1)}, f32[4,4]{1,0:T(4,128)}, u32[]{:S(2)}) copy-start(f32[4,4]{1,0:T(4,128)} %spec_ref.1) | copy-start | bytes 196
  5.8 0.9 %copy-start = (bf16[2,256,128]{2,1,0:T(8,128)(2,1)S(1)}, bf16[2,256,128]{2,1,0:T(8,128)(2,1)}, u32[]{:S(2)}) copy-start(bf16[2,256,128]{2,1,0:T(8,128)(2,1)} %dirty_ref.1) | copy-start | bytes 393220
  6.7 0.6 %copy-start.1 = (bf16[2,2,128,128]{3,2,1,0:T(8,128)(2,1)}, bf16[2,2,128,128]{3,2,1,0:T(8,128)(2,1)S(1)}, u32[]{:S(2)}) copy-start(bf16[2,2,128,128]{3,2,1,0:T(8,128)(2,1)S(1)} %copy.7) | copy-start | bytes 393220
  7.4 6.3 %copy-start.5 = (f32[4,4,129]{2,1,0:T(4,128)S(1)}, f32[4,4,129]{2,1,0:T(4,128)}, u32[]{:S(2)}) copy-start(f32[4,4,129]{2,1,0:T(4,128)} %param.9) | copy-start | bytes 24772
  7.5 9.3 %collective-permute-start = (bf16[2,384,128]{2,1,0:T(8,128)(2,1)S(1)}, bf16[2,384,128]{2,1,0:T(8,128)(2,1)S(1)}, u32[]{:S(2)}, u32[]{:S(2)}) collective-permute-start(bf16[2,384,128]{2,1,0:T(8,128)(2,1)S(1)} %get-tuple-element.15), channel_id=1, source_target_pairs={{0,1},{1,2},{2,3},{3,4},{4,5},{5,6},{6,7},{7,8},{8,9},{9,10},{10,1... | collective-permute-start | bytes 589832 | tf_op jit(solution)/shard_map/ppermute | solution.py:18
  12.4 1.5 %copy-start.6 = (f32[4,4,129]{2,1,0:T(4,128)S(1)}, f32[4,4,129]{2,1,0:T(4,128)}, u32[]{:S(2)}) copy-start(f32[4,4,129]{2,1,0:T(4,128)} %param.10) | copy-start | bytes 24772
  12.4 10.6 %collective-permute-start.1 = (bf16[2,384,128]{2,1,0:T(8,128)(2,1)S(1)}, bf16[2,384,128]{2,1,0:T(8,128)(2,1)S(1)}, u32[]{:S(2)}, u32[]{:S(2)}) collective-permute-start(bf16[2,384,128]{2,1,0:T(8,128)(2,1)S(1)} %get-tuple-element.14), channel_id=1, source_target_pairs={{1,0},{2,1},{3,2},{4,3},{5,4},{6,5},{7,6},{8,7},{9,8},{10,9},{11,1... | collective-permute-start | bytes 589832 | tf_op jit(solution)/shard_map/ppermute | solution.py:18
  16.8 6.2 %copy-start.3 = (bf16[2,384,128]{2,1,0:T(8,128)(2,1)}, bf16[2,384,128]{2,1,0:T(8,128)(2,1)S(1)}, u32[]{:S(2)}) copy-start(bf16[2,384,128]{2,1,0:T(8,128)(2,1)S(1)} %collective-permute-done.left_ref) | copy-start | bytes 589828
  23.0 0.7 %copy-start.4 = (bf16[2,384,128]{2,1,0:T(8,128)(2,1)}, bf16[2,384,128]{2,1,0:T(8,128)(2,1)S(1)}, u32[]{:S(2)}) copy-start(bf16[2,384,128]{2,1,0:T(8,128)(2,1)S(1)} %collective-permute-done.1.right_ref) | copy-start | bytes 589828
  34.0 1.0 %copy-start.2 = (f32[4,128,128]{2,1,0:T(8,128)S(1)}, f32[4,128,128]{2,1,0:T(8,128)}, u32[]{:S(2)}) copy-start(f32[4,128,128]{2,1,0:T(8,128)} %param.7) | copy-start | bytes 786436

commit v5 on v4

--- a/solution.py
+++ b/solution.py
@@ -43,16 +43,9 @@
     return jnp.concatenate([packed[:, :HALF], pltpu.roll(packed, HALF, 1)[:, :HALF]], axis=0)
 
 
-def main_kernel(
-    rank_count, local_chans, sky_count, spec_ref, taps_ref, left_ref, xc_ref, right_ref, dirty_ref,
-    res_ref, part_ref, colf_ref, rowf_ref, cola_ref, rowa_ref,
-):
-    slot = xc_ref.shape[-1]
-    rows = xc_ref.shape[1]
-    pieces, basis, piece_rows, _ = part_ref.shape
+def band_kernel(rank_count, local_chans, slot, taps_ref, colf_ref, rowf_ref, cola_ref, rowa_ref):
+    rows = rowf_ref.shape[-1]
     first_chan = lax.axis_index("chan") * local_chans
-    sky_index = lax.axis_index("sky")
-    lane = lax.broadcasted_iota(jnp.int32, (rows, slot), 1)
     flip = (
         lax.broadcasted_iota(jnp.int32, (LANES // 2, LANES), 0)
         + lax.broadcasted_iota(jnp.int32, (LANES // 2, LANES), 1)
@@ -65,11 +58,24 @@
         for r in range(rank_count):
             u, v = taps[r : r + 1], taps[rank_count + r : rank_count + r + 1]
             u_rev, v_rev = rev[r : r + 1], rev[rank_count + r : rank_count + r + 1]
-            colf_ref[:, r * slot : (r + 1) * slot] = col_band(v_rev, slot).astype(jnp.bfloat16)
-            cola_ref[:, r * slot : (r + 1) * slot] = col_band(v, slot).astype(jnp.bfloat16)
-            rowf_ref[r] = row_band(u, rows).astype(jnp.bfloat16)
-            rowa_ref[r] = row_band(u_rev, rows).astype(jnp.bfloat16)
-        band = colf_ref[...]
+            colf_ref[c, :, r * slot : (r + 1) * slot] = col_band(v_rev, slot).astype(jnp.bfloat16)
+            cola_ref[c, :, r * slot : (r + 1) * slot] = col_band(v, slot).astype(jnp.bfloat16)
+            rowf_ref[c, r] = row_band(u, rows).astype(jnp.bfloat16)
+            rowa_ref[c, r] = row_band(u_rev, rows).astype(jnp.bfloat16)
+
+
+def main_kernel(
+    rank_count, local_chans, sky_count, spec_ref, colf_ref, rowf_ref, cola_ref, rowa_ref,
+    left_ref, xc_ref, right_ref, dirty_ref, res_ref, part_ref,
+):
+    slot = xc_ref.shape[-1]
+    rows = xc_ref.shape[1]
+    pieces, basis, piece_rows, _ = part_ref.shape
+    first_chan = lax.axis_index("chan") * local_chans
+    sky_index = lax.axis_index("sky")
+    lane = lax.broadcasted_iota(jnp.int32, (rows, slot), 1)
+    for c in range(local_chans):
+        band = colf_ref[c]
         xl, xc, xr = left_ref[c, :rows], xc_ref[c], right_ref[c, :rows]
         low = (
             jnp.dot(xl, band[:slot], preferred_element_type=jnp.float32)
@@ -79,8 +85,8 @@
             jnp.dot(xc, band[:slot], preferred_element_type=jnp.float32)
             + jnp.dot(xr, band[slot:], preferred_element_type=jnp.float32)
         ).astype(jnp.bfloat16)
-        pred_low = row_pass(rowf_ref, low, rank_count, slot)
-        pred_high = row_pass(rowf_ref, high, rank_count, slot)
+        pred_low = row_pass(rowf_ref.at[c], low, rank_count, slot)
+        pred_high = row_pass(rowf_ref.at[c], high, rank_count, slot)
         pred_own = pltpu.roll(jnp.where(lane < HALF, pred_high, pred_low), HALF, 1)
         res_own = (dirty_ref[c].astype(jnp.float32) - pred_own).astype(jnp.bfloat16)
         res_ref[c] = res_own
@@ -89,13 +95,13 @@
         halo_l = jnp.where(sky_index > 0, dl - pred_low[:, :HALF], 0.0)
         pred_right = pltpu.roll(pred_high, slot - HALF, 1)[:, :HALF]
         halo_r = jnp.where(sky_index < sky_count - 1, dr - pred_right, 0.0)
-        adj = cola_ref[...]
+        adj = cola_ref[c]
         col_pass = (
             jnp.dot(halo_l.astype(jnp.bfloat16), adj[:HALF], preferred_element_type=jnp.float32)
             + jnp.dot(res_own, adj[HALF : HALF + slot], preferred_element_type=jnp.float32)
             + jnp.dot(halo_r.astype(jnp.bfloat16), adj[HALF + slot :], preferred_element_type=jnp.float32)
         ).astype(jnp.bfloat16)
-        grad_chan = row_pass(rowa_ref, col_pass, rank_count, slot)
+        grad_chan = row_pass(rowa_ref.at[c], col_pass, rank_count, slot)
         for j in range(pieces):
             block = grad_chan[j * piece_rows : (j + 1) * piece_rows]
             for b in range(basis):
@@ -138,21 +144,25 @@
     taps = jnp.pad(taps, ((0, 0), (0, 0), (0, LANES - TAPS)))
     piece_rows = row_count // chan_count
     ext = slot_width + 2 * HALF
+    band_shapes = (
+        jax.ShapeDtypeStruct((local_chans, ext, rank_count * slot_width), jnp.bfloat16),
+        jax.ShapeDtypeStruct((local_chans, rank_count, row_count, row_count), jnp.bfloat16),
+    )
+    bands = pl.pallas_call(
+        functools.partial(band_kernel, rank_count, local_chans, slot_width),
+        out_shape=band_shapes * 2,
+        in_specs=[vmem_spec()],
+        out_specs=[vmem_spec()] * 4,
+    )(taps)
     residual, partial_value = pl.pallas_call(
         functools.partial(main_kernel, rank_count, local_chans, sky_count),
         out_shape=(
             jax.ShapeDtypeStruct(dirty.shape, jnp.bfloat16),
             jax.ShapeDtypeStruct((chan_count, basis, piece_rows, slot_width), jnp.float32),
         ),
-        in_specs=[smem_spec()] + [vmem_spec()] * 5,
+        in_specs=[smem_spec()] + [vmem_spec()] * 8,
         out_specs=[vmem_spec()] * 2,
-        scratch_shapes=[
-            pltpu.VMEM((ext, rank_count * slot_width), jnp.bfloat16),
-            pltpu.VMEM((rank_count, row_count, row_count), jnp.bfloat16),
-            pltpu.VMEM((ext, rank_count * slot_width), jnp.bfloat16),
-            pltpu.VMEM((rank_count, row_count, row_count), jnp.bfloat16),
-        ],
-    )(spectral, taps, left, image, right, dirty)
+    )(spectral, *bands, left, image, right, dirty)
 
     pieces = lax.all_to_all(partial_value, "chan", 0, 0, tiled=True)
     grad_share = pieces.sum(0)

time: 36.2 us -> 36.4 us (level)
  Pallas kernels: 5.13 us -> 8.67 us
  waiting for transfers between devices: 8.12 us -> 4.72 us
    ppermute x2, waiting for transfers between devices: 8.12 us -> 4.72 us  [from_behind(): lax.ppermute(value, axis, [(source, source + steps) for source in range(f...]
    pallas_call x0 -> x1, Pallas kernels: none -> 3.38 us  [body(): pl.pallas_call(functools.partial(band_kernel, rank_count, local_chans, sl...]
  transfers between devices with their start and end apart: 2 -> 2, of which waited for: 2 -> 1; matrix products, arithmetic and copies ran while one was open for 3% -> 3% of each run, Pallas kernels for 0% -> 9%
where the time goes in v5:
time: 36.4 us; the launch traced here: 35.9 us
  blocking collectives  9.05 us (25%)
  Pallas kernels  8.67 us (24%)
  starting transfers between devices  6.15 us (17%)
  waiting for transfers between devices  4.72 us (13%)
  local copies, waits for them, and re-layouts  4.34 us (12%)
  other arithmetic  1.84 us (5%)
  between operations  0.72 us (2%)
  matrix products  0.42 us (1%)
    ppermute x2, starting transfers between devices, from_behind(): lax.ppermute(value, axis, [(source, source + steps) for source in range(f...  6.15 us
    pallas_call x1, Pallas kernels, body(): pl.pallas_call(functools.partial(main_kernel, rank_count, local_chans, sk...  5.29 us
    all_to_all x1, blocking collectives, body(): pieces = lax.all_to_all(partial_value, 'chan', 0, 0, tiled=True)  5.21 us
    ppermute x2, waiting for transfers between devices, from_behind(): lax.ppermute(value, axis, [(source, source + steps) for source in range(f...  4.72 us
    all_to_all x1, blocking collectives, body(): image = lax.all_to_all(image_rows, 'chan', 0, 1, tiled=True)  3.84 us
    pallas_call x1, Pallas kernels, body(): pl.pallas_call(functools.partial(band_kernel, rank_count, local_chans, sl...  3.38 us
    unnamed x16, local copies, waits for them, and re-layouts  3.05 us
    mul x1, local copies, waits for them, and re-layouts, body(): image_rows = spectral[:, 0][:, None, None] * model[0][None]  0.96 us
  transfers between devices with their start and end apart: 2, of which 1 were waited for; matrix products, arithmetic and copies ran while one was open for 3% of the time, Pallas kernels for 9%

profile of v5, /device:TPU:0, one launch (start us, length us, event | category | flops | bytes accessed | tf_op | source)
XLA Modules:
  0.0 35.9 jit_solution(10033905991837864612)
XLA Ops:
  0.6 0.0 copy-start.7
  0.6 1.0 %slice_bitcast_fusion.3 = (f32[128,128]{1,0:T(8,128)S(1)}, f32[128,128]{1,0:T(8,128)S(1)}, f32[128,128]{1,0:T(8,128)S(1)}, f32[128,128]{1,0:T(8,128)S(1)}) fusion(f32[4,128,128]{2,1,0:T(8,128)} %param.7), kind=kLoop, calls=%fused_computation.11 | loop fusion | bytes 524288 | tf_op jit(solution)/shard_map/mul | solution.py:130
  1.6 0.0 copy-done.7
  1.6 0.2 slice_reduce_fusion.3
  1.8 0.2 add_convert_fusion
  2.0 3.8 %all_to_all.23 = bf16[4,128,128]{2,1,0:T(8,128)(2,1)S(1)} all-to-all(bf16[4,128,128]{2,1,0:T(8,128)(2,1)S(1)} %add_convert_fusion), channel_id=1, replica_groups=mesh['chan'=2,'sky'=16] {'chan'}, dimensions={0} | all-to-all | bytes 262144 | tf_op jit(solution)/shard_map/all_to_all | solution.py:134
  5.8 0.0 copy-start
  5.8 0.9 %copy-done = bf16[2,256,128]{2,1,0:T(8,128)(2,1)S(1)} copy-done((bf16[2,256,128]{2,1,0:T(8,128)(2,1)S(1)}, bf16[2,256,128]{2,1,0:T(8,128)(2,1)}, u32[]{:S(2)}) %copy-start) | copy-done | bytes 131096
  6.7 0.0 copy-start.1
  6.7 0.1 fusion.1
  6.9 0.5 %copy-done.1 = bf16[2,2,128,128]{3,2,1,0:T(8,128)(2,1)} copy-done((bf16[2,2,128,128]{3,2,1,0:T(8,128)(2,1)}, bf16[2,2,128,128]{3,2,1,0:T(8,128)(2,1)S(1)}, u32[]{:S(2)}) %copy-start.1) | copy-done | bytes 131096
  7.4 0.0 copy-start.5
  7.4 0.1 pad_maximum_fusion
  7.5 4.9 %collective-permute-start = (bf16[2,384,128]{2,1,0:T(8,128)(2,1)S(1)}, bf16[2,384,128]{2,1,0:T(8,128)(2,1)S(1)}, u32[]{:S(2)}, u32[]{:S(2)}) collective-permute-start(bf16[2,384,128]{2,1,0:T(8,128)(2,1)S(1)} %get-tuple-element.23), channel_id=1, source_target_pairs={{0,1},{1,2},{2,3},{3,4},{4,5},{5,6},{6,7},{7,8},{8,9},{9,10},{10,1... | collective-permute-start | bytes 589832 | tf_op jit(solution)/shard_map/ppermute | solution.py:18
  12.4 0.0 copy-start.6
  12.4 1.3 %collective-permute-start.1 = (bf16[2,384,128]{2,1,0:T(8,128)(2,1)S(1)}, bf16[2,384,128]{2,1,0:T(8,128)(2,1)S(1)}, u32[]{:S(2)}, u32[]{:S(2)}) collective-permute-start(bf16[2,384,128]{2,1,0:T(8,128)(2,1)S(1)} %get-tuple-element.22), channel_id=1, source_target_pairs={{1,0},{2,1},{3,2},{4,3},{5,4},{6,5},{7,6},{8,7},{9,8},{10,9},{11,1... | collective-permute-start | bytes 589832 | tf_op jit(solution)/shard_map/ppermute | solution.py:18
  13.7 0.0 copy-done.5
  13.7 0.2 fusion.2
  13.8 0.0 copy-done.6
  13.8 0.7 %select_maximum_fusion.taps_ref = f32[4,8,512]{2,1,0:T(8,128)} fusion(f32[4,4,129]{2,1,0:T(4,128)S(1)} %copy-done.6, f32[4,4,129]{2,1,0:T(4,128)S(1)} %copy-done.5), kind=kLoop, calls=%fused_computation.6 | loop fusion | flops 65536 | bytes 82048 | tf_op jit(solution)/shard_map/concatenate | solution.py:143
  14.5 3.4 %shard_map.68 = (bf16[2,256,512]{2,1,0:T(8,128)(2,1)}, bf16[2,4,256,256]{3,2,1,0:T(8,128)(2,1)}, bf16[2,256,512]{2,1,0:T(8,128)(2,1)}, bf16[2,4,256,256]{3,2,1,0:T(8,128)(2,1)}) custom-call(f32[4,8,512]{2,1,0:T(8,128)} %select_maximum_fusion.taps_ref), custom_call_target="tpu_custom_call" | custom-call | tf_op jit(solution)/shard_map/pallas_call | solution.py:151
  17.9 0.3 fusion
  18.2 0.1 multiply_reduce_fusion
  18.2 0.0 collective-permute-done.left_ref
  18.2 0.0 copy-start.3
  18.3 4.7 %collective-permute-done.1.right_ref = bf16[2,384,128]{2,1,0:T(8,128)(2,1)S(1)} collective-permute-done((bf16[2,384,128]{2,1,0:T(8,128)(2,1)S(1)}, bf16[2,384,128]{2,1,0:T(8,128)(2,1)S(1)}, u32[]{:S(2)}, u32[]{:S(2)}) %collective-permute-start.1) | collective-permute-done | bytes 196640 | tf_op jit(solution)/shard_map/ppermute | solution.py:18
  23.0 0.0 copy-done.3
  23.0 0.7 %copy-done.4 = bf16[2,384,128]{2,1,0:T(8,128)(2,1)} copy-done((bf16[2,384,128]{2,1,0:T(8,128)(2,1)}, bf16[2,384,128]{2,1,0:T(8,128)(2,1)S(1)}, u32[]{:S(2)}) %copy-start.4) | copy-done | bytes 196632
  23.7 5.3 %shard_map.69 = (bf16[2,256,128]{2,1,0:T(8,128)(2,1)}, f32[2,4,128,128]{3,2,1,0:T(8,128)}) custom-call(f32[4,4]{1,0:T(4,128)} %spec_ref.1, bf16[2,256,512]{2,1,0:T(8,128)(2,1)} %get-tuple-element.8.colf_ref, bf16[2,4,256,256]{3,2,1,0:T(8,128)(2,1)} %get-tuple-element.9.rowf_ref, bf16[2,256,512]{2,1,0:T(8,128)(2,1)} %get-tuple-element.10.cola_ref, ...), custom_call_target="tpu_custom_call" | custom-call | tf_op jit(solution)/shard_map/pallas_call | solution.py:157
  29.0 5.2 %all_to_all.24 = f32[2,4,128,128]{3,2,1,0:T(8,128)S(1)} all-to-all(f32[2,4,128,128]{3,2,1,0:T(8,128)} %get-tuple-element.13), channel_id=1, replica_groups=mesh['chan'=2,'sky'=16] {'chan'}, dimensions={0} | all-to-all | bytes 1048576 | tf_op jit(solution)/shard_map/all_to_all | solution.py:167
  34.2 0.9 %copy-done.2 = f32[4,128,128]{2,1,0:T(8,128)S(1)} copy-done((f32[4,128,128]{2,1,0:T(8,128)S(1)}, f32[4,128,128]{2,1,0:T(8,128)}, u32[]{:S(2)}) %copy-start.2) | copy-done | bytes 262168
  35.1 0.8 %divide_add_fusion = f32[4,128,128]{2,1,0:T(8,128)} fusion(f32[4,128,128]{2,1,0:T(8,128)S(1)} %copy-done.2, f32[4,128,128]{2,1,0:T(8,128)S(1)} %reduce_sum.27, f32[4]{0:T(128)S(1)} %multiply_reduce_fusion), kind=kLoop, calls=%fused_computation.2 | loop fusion | flops 131072 | bytes 786448 | tf_op jit(solution)/shard_map/add | solution.py:174
  (4 shorter events, 0.0 us)
Async XLA Ops:
  0.6 1.0 %copy-start.7 = (f32[4,4]{1,0:T(4,128)S(1)}, f32[4,4]{1,0:T(4,128)}, u32[]{:S(2)}) copy-start(f32[4,4]{1,0:T(4,128)} %spec_ref.1) | copy-start | bytes 196
  5.8 0.9 %copy-start = (bf16[2,256,128]{2,1,0:T(8,128)(2,1)S(1)}, bf16[2,256,128]{2,1,0:T(8,128)(2,1)}, u32[]{:S(2)}) copy-start(bf16[2,256,128]{2,1,0:T(8,128)(2,1)} %dirty_ref.1) | copy-start | bytes 393220
  6.7 0.7 %copy-start.1 = (bf16[2,2,128,128]{3,2,1,0:T(8,128)(2,1)}, bf16[2,2,128,128]{3,2,1,0:T(8,128)(2,1)S(1)}, u32[]{:S(2)}) copy-start(bf16[2,2,128,128]{3,2,1,0:T(8,128)(2,1)S(1)} %copy.7) | copy-start | bytes 393220
  7.4 6.3 %copy-start.5 = (f32[4,4,129]{2,1,0:T(4,128)S(1)}, f32[4,4,129]{2,1,0:T(4,128)}, u32[]{:S(2)}) copy-start(f32[4,4,129]{2,1,0:T(4,128)} %param.9) | copy-start | bytes 24772
  7.5 10.7 %collective-permute-start = (bf16[2,384,128]{2,1,0:T(8,128)(2,1)S(1)}, bf16[2,384,128]{2,1,0:T(8,128)(2,1)S(1)}, u32[]{:S(2)}, u32[]{:S(2)}) collective-permute-start(bf16[2,384,128]{2,1,0:T(8,128)(2,1)S(1)} %get-tuple-element.23), channel_id=1, source_target_pairs={{0,1},{1,2},{2,3},{3,4},{4,5},{5,6},{6,7},{7,8},{8,9},{9,10},{10,1... | collective-permute-start | bytes 589832 | tf_op jit(solution)/shard_map/ppermute | solution.py:18
  12.4 1.5 %copy-start.6 = (f32[4,4,129]{2,1,0:T(4,128)S(1)}, f32[4,4,129]{2,1,0:T(4,128)}, u32[]{:S(2)}) copy-start(f32[4,4,129]{2,1,0:T(4,128)} %param.10) | copy-start | bytes 24772
  12.4 10.6 %collective-permute-start.1 = (bf16[2,384,128]{2,1,0:T(8,128)(2,1)S(1)}, bf16[2,384,128]{2,1,0:T(8,128)(2,1)S(1)}, u32[]{:S(2)}, u32[]{:S(2)}) collective-permute-start(bf16[2,384,128]{2,1,0:T(8,128)(2,1)S(1)} %get-tuple-element.22), channel_id=1, source_target_pairs={{1,0},{2,1},{3,2},{4,3},{5,4},{6,5},{7,6},{8,7},{9,8},{10,9},{11,1... | collective-permute-start | bytes 589832 | tf_op jit(solution)/shard_map/ppermute | solution.py:18
  18.2 4.7 %copy-start.3 = (bf16[2,384,128]{2,1,0:T(8,128)(2,1)}, bf16[2,384,128]{2,1,0:T(8,128)(2,1)S(1)}, u32[]{:S(2)}) copy-start(bf16[2,384,128]{2,1,0:T(8,128)(2,1)S(1)} %collective-permute-done.left_ref) | copy-start | bytes 589828
  23.0 0.7 %copy-start.4 = (bf16[2,384,128]{2,1,0:T(8,128)(2,1)}, bf16[2,384,128]{2,1,0:T(8,128)(2,1)S(1)}, u32[]{:S(2)}) copy-start(bf16[2,384,128]{2,1,0:T(8,128)(2,1)S(1)} %collective-permute-done.1.right_ref) | copy-start | bytes 589828
  34.2 1.0 %copy-start.2 = (f32[4,128,128]{2,1,0:T(8,128)S(1)}, f32[4,128,128]{2,1,0:T(8,128)}, u32[]{:S(2)}) copy-start(f32[4,128,128]{2,1,0:T(8,128)} %param.7) | copy-start | bytes 786436

commit v6 on v5

--- a/solution.py
+++ b/solution.py
@@ -39,10 +39,6 @@
     return total
 
 
-def unpack_cols(packed):
-    return jnp.concatenate([packed[:, :HALF], pltpu.roll(packed, HALF, 1)[:, :HALF]], axis=0)
-
-
 def band_kernel(rank_count, local_chans, slot, taps_ref, colf_ref, rowf_ref, cola_ref, rowa_ref):
     rows = rowf_ref.shape[-1]
     first_chan = lax.axis_index("chan") * local_chans
@@ -75,33 +71,33 @@
     sky_index = lax.axis_index("sky")
     lane = lax.broadcasted_iota(jnp.int32, (rows, slot), 1)
     for c in range(local_chans):
-        band = colf_ref[c]
         xl, xc, xr = left_ref[c, :rows], xc_ref[c], right_ref[c, :rows]
-        low = (
-            jnp.dot(xl, band[:slot], preferred_element_type=jnp.float32)
-            + jnp.dot(xc, band[slot:], preferred_element_type=jnp.float32)
-        ).astype(jnp.bfloat16)
-        high = (
-            jnp.dot(xc, band[:slot], preferred_element_type=jnp.float32)
-            + jnp.dot(xr, band[slot:], preferred_element_type=jnp.float32)
-        ).astype(jnp.bfloat16)
-        pred_low = row_pass(rowf_ref.at[c], low, rank_count, slot)
-        pred_high = row_pass(rowf_ref.at[c], high, rank_count, slot)
+        stacked = jnp.concatenate(
+            [jnp.concatenate([xl, xc], axis=1), jnp.concatenate([xc, xr], axis=1)], axis=0
+        )
+        col_pass = jnp.dot(stacked, colf_ref[c], preferred_element_type=jnp.float32).astype(jnp.bfloat16)
+        pred = None
+        for r in range(rank_count):
+            both = jnp.concatenate(
+                [col_pass[:rows, r * slot : (r + 1) * slot], col_pass[rows:, r * slot : (r + 1) * slot]], axis=1
+            )
+            part = jnp.dot(rowf_ref[c, r], both, preferred_element_type=jnp.float32)
+            pred = part if pred is None else pred + part
+        pred_low, pred_high = pred[:, :slot], pred[:, slot:]
         pred_own = pltpu.roll(jnp.where(lane < HALF, pred_high, pred_low), HALF, 1)
         res_own = (dirty_ref[c].astype(jnp.float32) - pred_own).astype(jnp.bfloat16)
         res_ref[c] = res_own
-        dl = unpack_cols(left_ref[c, rows:]).astype(jnp.float32)
-        dr = unpack_cols(right_ref[c, rows:]).astype(jnp.float32)
-        halo_l = jnp.where(sky_index > 0, dl - pred_low[:, :HALF], 0.0)
-        pred_right = pltpu.roll(pred_high, slot - HALF, 1)[:, :HALF]
-        halo_r = jnp.where(sky_index < sky_count - 1, dr - pred_right, 0.0)
-        adj = cola_ref[c]
-        col_pass = (
-            jnp.dot(halo_l.astype(jnp.bfloat16), adj[:HALF], preferred_element_type=jnp.float32)
-            + jnp.dot(res_own, adj[HALF : HALF + slot], preferred_element_type=jnp.float32)
-            + jnp.dot(halo_r.astype(jnp.bfloat16), adj[HALF + slot :], preferred_element_type=jnp.float32)
-        ).astype(jnp.bfloat16)
-        grad_chan = row_pass(rowa_ref.at[c], col_pass, rank_count, slot)
+        packed_l, packed_r = left_ref[c, rows:], right_ref[c, rows:]
+        dl = jnp.concatenate([packed_l, pltpu.roll(packed_l, HALF, 1)], axis=0).astype(jnp.float32)
+        dr = jnp.concatenate([pltpu.roll(packed_r, HALF, 1), packed_r], axis=0).astype(jnp.float32)
+        halo_l = jnp.where(sky_index > 0, dl - pred_low, 0.0).astype(jnp.bfloat16)
+        halo_r = jnp.where(sky_index < sky_count - 1, dr - pred_high, 0.0).astype(jnp.bfloat16)
+        shifted = pltpu.roll(res_own, HALF, 1)
+        res_low = jnp.where(lane < HALF, halo_l, shifted)
+        res_high = jnp.where(lane < HALF, shifted, halo_r)
+        adj_in = jnp.concatenate([res_low, res_high], axis=1)
+        adj_pass = jnp.dot(adj_in, cola_ref[c], preferred_element_type=jnp.float32).astype(jnp.bfloat16)
+        grad_chan = row_pass(rowa_ref.at[c], adj_pass, rank_count, slot)
         for j in range(pieces):
             block = grad_chan[j * piece_rows : (j + 1) * piece_rows]
             for b in range(basis):

time: 36.4 us -> 36.3 us (level)
  no operation moved by 1% of the time
where the time goes in v6:
time: 36.3 us; the launch traced here: 35.8 us
  blocking collectives  9.05 us (25%)
  Pallas kernels  8.57 us (24%)
  starting transfers between devices  6.15 us (17%)
  waiting for transfers between devices  4.72 us (13%)
  local copies, waits for them, and re-layouts  4.34 us (12%)
  other arithmetic  1.84 us (5%)
  between operations  0.72 us (2%)
  matrix products  0.42 us (1%)
    ppermute x2, starting transfers between devices, from_behind(): lax.ppermute(value, axis, [(source, source + steps) for source in range(f...  6.15 us
    all_to_all x1, blocking collectives, body(): pieces = lax.all_to_all(partial_value, 'chan', 0, 0, tiled=True)  5.21 us
    pallas_call x1, Pallas kernels, body(): pl.pallas_call(functools.partial(main_kernel, rank_count, local_chans, sk...  5.18 us
    ppermute x2, waiting for transfers between devices, from_behind(): lax.ppermute(value, axis, [(source, source + steps) for source in range(f...  4.72 us
    all_to_all x1, blocking collectives, body(): image = lax.all_to_all(image_rows, 'chan', 0, 1, tiled=True)  3.84 us
    pallas_call x1, Pallas kernels, body(): pl.pallas_call(functools.partial(band_kernel, rank_count, local_chans, sl...  3.38 us
    unnamed x16, local copies, waits for them, and re-layouts  3.05 us
    mul x1, local copies, waits for them, and re-layouts, body(): image_rows = spectral[:, 0][:, None, None] * model[0][None]  0.96 us
  transfers between devices with their start and end apart: 2, of which 1 were waited for; matrix products, arithmetic and copies ran while one was open for 3% of the time, Pallas kernels for 9%

profile of v6, /device:TPU:0, one launch (start us, length us, event | category | flops | bytes accessed | tf_op | source)
XLA Modules:
  0.0 35.8 jit_solution(1326490470822927052)
XLA Ops:
  0.6 0.0 copy-start.7
  0.6 1.0 %slice_bitcast_fusion.3 = (f32[128,128]{1,0:T(8,128)S(1)}, f32[128,128]{1,0:T(8,128)S(1)}, f32[128,128]{1,0:T(8,128)S(1)}, f32[128,128]{1,0:T(8,128)S(1)}) fusion(f32[4,128,128]{2,1,0:T(8,128)} %param.7), kind=kLoop, calls=%fused_computation.11 | loop fusion | bytes 524288 | tf_op jit(solution)/shard_map/mul | solution.py:126
  1.6 0.0 copy-done.7
  1.6 0.2 slice_reduce_fusion.3
  1.8 0.2 add_convert_fusion
  2.0 3.8 %all_to_all.23 = bf16[4,128,128]{2,1,0:T(8,128)(2,1)S(1)} all-to-all(bf16[4,128,128]{2,1,0:T(8,128)(2,1)S(1)} %add_convert_fusion), channel_id=1, replica_groups=mesh['chan'=2,'sky'=16] {'chan'}, dimensions={0} | all-to-all | bytes 262144 | tf_op jit(solution)/shard_map/all_to_all | solution.py:130
  5.8 0.0 copy-start
  5.8 0.9 %copy-done = bf16[2,256,128]{2,1,0:T(8,128)(2,1)S(1)} copy-done((bf16[2,256,128]{2,1,0:T(8,128)(2,1)S(1)}, bf16[2,256,128]{2,1,0:T(8,128)(2,1)}, u32[]{:S(2)}) %copy-start) | copy-done | bytes 131096
  6.7 0.0 copy-start.1
  6.7 0.1 fusion.1
  6.9 0.5 %copy-done.1 = bf16[2,2,128,128]{3,2,1,0:T(8,128)(2,1)} copy-done((bf16[2,2,128,128]{3,2,1,0:T(8,128)(2,1)}, bf16[2,2,128,128]{3,2,1,0:T(8,128)(2,1)S(1)}, u32[]{:S(2)}) %copy-start.1) | copy-done | bytes 131096
  7.4 0.0 copy-start.5
  7.4 0.1 pad_maximum_fusion
  7.5 4.9 %collective-permute-start = (bf16[2,384,128]{2,1,0:T(8,128)(2,1)S(1)}, bf16[2,384,128]{2,1,0:T(8,128)(2,1)S(1)}, u32[]{:S(2)}, u32[]{:S(2)}) collective-permute-start(bf16[2,384,128]{2,1,0:T(8,128)(2,1)S(1)} %get-tuple-element.23), channel_id=1, source_target_pairs={{0,1},{1,2},{2,3},{3,4},{4,5},{5,6},{6,7},{7,8},{8,9},{9,10},{10,1... | collective-permute-start | bytes 589832 | tf_op jit(solution)/shard_map/ppermute | solution.py:18
  12.4 0.0 copy-start.6
  12.4 1.3 %collective-permute-start.1 = (bf16[2,384,128]{2,1,0:T(8,128)(2,1)S(1)}, bf16[2,384,128]{2,1,0:T(8,128)(2,1)S(1)}, u32[]{:S(2)}, u32[]{:S(2)}) collective-permute-start(bf16[2,384,128]{2,1,0:T(8,128)(2,1)S(1)} %get-tuple-element.22), channel_id=1, source_target_pairs={{1,0},{2,1},{3,2},{4,3},{5,4},{6,5},{7,6},{8,7},{9,8},{10,9},{11,1... | collective-permute-start | bytes 589832 | tf_op jit(solution)/shard_map/ppermute | solution.py:18
  13.7 0.0 copy-done.5
  13.7 0.2 fusion.2
  13.8 0.0 copy-done.6
  13.8 0.7 %select_maximum_fusion.taps_ref = f32[4,8,512]{2,1,0:T(8,128)} fusion(f32[4,4,129]{2,1,0:T(4,128)S(1)} %copy-done.6, f32[4,4,129]{2,1,0:T(4,128)S(1)} %copy-done.5), kind=kLoop, calls=%fused_computation.6 | loop fusion | flops 65536 | bytes 82048 | tf_op jit(solution)/shard_map/concatenate | solution.py:139
  14.5 3.4 %shard_map.68 = (bf16[2,256,512]{2,1,0:T(8,128)(2,1)}, bf16[2,4,256,256]{3,2,1,0:T(8,128)(2,1)}, bf16[2,256,512]{2,1,0:T(8,128)(2,1)}, bf16[2,4,256,256]{3,2,1,0:T(8,128)(2,1)}) custom-call(f32[4,8,512]{2,1,0:T(8,128)} %select_maximum_fusion.taps_ref), custom_call_target="tpu_custom_call" | custom-call | tf_op jit(solution)/shard_map/pallas_call | solution.py:147
  17.9 0.3 fusion
  18.2 0.1 multiply_reduce_fusion
  18.2 0.0 collective-permute-done.left_ref
  18.2 0.0 copy-start.3
  18.3 4.7 %collective-permute-done.1.right_ref = bf16[2,384,128]{2,1,0:T(8,128)(2,1)S(1)} collective-permute-done((bf16[2,384,128]{2,1,0:T(8,128)(2,1)S(1)}, bf16[2,384,128]{2,1,0:T(8,128)(2,1)S(1)}, u32[]{:S(2)}, u32[]{:S(2)}) %collective-permute-start.1) | collective-permute-done | bytes 196640 | tf_op jit(solution)/shard_map/ppermute | solution.py:18
  23.0 0.0 copy-done.3
  23.0 0.7 %copy-done.4 = bf16[2,384,128]{2,1,0:T(8,128)(2,1)} copy-done((bf16[2,384,128]{2,1,0:T(8,128)(2,1)}, bf16[2,384,128]{2,1,0:T(8,128)(2,1)S(1)}, u32[]{:S(2)}) %copy-start.4) | copy-done | bytes 196632
  23.7 5.2 %shard_map.69 = (bf16[2,256,128]{2,1,0:T(8,128)(2,1)}, f32[2,4,128,128]{3,2,1,0:T(8,128)}) custom-call(f32[4,4]{1,0:T(4,128)} %spec_ref.1, bf16[2,256,512]{2,1,0:T(8,128)(2,1)} %get-tuple-element.8.colf_ref, bf16[2,4,256,256]{3,2,1,0:T(8,128)(2,1)} %get-tuple-element.9.rowf_ref, bf16[2,256,512]{2,1,0:T(8,128)(2,1)} %get-tuple-element.10.cola_ref, ...), custom_call_target="tpu_custom_call" | custom-call | tf_op jit(solution)/shard_map/pallas_call | solution.py:153
  28.9 5.2 %all_to_all.24 = f32[2,4,128,128]{3,2,1,0:T(8,128)S(1)} all-to-all(f32[2,4,128,128]{3,2,1,0:T(8,128)} %get-tuple-element.13), channel_id=1, replica_groups=mesh['chan'=2,'sky'=16] {'chan'}, dimensions={0} | all-to-all | bytes 1048576 | tf_op jit(solution)/shard_map/all_to_all | solution.py:163
  34.1 0.9 %copy-done.2 = f32[4,128,128]{2,1,0:T(8,128)S(1)} copy-done((f32[4,128,128]{2,1,0:T(8,128)S(1)}, f32[4,128,128]{2,1,0:T(8,128)}, u32[]{:S(2)}) %copy-start.2) | copy-done | bytes 262168
  35.0 0.8 %divide_add_fusion = f32[4,128,128]{2,1,0:T(8,128)} fusion(f32[4,128,128]{2,1,0:T(8,128)S(1)} %copy-done.2, f32[4,128,128]{2,1,0:T(8,128)S(1)} %reduce_sum.27, f32[4]{0:T(128)S(1)} %multiply_reduce_fusion), kind=kLoop, calls=%fused_computation.2 | loop fusion | flops 131072 | bytes 786448 | tf_op jit(solution)/shard_map/add | solution.py:170
  (4 shorter events, 0.0 us)
Async XLA Ops:
  0.6 1.0 %copy-start.7 = (f32[4,4]{1,0:T(4,128)S(1)}, f32[4,4]{1,0:T(4,128)}, u32[]{:S(2)}) copy-start(f32[4,4]{1,0:T(4,128)} %spec_ref.1) | copy-start | bytes 196
  5.8 0.9 %copy-start = (bf16[2,256,128]{2,1,0:T(8,128)(2,1)S(1)}, bf16[2,256,128]{2,1,0:T(8,128)(2,1)}, u32[]{:S(2)}) copy-start(bf16[2,256,128]{2,1,0:T(8,128)(2,1)} %dirty_ref.1) | copy-start | bytes 393220
  6.7 0.7 %copy-start.1 = (bf16[2,2,128,128]{3,2,1,0:T(8,128)(2,1)}, bf16[2,2,128,128]{3,2,1,0:T(8,128)(2,1)S(1)}, u32[]{:S(2)}) copy-start(bf16[2,2,128,128]{3,2,1,0:T(8,128)(2,1)S(1)} %copy.7) | copy-start | bytes 393220
  7.4 6.3 %copy-start.5 = (f32[4,4,129]{2,1,0:T(4,128)S(1)}, f32[4,4,129]{2,1,0:T(4,128)}, u32[]{:S(2)}) copy-start(f32[4,4,129]{2,1,0:T(4,128)} %param.9) | copy-start | bytes 24772
  7.5 10.7 %collective-permute-start = (bf16[2,384,128]{2,1,0:T(8,128)(2,1)S(1)}, bf16[2,384,128]{2,1,0:T(8,128)(2,1)S(1)}, u32[]{:S(2)}, u32[]{:S(2)}) collective-permute-start(bf16[2,384,128]{2,1,0:T(8,128)(2,1)S(1)} %get-tuple-element.23), channel_id=1, source_target_pairs={{0,1},{1,2},{2,3},{3,4},{4,5},{5,6},{6,7},{7,8},{8,9},{9,10},{10,1... | collective-permute-start | bytes 589832 | tf_op jit(solution)/shard_map/ppermute | solution.py:18
  12.4 1.5 %copy-start.6 = (f32[4,4,129]{2,1,0:T(4,128)S(1)}, f32[4,4,129]{2,1,0:T(4,128)}, u32[]{:S(2)}) copy-start(f32[4,4,129]{2,1,0:T(4,128)} %param.10) | copy-start | bytes 24772
  12.4 10.6 %collective-permute-start.1 = (bf16[2,384,128]{2,1,0:T(8,128)(2,1)S(1)}, bf16[2,384,128]{2,1,0:T(8,128)(2,1)S(1)}, u32[]{:S(2)}, u32[]{:S(2)}) collective-permute-start(bf16[2,384,128]{2,1,0:T(8,128)(2,1)S(1)} %get-tuple-element.22), channel_id=1, source_target_pairs={{1,0},{2,1},{3,2},{4,3},{5,4},{6,5},{7,6},{8,7},{9,8},{10,9},{11,1... | collective-permute-start | bytes 589832 | tf_op jit(solution)/shard_map/ppermute | solution.py:18
  18.2 4.7 %copy-start.3 = (bf16[2,384,128]{2,1,0:T(8,128)(2,1)}, bf16[2,384,128]{2,1,0:T(8,128)(2,1)S(1)}, u32[]{:S(2)}) copy-start(bf16[2,384,128]{2,1,0:T(8,128)(2,1)S(1)} %collective-permute-done.left_ref) | copy-start | bytes 589828
  23.0 0.7 %copy-start.4 = (bf16[2,384,128]{2,1,0:T(8,128)(2,1)}, bf16[2,384,128]{2,1,0:T(8,128)(2,1)S(1)}, u32[]{:S(2)}) copy-start(bf16[2,384,128]{2,1,0:T(8,128)(2,1)S(1)} %collective-permute-done.1.right_ref) | copy-start | bytes 589828
  34.1 1.0 %copy-start.2 = (f32[4,128,128]{2,1,0:T(8,128)S(1)}, f32[4,128,128]{2,1,0:T(8,128)}, u32[]{:S(2)}) copy-start(f32[4,128,128]{2,1,0:T(8,128)} %param.7) | copy-start | bytes 786436

commit v7 on v6

--- a/solution.py
+++ b/solution.py
@@ -65,29 +65,30 @@
     left_ref, xc_ref, right_ref, dirty_ref, res_ref, part_ref,
 ):
     slot = xc_ref.shape[-1]
-    rows = xc_ref.shape[1]
+    rows = xc_ref.shape[0]
     pieces, basis, piece_rows, _ = part_ref.shape
     first_chan = lax.axis_index("chan") * local_chans
     sky_index = lax.axis_index("sky")
     lane = lax.broadcasted_iota(jnp.int32, (rows, slot), 1)
-    for c in range(local_chans):
-        xl, xc, xr = left_ref[c, :rows], xc_ref[c], right_ref[c, :rows]
+    step = pl.program_id(0)
+    if True:
+        xl, xc, xr = left_ref[:rows], xc_ref[...], right_ref[:rows]
         stacked = jnp.concatenate(
             [jnp.concatenate([xl, xc], axis=1), jnp.concatenate([xc, xr], axis=1)], axis=0
         )
-        col_pass = jnp.dot(stacked, colf_ref[c], preferred_element_type=jnp.float32).astype(jnp.bfloat16)
+        col_pass = jnp.dot(stacked, colf_ref[...], preferred_element_type=jnp.float32).astype(jnp.bfloat16)
         pred = None
         for r in range(rank_count):
             both = jnp.concatenate(
                 [col_pass[:rows, r * slot : (r + 1) * slot], col_pass[rows:, r * slot : (r + 1) * slot]], axis=1
             )
-            part = jnp.dot(rowf_ref[c, r], both, preferred_element_type=jnp.float32)
+            part = jnp.dot(rowf_ref[r], both, preferred_element_type=jnp.float32)
             pred = part if pred is None else pred + part
         pred_low, pred_high = pred[:, :slot], pred[:, slot:]
         pred_own = pltpu.roll(jnp.where(lane < HALF, pred_high, pred_low), HALF, 1)
-        res_own = (dirty_ref[c].astype(jnp.float32) - pred_own).astype(jnp.bfloat16)
-        res_ref[c] = res_own
-        packed_l, packed_r = left_ref[c, rows:], right_ref[c, rows:]
+        res_own = (dirty_ref[...].astype(jnp.float32) - pred_own).astype(jnp.bfloat16)
+        res_ref[...] = res_own
+        packed_l, packed_r = left_ref[rows:], right_ref[rows:]
         dl = jnp.concatenate([packed_l, pltpu.roll(packed_l, HALF, 1)], axis=0).astype(jnp.float32)
         dr = jnp.concatenate([pltpu.roll(packed_r, HALF, 1), packed_r], axis=0).astype(jnp.float32)
         halo_l = jnp.where(sky_index > 0, dl - pred_low, 0.0).astype(jnp.bfloat16)
@@ -96,20 +97,29 @@
         res_low = jnp.where(lane < HALF, halo_l, shifted)
         res_high = jnp.where(lane < HALF, shifted, halo_r)
         adj_in = jnp.concatenate([res_low, res_high], axis=1)
-        adj_pass = jnp.dot(adj_in, cola_ref[c], preferred_element_type=jnp.float32).astype(jnp.bfloat16)
-        grad_chan = row_pass(rowa_ref.at[c], adj_pass, rank_count, slot)
-        for j in range(pieces):
-            block = grad_chan[j * piece_rows : (j + 1) * piece_rows]
-            for b in range(basis):
-                term = spec_ref[first_chan + c, b] * block
-                if c == 0:
-                    part_ref[j, b] = term
-                else:
-                    part_ref[j, b] = part_ref[j, b] + term
+        adj_pass = jnp.dot(adj_in, cola_ref[...], preferred_element_type=jnp.float32).astype(jnp.bfloat16)
+        grad_chan = row_pass(rowa_ref, adj_pass, rank_count, slot)
+        @pl.when(step == 0)
+        def _():
+            for j in range(pieces):
+                block = grad_chan[j * piece_rows : (j + 1) * piece_rows]
+                for b in range(basis):
+                    part_ref[j, b] = spec_ref[first_chan, b] * block
+
+        @pl.when(step > 0)
+        def _():
+            for j in range(pieces):
+                block = grad_chan[j * piece_rows : (j + 1) * piece_rows]
+                for b in range(basis):
+                    part_ref[j, b] = part_ref[j, b] + spec_ref[first_chan + step, b] * block
 
 
 def vmem_spec():
     return pl.BlockSpec(memory_space=pltpu.VMEM)
+
+
+def per_chan(shape):
+    return pl.BlockSpec((None,) + tuple(shape[1:]), lambda c: (c,) + (0,) * (len(shape) - 1))
 
 
 def smem_spec():
@@ -156,8 +166,12 @@
             jax.ShapeDtypeStruct(dirty.shape, jnp.bfloat16),
             jax.ShapeDtypeStruct((chan_count, basis, piece_rows, slot_width), jnp.float32),
         ),
-        in_specs=[smem_spec()] + [vmem_spec()] * 8,
-        out_specs=[vmem_spec()] * 2,
+        grid=(local_chans,),
+        in_specs=[smem_spec()] + [per_chan(a.shape) for a in (*bands, left, image, right, dirty)],
+        out_specs=[
+            per_chan(dirty.shape),
+            pl.BlockSpec((chan_count, basis, piece_rows, slot_width), lambda c: (0, 0, 0, 0)),
+        ],
     )(spectral, *bands, left, image, right, dirty)
 
     pieces = lax.all_to_all(partial_value, "chan", 0, 0, tiled=True)

time: 36.3 us -> 36.1 us (level)
  transfers between devices with their start and end apart: 2 -> 2, of which waited for: 1 -> 1; matrix products, arithmetic and copies ran while one was open for 3% -> 3% of each run, Pallas kernels for 9% -> 10%
where the time goes in v7:
time: 36.1 us; the launch traced here: 35.6 us
  blocking collectives  9.07 us (25%)
  Pallas kernels  8.38 us (23%)
  starting transfers between devices  6.15 us (17%)
  waiting for transfers between devices  4.72 us (13%)
  local copies, waits for them, and re-layouts  4.34 us (12%)
  other arithmetic  1.84 us (5%)
  between operations  0.72 us (2%)
  matrix products  0.42 us (1%)
    ppermute x2, starting transfers between devices, from_behind(): lax.ppermute(value, axis, [(source, source + steps) for source in range(f...  6.15 us
    all_to_all x1, blocking collectives, body(): pieces = lax.all_to_all(partial_value, 'chan', 0, 0, tiled=True)  5.23 us
    pallas_call x1, Pallas kernels, body(): pl.pallas_call(functools.partial(main_kernel, rank_count, local_chans, sk...  4.99 us
    ppermute x2, waiting for transfers between devices, from_behind(): lax.ppermute(value, axis, [(source, source + steps) for source in range(f...  4.72 us
    all_to_all x1, blocking collectives, body(): image = lax.all_to_all(image_rows, 'chan', 0, 1, tiled=True)  3.84 us
    pallas_call x1, Pallas kernels, body(): pl.pallas_call(functools.partial(band_kernel, rank_count, local_chans, sl...  3.38 us
    unnamed x16, local copies, waits for them, and re-layouts  3.05 us
    mul x1, local copies, waits for them, and re-layouts, body(): image_rows = spectral[:, 0][:, None, None] * model[0][None]  0.96 us
  transfers between devices with their start and end apart: 2, of which 1 were waited for; matrix products, arithmetic and copies ran while one was open for 3% of the time, Pallas kernels for 10%

profile of v7, /device:TPU:0, one launch (start us, length us, event | category | flops | bytes accessed | tf_op | source)
XLA Modules:
  0.0 35.6 jit_solution(9863812943565019320)
XLA Ops:
  0.6 0.0 copy-start.7
  0.6 1.0 %slice_bitcast_fusion.3 = (f32[128,128]{1,0:T(8,128)S(1)}, f32[128,128]{1,0:T(8,128)S(1)}, f32[128,128]{1,0:T(8,128)S(1)}, f32[128,128]{1,0:T(8,128)S(1)}) fusion(f32[4,128,128]{2,1,0:T(8,128)} %param.7), kind=kLoop, calls=%fused_computation.11 | loop fusion | bytes 524288 | tf_op jit(solution)/shard_map/mul | solution.py:136
  1.6 0.0 copy-done.7
  1.6 0.2 slice_reduce_fusion.3
  1.8 0.2 add_convert_fusion
  2.0 3.8 %all_to_all.23 = bf16[4,128,128]{2,1,0:T(8,128)(2,1)S(1)} all-to-all(bf16[4,128,128]{2,1,0:T(8,128)(2,1)S(1)} %add_convert_fusion), channel_id=1, replica_groups=mesh['chan'=2,'sky'=16] {'chan'}, dimensions={0} | all-to-all | bytes 262144 | tf_op jit(solution)/shard_map/all_to_all | solution.py:140
  5.8 0.9 %copy-done = bf16[2,256,128]{2,1,0:T(8,128)(2,1)S(1)} copy-done((bf16[2,256,128]{2,1,0:T(8,128)(2,1)S(1)}, bf16[2,256,128]{2,1,0:T(8,128)(2,1)}, u32[]{:S(2)}) %copy-start) | copy-done | bytes 131096
  6.7 0.0 copy-start.1
  6.7 0.1 fusion.1
  6.9 0.5 %copy-done.1 = bf16[2,2,128,128]{3,2,1,0:T(8,128)(2,1)} copy-done((bf16[2,2,128,128]{3,2,1,0:T(8,128)(2,1)}, bf16[2,2,128,128]{3,2,1,0:T(8,128)(2,1)S(1)}, u32[]{:S(2)}) %copy-start.1) | copy-done | bytes 131096
  7.4 0.0 copy-start.5
  7.4 0.1 pad_maximum_fusion
  7.5 4.9 %collective-permute-start = (bf16[2,384,128]{2,1,0:T(8,128)(2,1)S(1)}, bf16[2,384,128]{2,1,0:T(8,128)(2,1)S(1)}, u32[]{:S(2)}, u32[]{:S(2)}) collective-permute-start(bf16[2,384,128]{2,1,0:T(8,128)(2,1)S(1)} %get-tuple-element.23), channel_id=1, source_target_pairs={{0,1},{1,2},{2,3},{3,4},{4,5},{5,6},{6,7},{7,8},{8,9},{9,10},{10,1... | collective-permute-start | bytes 589832 | tf_op jit(solution)/shard_map/ppermute | solution.py:18
  12.4 0.0 copy-start.6
  12.4 1.3 %collective-permute-start.1 = (bf16[2,384,128]{2,1,0:T(8,128)(2,1)S(1)}, bf16[2,384,128]{2,1,0:T(8,128)(2,1)S(1)}, u32[]{:S(2)}, u32[]{:S(2)}) collective-permute-start(bf16[2,384,128]{2,1,0:T(8,128)(2,1)S(1)} %get-tuple-element.22), channel_id=1, source_target_pairs={{1,0},{2,1},{3,2},{4,3},{5,4},{6,5},{7,6},{8,7},{9,8},{10,9},{11,1... | collective-permute-start | bytes 589832 | tf_op jit(solution)/shard_map/ppermute | solution.py:18
  13.7 0.0 copy-done.5
  13.7 0.2 fusion.2
  13.8 0.0 copy-done.6
  13.8 0.7 %select_maximum_fusion.taps_ref = f32[4,8,512]{2,1,0:T(8,128)} fusion(f32[4,4,129]{2,1,0:T(4,128)S(1)} %copy-done.6, f32[4,4,129]{2,1,0:T(4,128)S(1)} %copy-done.5), kind=kLoop, calls=%fused_computation.6 | loop fusion | flops 65536 | bytes 82048 | tf_op jit(solution)/shard_map/concatenate | solution.py:149
  14.5 3.4 %shard_map.68 = (bf16[2,256,512]{2,1,0:T(8,128)(2,1)}, bf16[2,4,256,256]{3,2,1,0:T(8,128)(2,1)}, bf16[2,256,512]{2,1,0:T(8,128)(2,1)}, bf16[2,4,256,256]{3,2,1,0:T(8,128)(2,1)}) custom-call(f32[4,8,512]{2,1,0:T(8,128)} %select_maximum_fusion.taps_ref), custom_call_target="tpu_custom_call" | custom-call | tf_op jit(solution)/shard_map/pallas_call | solution.py:157
  17.9 0.3 fusion
  18.2 0.1 multiply_reduce_fusion
  18.2 0.0 collective-permute-done.left_ref
  18.2 0.0 copy-start.3
  18.3 4.7 %collective-permute-done.1.right_ref = bf16[2,384,128]{2,1,0:T(8,128)(2,1)S(1)} collective-permute-done((bf16[2,384,128]{2,1,0:T(8,128)(2,1)S(1)}, bf16[2,384,128]{2,1,0:T(8,128)(2,1)S(1)}, u32[]{:S(2)}, u32[]{:S(2)}) %collective-permute-start.1) | collective-permute-done | bytes 196640 | tf_op jit(solution)/shard_map/ppermute | solution.py:18
  23.0 0.0 copy-start.4
  23.0 0.0 copy-done.3
  23.0 0.7 %copy-done.4 = bf16[2,384,128]{2,1,0:T(8,128)(2,1)} copy-done((bf16[2,384,128]{2,1,0:T(8,128)(2,1)}, bf16[2,384,128]{2,1,0:T(8,128)(2,1)S(1)}, u32[]{:S(2)}) %copy-start.4) | copy-done | bytes 196632
  23.7 5.0 %shard_map.69 = (bf16[2,256,128]{2,1,0:T(8,128)(2,1)}, f32[2,4,128,128]{3,2,1,0:T(8,128)}) custom-call(f32[4,4]{1,0:T(4,128)} %spec_ref.1, bf16[2,256,512]{2,1,0:T(8,128)(2,1)} %get-tuple-element.8.colf_ref, bf16[2,4,256,256]{3,2,1,0:T(8,128)(2,1)} %get-tuple-element.9.rowf_ref, bf16[2,256,512]{2,1,0:T(8,128)(2,1)} %get-tuple-element.10.cola_ref, ...), custom_call_target="tpu_custom_call" | custom-call | tf_op jit(solution)/shard_map/pallas_call | solution.py:163
  28.7 5.2 %all_to_all.24 = f32[2,4,128,128]{3,2,1,0:T(8,128)S(1)} all-to-all(f32[2,4,128,128]{3,2,1,0:T(8,128)} %get-tuple-element.13), channel_id=1, replica_groups=mesh['chan'=2,'sky'=16] {'chan'}, dimensions={0} | all-to-all | bytes 1048576 | tf_op jit(solution)/shard_map/all_to_all | solution.py:177
  33.9 0.9 %copy-done.2 = f32[4,128,128]{2,1,0:T(8,128)S(1)} copy-done((f32[4,128,128]{2,1,0:T(8,128)S(1)}, f32[4,128,128]{2,1,0:T(8,128)}, u32[]{:S(2)}) %copy-start.2) | copy-done | bytes 262168
  34.8 0.8 %divide_add_fusion = f32[4,128,128]{2,1,0:T(8,128)} fusion(f32[4,128,128]{2,1,0:T(8,128)S(1)} %copy-done.2, f32[4,128,128]{2,1,0:T(8,128)S(1)} %reduce_sum.27, f32[4]{0:T(128)S(1)} %multiply_reduce_fusion), kind=kLoop, calls=%fused_computation.2 | loop fusion | flops 131072 | bytes 786448 | tf_op jit(solution)/shard_map/add | solution.py:184
  (4 shorter events, 0.0 us)
Async XLA Ops:
  0.6 1.0 %copy-start.7 = (f32[4,4]{1,0:T(4,128)S(1)}, f32[4,4]{1,0:T(4,128)}, u32[]{:S(2)}) copy-start(f32[4,4]{1,0:T(4,128)} %spec_ref.1) | copy-start | bytes 196
  5.8 0.9 %copy-start = (bf16[2,256,128]{2,1,0:T(8,128)(2,1)S(1)}, bf16[2,256,128]{2,1,0:T(8,128)(2,1)}, u32[]{:S(2)}) copy-start(bf16[2,256,128]{2,1,0:T(8,128)(2,1)} %dirty_ref.1) | copy-start | bytes 393220
  6.7 0.7 %copy-start.1 = (bf16[2,2,128,128]{3,2,1,0:T(8,128)(2,1)}, bf16[2,2,128,128]{3,2,1,0:T(8,128)(2,1)S(1)}, u32[]{:S(2)}) copy-start(bf16[2,2,128,128]{3,2,1,0:T(8,128)(2,1)S(1)} %copy.7) | copy-start | bytes 393220
  7.4 6.3 %copy-start.5 = (f32[4,4,129]{2,1,0:T(4,128)S(1)}, f32[4,4,129]{2,1,0:T(4,128)}, u32[]{:S(2)}) copy-start(f32[4,4,129]{2,1,0:T(4,128)} %param.9) | copy-start | bytes 24772
  7.5 10.7 %collective-permute-start = (bf16[2,384,128]{2,1,0:T(8,128)(2,1)S(1)}, bf16[2,384,128]{2,1,0:T(8,128)(2,1)S(1)}, u32[]{:S(2)}, u32[]{:S(2)}) collective-permute-start(bf16[2,384,128]{2,1,0:T(8,128)(2,1)S(1)} %get-tuple-element.23), channel_id=1, source_target_pairs={{0,1},{1,2},{2,3},{3,4},{4,5},{5,6},{6,7},{7,8},{8,9},{9,10},{10,1... | collective-permute-start | bytes 589832 | tf_op jit(solution)/shard_map/ppermute | solution.py:18
  12.4 1.5 %copy-start.6 = (f32[4,4,129]{2,1,0:T(4,128)S(1)}, f32[4,4,129]{2,1,0:T(4,128)}, u32[]{:S(2)}) copy-start(f32[4,4,129]{2,1,0:T(4,128)} %param.10) | copy-start | bytes 24772
  12.4 10.6 %collective-permute-start.1 = (bf16[2,384,128]{2,1,0:T(8,128)(2,1)S(1)}, bf16[2,384,128]{2,1,0:T(8,128)(2,1)S(1)}, u32[]{:S(2)}, u32[]{:S(2)}) collective-permute-start(bf16[2,384,128]{2,1,0:T(8,128)(2,1)S(1)} %get-tuple-element.22), channel_id=1, source_target_pairs={{1,0},{2,1},{3,2},{4,3},{5,4},{6,5},{7,6},{8,7},{9,8},{10,9},{11,1... | collective-permute-start | bytes 589832 | tf_op jit(solution)/shard_map/ppermute | solution.py:18
  18.2 4.7 %copy-start.3 = (bf16[2,384,128]{2,1,0:T(8,128)(2,1)}, bf16[2,384,128]{2,1,0:T(8,128)(2,1)S(1)}, u32[]{:S(2)}) copy-start(bf16[2,384,128]{2,1,0:T(8,128)(2,1)S(1)} %collective-permute-done.left_ref) | copy-start | bytes 589828
  23.0 0.7 %copy-start.4 = (bf16[2,384,128]{2,1,0:T(8,128)(2,1)}, bf16[2,384,128]{2,1,0:T(8,128)(2,1)S(1)}, u32[]{:S(2)}) copy-start(bf16[2,384,128]{2,1,0:T(8,128)(2,1)S(1)} %collective-permute-done.1.right_ref) | copy-start | bytes 589828
  33.9 1.0 %copy-start.2 = (f32[4,128,128]{2,1,0:T(8,128)S(1)}, f32[4,128,128]{2,1,0:T(8,128)}, u32[]{:S(2)}) copy-start(f32[4,128,128]{2,1,0:T(8,128)} %param.7) | copy-start | bytes 786436

commit v8 on v7

--- a/solution.py
+++ b/solution.py
@@ -118,6 +118,14 @@
     return pl.BlockSpec(memory_space=pltpu.VMEM)
 
 
+def update_kernel(curv_ref, pieces_ref, model_ref, out_ref):
+    for b in range(out_ref.shape[0]):
+        grad = pieces_ref[0, b]
+        for j in range(1, pieces_ref.shape[0]):
+            grad = grad + pieces_ref[j, b]
+        out_ref[b] = model_ref[b] + grad / curv_ref[b]
+
+
 def per_chan(shape):
     return pl.BlockSpec((None,) + tuple(shape[1:]), lambda c: (c,) + (0,) * (len(shape) - 1))
 
@@ -133,11 +141,12 @@
     chan_count = lax.axis_size("chan")
     sky_count = lax.axis_size("sky")
 
-    image_rows = spectral[:, 0][:, None, None] * model[0][None]
+    model_full = lax.all_gather(model, "chan", axis=1, tiled=True)
+    spec_local = lax.dynamic_slice_in_dim(spectral, lax.axis_index("chan") * local_chans, local_chans, 0)
+    image = spec_local[:, 0][:, None, None] * model_full[0][None]
     for basis_idx in range(1, basis):
-        image_rows = image_rows + spectral[:, basis_idx][:, None, None] * model[basis_idx][None]
-    image_rows = image_rows.astype(jnp.bfloat16)
-    image = lax.all_to_all(image_rows, "chan", 0, 1, tiled=True)
+        image = image + spec_local[:, basis_idx][:, None, None] * model_full[basis_idx][None]
+    image = image.astype(jnp.bfloat16)
     def with_dirty(cols):
         return jnp.concatenate([image, jnp.concatenate([cols[:, : row_count // 2], cols[:, row_count // 2 :]], axis=2)], axis=1)
 
@@ -175,13 +184,17 @@
     )(spectral, *bands, left, image, right, dirty)
 
     pieces = lax.all_to_all(partial_value, "chan", 0, 0, tiled=True)
-    grad_share = pieces.sum(0)
 
     gram_rows = jnp.einsum("crt,cst->crs", psf_rows, psf_rows, precision=lax.Precision.HIGHEST)
     gram_cols = jnp.einsum("crt,cst->crs", psf_cols, psf_cols, precision=lax.Precision.HIGHEST)
     energy = jnp.sum(gram_rows * gram_cols, axis=(1, 2))
     curvature = jnp.sum(spectral * spectral * energy[:, None], axis=0)
-    model_new = model + grad_share / curvature[:, None, None]
+    model_new = pl.pallas_call(
+        update_kernel,
+        out_shape=jax.ShapeDtypeStruct(model.shape, model.dtype),
+        in_specs=[smem_spec(), vmem_spec(), vmem_spec()],
+        out_specs=vmem_spec(),
+    )(curvature, pieces, model)
     return (residual, model_new)
 
 

time: 36.1 us -> 35.2 us (0.975)
  Pallas kernels: 8.38 us -> 10.2 us
  local copies, waits for them, and re-layouts: 4.34 us -> 3.12 us
  blocking collectives: 9.07 us -> 8.54 us
  waiting for transfers between devices: 4.72 us -> 4.2 us
    all_to_all x1 -> x0, blocking collectives: 3.84 us -> none  [body(): image = lax.all_to_all(image_rows, 'chan', 0, 1, tiled=True)]
    all_gather x0 -> x1, blocking collectives: none -> 2.47 us  [body(): model_full = lax.all_gather(model, 'chan', axis=1, tiled=True)]
    pallas_call x0 -> x1, Pallas kernels: none -> 1.86 us  [body(): pl.pallas_call(update_kernel, out_shape=jax.ShapeDtypeStruct(model.shape,...]
    mul x1, local copies, waits for them, and re-layouts: 0.96 us -> 0.03 us  [body(): image = spec_local[:, 0][:, None, None] * model_full[0][None]]
    all_to_all x1, blocking collectives: 5.23 us -> 6.07 us  [body(): pieces = lax.all_to_all(partial_value, 'chan', 0, 0, tiled=True)]
    add x1 -> x0, other arithmetic: 0.8 us -> none  [body(): model_new = model + grad_share / curvature[:, None, None]]
    ppermute x2, waiting for transfers between devices: 4.72 us -> 4.2 us  [from_behind(): lax.ppermute(value, axis, [(source, source + steps) for source in range(f...]
    reduce_sum x1, other arithmetic: 0.09 us -> 0.6 us  [body(): curvature = jnp.sum(spectral * spectral * energy[:, None], axis=0)]
  transfers between devices with their start and end apart: 2 -> 2, of which waited for: 1 -> 1; matrix products, arithmetic and copies ran while one was open for 3% -> 5% of each run, Pallas kernels for 10% -> 10%
where the time goes in v8:
time: 35.2 us; the launch traced here: 34.8 us
  Pallas kernels  10.2 us (29%)
  blocking collectives  8.54 us (24%)
  starting transfers between devices  6.06 us (17%)
  waiting for transfers between devices  4.2 us (12%)
  local copies, waits for them, and re-layouts  3.12 us (9%)
  other arithmetic  1.51 us (4%)
  between operations  0.72 us (2%)
  matrix products  0.42 us (1%)
    all_to_all x1, blocking collectives, body(): pieces = lax.all_to_all(partial_value, 'chan', 0, 0, tiled=True)  6.07 us
    ppermute x2, starting transfers between devices, from_behind(): lax.ppermute(value, axis, [(source, source + steps) for source in range(f...  6.06 us
    pallas_call x1, Pallas kernels, body(): pl.pallas_call(functools.partial(main_kernel, rank_count, local_chans, sk...  4.99 us
    ppermute x2, waiting for transfers between devices, from_behind(): lax.ppermute(value, axis, [(source, source + steps) for source in range(f...  4.2 us
    pallas_call x1, Pallas kernels, body(): pl.pallas_call(functools.partial(band_kernel, rank_count, local_chans, sl...  3.38 us
    unnamed x14, local copies, waits for them, and re-layouts  2.76 us
    all_gather x1, blocking collectives, body(): model_full = lax.all_gather(model, 'chan', axis=1, tiled=True)  2.47 us
    pallas_call x1, Pallas kernels, body(): pl.pallas_call(update_kernel, out_shape=jax.ShapeDtypeStruct(model.shape,...  1.86 us
  transfers between devices with their start and end apart: 2, of which 1 were waited for; matrix products, arithmetic and copies ran while one was open for 5% of the time, Pallas kernels for 10%

profile of v8, /device:TPU:0, one launch (start us, length us, event | category | flops | bytes accessed | tf_op | source)
XLA Modules:
  0.0 34.8 jit_solution(6044172784586416428)
XLA Ops:
  0.6 0.0 copy-start.6
  0.6 0.7 %copy-done.6 = f32[4,4]{1,0:T(4,128)S(1)} copy-done((f32[4,4]{1,0:T(4,128)S(1)}, f32[4,4]{1,0:T(4,128)}, u32[]{:S(2)}) %copy-start.6) | copy-done | bytes 88
  1.3 0.2 slice_reduce_fusion.3
  1.5 2.5 %all_gather.3 = f32[4,256,128]{2,1,0:T(8,128)S(1)} all-gather(f32[4,128,128]{2,1,0:T(8,128)} %model_ref.1), channel_id=1, replica_groups=mesh['chan'=2,'sky'=16] {'chan'}, dimensions={1}, use_global_device_ids=true | all-gather | bytes 786432 | tf_op jit(solution)/shard_map/all_gather | solution.py:144
  4.0 0.0 copy-start
  4.1 0.9 %copy-done = bf16[2,256,128]{2,1,0:T(8,128)(2,1)S(1)} copy-done((bf16[2,256,128]{2,1,0:T(8,128)(2,1)S(1)}, bf16[2,256,128]{2,1,0:T(8,128)(2,1)}, u32[]{:S(2)}) %copy-start) | copy-done | bytes 131096
  4.9 0.1 fusion.1
  5.0 0.1 add_convert_fusion.xc_ref
  5.2 0.0 copy-start.1
  5.2 0.0 copy-start.4
  5.2 0.1 pad_maximum_fusion
  5.3 0.5 %copy-done.1 = bf16[2,256,128]{2,1,0:T(8,128)(2,1)} copy-done((bf16[2,256,128]{2,1,0:T(8,128)(2,1)}, bf16[2,256,128]{2,1,0:T(8,128)(2,1)S(1)}, u32[]{:S(2)}) %copy-start.1) | copy-done | bytes 131096
  5.8 4.8 %collective-permute-start = (bf16[2,384,128]{2,1,0:T(8,128)(2,1)S(1)}, bf16[2,384,128]{2,1,0:T(8,128)(2,1)S(1)}, u32[]{:S(2)}, u32[]{:S(2)}) collective-permute-start(bf16[2,384,128]{2,1,0:T(8,128)(2,1)S(1)} %get-tuple-element.23), channel_id=1, source_target_pairs={{0,1},{1,2},{2,3},{3,4},{4,5},{5,6},{6,7},{7,8},{8,9},{9,10},{10,1... | collective-permute-start | bytes 589832 | tf_op jit(solution)/shard_map/ppermute | solution.py:18
  10.6 0.0 copy-start.5
  10.6 1.3 %collective-permute-start.1 = (bf16[2,384,128]{2,1,0:T(8,128)(2,1)S(1)}, bf16[2,384,128]{2,1,0:T(8,128)(2,1)S(1)}, u32[]{:S(2)}, u32[]{:S(2)}) collective-permute-start(bf16[2,384,128]{2,1,0:T(8,128)(2,1)S(1)} %get-tuple-element.22), channel_id=1, source_target_pairs={{1,0},{2,1},{3,2},{4,3},{5,4},{6,5},{7,6},{8,7},{9,8},{10,9},{11,1... | collective-permute-start | bytes 589832 | tf_op jit(solution)/shard_map/ppermute | solution.py:18
  11.9 0.0 copy-done.4
  11.9 0.2 fusion.2
  12.1 0.0 copy-done.5
  12.1 0.7 %select_maximum_fusion.taps_ref = f32[4,8,512]{2,1,0:T(8,128)} fusion(f32[4,4,129]{2,1,0:T(4,128)S(1)} %copy-done.5, f32[4,4,129]{2,1,0:T(4,128)S(1)} %copy-done.4), kind=kLoop, calls=%fused_computation.9 | loop fusion | flops 65536 | bytes 82048 | tf_op jit(solution)/shard_map/concatenate | solution.py:158
  12.7 3.4 %shard_map.68 = (bf16[2,256,512]{2,1,0:T(8,128)(2,1)}, bf16[2,4,256,256]{3,2,1,0:T(8,128)(2,1)}, bf16[2,256,512]{2,1,0:T(8,128)(2,1)}, bf16[2,4,256,256]{3,2,1,0:T(8,128)(2,1)}) custom-call(f32[4,8,512]{2,1,0:T(8,128)} %select_maximum_fusion.taps_ref), custom_call_target="tpu_custom_call" | custom-call | tf_op jit(solution)/shard_map/pallas_call | solution.py:166
  16.1 0.3 fusion
  16.4 0.6 %multiply_reduce_fusion.curv_ref = f32[4]{0:T(128)} fusion(f32[4,4]{1,0:T(4,128)S(1)} %copy-done.6, f32[4]{0:T(128)S(1)} %fusion), kind=kLoop, calls=%fused_computation.11 | loop fusion | flops 44 | bytes 96 | tf_op jit(solution)/shard_map/reduce_sum | solution.py:191
  17.0 0.0 collective-permute-done.left_ref
  17.0 0.0 copy-start.2
  17.0 4.2 %collective-permute-done.1.right_ref = bf16[2,384,128]{2,1,0:T(8,128)(2,1)S(1)} collective-permute-done((bf16[2,384,128]{2,1,0:T(8,128)(2,1)S(1)}, bf16[2,384,128]{2,1,0:T(8,128)(2,1)S(1)}, u32[]{:S(2)}, u32[]{:S(2)}) %collective-permute-start.1) | collective-permute-done | bytes 196640 | tf_op jit(solution)/shard_map/ppermute | solution.py:18
  21.2 0.0 copy-start.3
  21.2 0.0 copy-done.2
  21.2 0.7 %copy-done.3 = bf16[2,384,128]{2,1,0:T(8,128)(2,1)} copy-done((bf16[2,384,128]{2,1,0:T(8,128)(2,1)}, bf16[2,384,128]{2,1,0:T(8,128)(2,1)S(1)}, u32[]{:S(2)}) %copy-start.3) | copy-done | bytes 196632
  21.9 5.0 %shard_map.69 = (bf16[2,256,128]{2,1,0:T(8,128)(2,1)}, f32[2,4,128,128]{3,2,1,0:T(8,128)}) custom-call(f32[4,4]{1,0:T(4,128)} %spec_ref.1, bf16[2,256,512]{2,1,0:T(8,128)(2,1)} %get-tuple-element.8.colf_ref, bf16[2,4,256,256]{3,2,1,0:T(8,128)(2,1)} %get-tuple-element.9.rowf_ref, bf16[2,256,512]{2,1,0:T(8,128)(2,1)} %get-tuple-element.10.cola_ref, ...), custom_call_target="tpu_custom_call" | custom-call | tf_op jit(solution)/shard_map/pallas_call | solution.py:172
  26.9 6.1 %all_to_all.5.pieces_ref = f32[2,4,128,128]{3,2,1,0:T(8,128)} all-to-all(f32[2,4,128,128]{3,2,1,0:T(8,128)} %get-tuple-element.13), channel_id=1, replica_groups=mesh['chan'=2,'sky'=16] {'chan'}, dimensions={0} | all-to-all | bytes 1048576 | tf_op jit(solution)/shard_map/all_to_all | solution.py:186
  32.9 1.9 %shard_map.70 = f32[4,128,128]{2,1,0:T(8,128)} custom-call(f32[4]{0:T(128)} %multiply_reduce_fusion.curv_ref, f32[2,4,128,128]{3,2,1,0:T(8,128)} %all_to_all.5.pieces_ref, f32[4,128,128]{2,1,0:T(8,128)} %model_ref.1), custom_call_target="tpu_custom_call" | custom-call | tf_op jit(solution)/shard_map/pallas_call | solution.py:192
  (2 shorter events, 0.0 us)
Async XLA Ops:
  0.6 0.7 %copy-start.6 = (f32[4,4]{1,0:T(4,128)S(1)}, f32[4,4]{1,0:T(4,128)}, u32[]{:S(2)}) copy-start(f32[4,4]{1,0:T(4,128)} %spec_ref.1) | copy-start | bytes 196
  4.0 0.9 %copy-start = (bf16[2,256,128]{2,1,0:T(8,128)(2,1)S(1)}, bf16[2,256,128]{2,1,0:T(8,128)(2,1)}, u32[]{:S(2)}) copy-start(bf16[2,256,128]{2,1,0:T(8,128)(2,1)} %dirty_ref.1) | copy-start | bytes 393220
  5.2 0.7 %copy-start.1 = (bf16[2,256,128]{2,1,0:T(8,128)(2,1)}, bf16[2,256,128]{2,1,0:T(8,128)(2,1)S(1)}, u32[]{:S(2)}) copy-start(bf16[2,256,128]{2,1,0:T(8,128)(2,1)S(1)} %add_convert_fusion.xc_ref) | copy-start | bytes 393220
  5.2 6.7 %copy-start.4 = (f32[4,4,129]{2,1,0:T(4,128)S(1)}, f32[4,4,129]{2,1,0:T(4,128)}, u32[]{:S(2)}) copy-start(f32[4,4,129]{2,1,0:T(4,128)} %param.9) | copy-start | bytes 24772
  5.8 11.2 %collective-permute-start = (bf16[2,384,128]{2,1,0:T(8,128)(2,1)S(1)}, bf16[2,384,128]{2,1,0:T(8,128)(2,1)S(1)}, u32[]{:S(2)}, u32[]{:S(2)}) collective-permute-start(bf16[2,384,128]{2,1,0:T(8,128)(2,1)S(1)} %get-tuple-element.23), channel_id=1, source_target_pairs={{0,1},{1,2},{2,3},{3,4},{4,5},{5,6},{6,7},{7,8},{8,9},{9,10},{10,1... | collective-permute-start | bytes 589832 | tf_op jit(solution)/shard_map/ppermute | solution.py:18
  10.6 1.5 %copy-start.5 = (f32[4,4,129]{2,1,0:T(4,128)S(1)}, f32[4,4,129]{2,1,0:T(4,128)}, u32[]{:S(2)}) copy-start(f32[4,4,129]{2,1,0:T(4,128)} %param.10) | copy-start | bytes 24772
  10.6 10.6 %collective-permute-start.1 = (bf16[2,384,128]{2,1,0:T(8,128)(2,1)S(1)}, bf16[2,384,128]{2,1,0:T(8,128)(2,1)S(1)}, u32[]{:S(2)}, u32[]{:S(2)}) collective-permute-start(bf16[2,384,128]{2,1,0:T(8,128)(2,1)S(1)} %get-tuple-element.22), channel_id=1, source_target_pairs={{1,0},{2,1},{3,2},{4,3},{5,4},{6,5},{7,6},{8,7},{9,8},{10,9},{11,1... | collective-permute-start | bytes 589832 | tf_op jit(solution)/shard_map/ppermute | solution.py:18
  17.0 4.2 %copy-start.2 = (bf16[2,384,128]{2,1,0:T(8,128)(2,1)}, bf16[2,384,128]{2,1,0:T(8,128)(2,1)S(1)}, u32[]{:S(2)}) copy-start(bf16[2,384,128]{2,1,0:T(8,128)(2,1)S(1)} %collective-permute-done.left_ref) | copy-start | bytes 589828
  21.2 0.7 %copy-start.3 = (bf16[2,384,128]{2,1,0:T(8,128)(2,1)}, bf16[2,384,128]{2,1,0:T(8,128)(2,1)S(1)}, u32[]{:S(2)}) copy-start(bf16[2,384,128]{2,1,0:T(8,128)(2,1)S(1)} %collective-permute-done.1.right_ref) | copy-start | bytes 589828

commit v9 on v7

--- a/solution.py
+++ b/solution.py
@@ -133,11 +133,12 @@
     chan_count = lax.axis_size("chan")
     sky_count = lax.axis_size("sky")
 
-    image_rows = spectral[:, 0][:, None, None] * model[0][None]
+    model_full = lax.all_gather(model, "chan", axis=1, tiled=True)
+    spec_local = lax.dynamic_slice_in_dim(spectral, lax.axis_index("chan") * local_chans, local_chans, 0)
+    image = spec_local[:, 0][:, None, None] * model_full[0][None]
     for basis_idx in range(1, basis):
-        image_rows = image_rows + spectral[:, basis_idx][:, None, None] * model[basis_idx][None]
-    image_rows = image_rows.astype(jnp.bfloat16)
-    image = lax.all_to_all(image_rows, "chan", 0, 1, tiled=True)
+        image = image + spec_local[:, basis_idx][:, None, None] * model_full[basis_idx][None]
+    image = image.astype(jnp.bfloat16)
     def with_dirty(cols):
         return jnp.concatenate([image, jnp.concatenate([cols[:, : row_count // 2], cols[:, row_count // 2 :]], axis=2)], axis=1)
 
@@ -175,13 +176,12 @@
     )(spectral, *bands, left, image, right, dirty)
 
     pieces = lax.all_to_all(partial_value, "chan", 0, 0, tiled=True)
-    grad_share = pieces.sum(0)
 
     gram_rows = jnp.einsum("crt,cst->crs", psf_rows, psf_rows, precision=lax.Precision.HIGHEST)
     gram_cols = jnp.einsum("crt,cst->crs", psf_cols, psf_cols, precision=lax.Precision.HIGHEST)
     energy = jnp.sum(gram_rows * gram_cols, axis=(1, 2))
     curvature = jnp.sum(spectral * spectral * energy[:, None], axis=0)
-    model_new = model + grad_share / curvature[:, None, None]
+    model_new = model + pieces.sum(0) / curvature[:, None, None]
     return (residual, model_new)
 
 

time: 36.1 us -> 34.2 us (0.947)
  blocking collectives: 9.07 us -> 7.7 us
    all_to_all x1 -> x0, blocking collectives: 3.84 us -> none  [body(): image = lax.all_to_all(image_rows, 'chan', 0, 1, tiled=True)]
    all_gather x0 -> x1, blocking collectives: none -> 2.47 us  [body(): model_full = lax.all_gather(model, 'chan', axis=1, tiled=True)]
    mul x1, local copies, waits for them, and re-layouts: 0.96 us -> 0.03 us  [body(): image = spec_local[:, 0][:, None, None] * model_full[0][None]]
    unnamed x16, local copies, waits for them, and re-layouts: 3.05 us -> 3.68 us
where the time goes in v9:
time: 34.2 us; the launch traced here: 33.8 us
  Pallas kernels  8.37 us (24%)
  blocking collectives  7.7 us (23%)
  starting transfers between devices  6.06 us (18%)
  waiting for transfers between devices  4.71 us (14%)
  local copies, waits for them, and re-layouts  4.04 us (12%)
  other arithmetic  1.82 us (5%)
  between operations  0.73 us (2%)
  matrix products  0.42 us (1%)
    ppermute x2, starting transfers between devices, from_behind(): lax.ppermute(value, axis, [(source, source + steps) for source in range(f...  6.06 us
    all_to_all x1, blocking collectives, body(): pieces = lax.all_to_all(partial_value, 'chan', 0, 0, tiled=True)  5.23 us
    pallas_call x1, Pallas kernels, body(): pl.pallas_call(functools.partial(main_kernel, rank_count, local_chans, sk...  4.99 us
    ppermute x2, waiting for transfers between devices, from_behind(): lax.ppermute(value, axis, [(source, source + steps) for source in range(f...  4.71 us
    unnamed x16, local copies, waits for them, and re-layouts  3.68 us
    pallas_call x1, Pallas kernels, body(): pl.pallas_call(functools.partial(band_kernel, rank_count, local_chans, sl...  3.38 us
    all_gather x1, blocking collectives, body(): model_full = lax.all_gather(model, 'chan', axis=1, tiled=True)  2.47 us
    add x1, other arithmetic, body(): model_new = model + pieces.sum(0) / curvature[:, None, None]  0.8 us
  transfers between devices with their start and end apart: 2, of which 1 were waited for; matrix products, arithmetic and copies ran while one was open for 3% of the time, Pallas kernels for 10%

profile of v9, /device:TPU:0, one launch (start us, length us, event | category | flops | bytes accessed | tf_op | source)
XLA Modules:
  0.0 33.8 jit_solution(12551093047205812268)
XLA Ops:
  0.6 0.0 copy-start.7
  0.6 0.7 %copy-done.7 = f32[4,4]{1,0:T(4,128)S(1)} copy-done((f32[4,4]{1,0:T(4,128)S(1)}, f32[4,4]{1,0:T(4,128)}, u32[]{:S(2)}) %copy-start.7) | copy-done | bytes 88
  1.3 0.2 slice_reduce_fusion.3
  1.5 2.5 %all_gather.3 = f32[4,256,128]{2,1,0:T(8,128)S(1)} all-gather(f32[4,128,128]{2,1,0:T(8,128)} %param.7), channel_id=1, replica_groups=mesh['chan'=2,'sky'=16] {'chan'}, dimensions={1}, use_global_device_ids=true | all-gather | bytes 786432 | tf_op jit(solution)/shard_map/all_gather | solution.py:136
  4.0 0.0 copy-start
  4.1 0.9 %copy-done = bf16[2,256,128]{2,1,0:T(8,128)(2,1)S(1)} copy-done((bf16[2,256,128]{2,1,0:T(8,128)(2,1)S(1)}, bf16[2,256,128]{2,1,0:T(8,128)(2,1)}, u32[]{:S(2)}) %copy-start) | copy-done | bytes 131096
  4.9 0.1 fusion.1
  5.0 0.1 add_convert_fusion.xc_ref
  5.2 0.0 copy-start.1
  5.2 0.0 copy-start.5
  5.2 0.1 pad_maximum_fusion
  5.3 0.5 %copy-done.1 = bf16[2,256,128]{2,1,0:T(8,128)(2,1)} copy-done((bf16[2,256,128]{2,1,0:T(8,128)(2,1)}, bf16[2,256,128]{2,1,0:T(8,128)(2,1)S(1)}, u32[]{:S(2)}) %copy-start.1) | copy-done | bytes 131096
  5.8 4.8 %collective-permute-start = (bf16[2,384,128]{2,1,0:T(8,128)(2,1)S(1)}, bf16[2,384,128]{2,1,0:T(8,128)(2,1)S(1)}, u32[]{:S(2)}, u32[]{:S(2)}) collective-permute-start(bf16[2,384,128]{2,1,0:T(8,128)(2,1)S(1)} %get-tuple-element.23), channel_id=1, source_target_pairs={{0,1},{1,2},{2,3},{3,4},{4,5},{5,6},{6,7},{7,8},{8,9},{9,10},{10,1... | collective-permute-start | bytes 589832 | tf_op jit(solution)/shard_map/ppermute | solution.py:18
  10.6 0.0 copy-start.6
  10.6 1.3 %collective-permute-start.1 = (bf16[2,384,128]{2,1,0:T(8,128)(2,1)S(1)}, bf16[2,384,128]{2,1,0:T(8,128)(2,1)S(1)}, u32[]{:S(2)}, u32[]{:S(2)}) collective-permute-start(bf16[2,384,128]{2,1,0:T(8,128)(2,1)S(1)} %get-tuple-element.22), channel_id=1, source_target_pairs={{1,0},{2,1},{3,2},{4,3},{5,4},{6,5},{7,6},{8,7},{9,8},{10,9},{11,1... | collective-permute-start | bytes 589832 | tf_op jit(solution)/shard_map/ppermute | solution.py:18
  11.9 0.0 copy-done.5
  11.9 0.2 fusion.2
  12.1 0.0 copy-done.6
  12.1 0.7 %select_maximum_fusion.taps_ref = f32[4,8,512]{2,1,0:T(8,128)} fusion(f32[4,4,129]{2,1,0:T(4,128)S(1)} %copy-done.6, f32[4,4,129]{2,1,0:T(4,128)S(1)} %copy-done.5), kind=kLoop, calls=%fused_computation.10 | loop fusion | flops 65536 | bytes 82048 | tf_op jit(solution)/shard_map/concatenate | solution.py:150
  12.7 3.4 %shard_map.68 = (bf16[2,256,512]{2,1,0:T(8,128)(2,1)}, bf16[2,4,256,256]{3,2,1,0:T(8,128)(2,1)}, bf16[2,256,512]{2,1,0:T(8,128)(2,1)}, bf16[2,4,256,256]{3,2,1,0:T(8,128)(2,1)}) custom-call(f32[4,8,512]{2,1,0:T(8,128)} %select_maximum_fusion.taps_ref), custom_call_target="tpu_custom_call" | custom-call | tf_op jit(solution)/shard_map/pallas_call | solution.py:158
  16.1 0.3 fusion
  16.4 0.1 multiply_reduce_fusion
  16.5 0.0 collective-permute-done.left_ref
  16.5 0.0 copy-start.3
  16.5 4.7 %collective-permute-done.1.right_ref = bf16[2,384,128]{2,1,0:T(8,128)(2,1)S(1)} collective-permute-done((bf16[2,384,128]{2,1,0:T(8,128)(2,1)S(1)}, bf16[2,384,128]{2,1,0:T(8,128)(2,1)S(1)}, u32[]{:S(2)}, u32[]{:S(2)}) %collective-permute-start.1) | collective-permute-done | bytes 196640 | tf_op jit(solution)/shard_map/ppermute | solution.py:18
  21.2 0.0 copy-start.4
  21.2 0.0 copy-done.3
  21.2 0.7 %copy-done.4 = bf16[2,384,128]{2,1,0:T(8,128)(2,1)} copy-done((bf16[2,384,128]{2,1,0:T(8,128)(2,1)}, bf16[2,384,128]{2,1,0:T(8,128)(2,1)S(1)}, u32[]{:S(2)}) %copy-start.4) | copy-done | bytes 196632
  21.9 5.0 %shard_map.69 = (bf16[2,256,128]{2,1,0:T(8,128)(2,1)}, f32[2,4,128,128]{3,2,1,0:T(8,128)}) custom-call(f32[4,4]{1,0:T(4,128)} %spec_ref.1, bf16[2,256,512]{2,1,0:T(8,128)(2,1)} %get-tuple-element.8.colf_ref, bf16[2,4,256,256]{3,2,1,0:T(8,128)(2,1)} %get-tuple-element.9.rowf_ref, bf16[2,256,512]{2,1,0:T(8,128)(2,1)} %get-tuple-element.10.cola_ref, ...), custom_call_target="tpu_custom_call" | custom-call | tf_op jit(solution)/shard_map/pallas_call | solution.py:164
  26.9 5.2 %all_to_all.5 = f32[2,4,128,128]{3,2,1,0:T(8,128)S(1)} all-to-all(f32[2,4,128,128]{3,2,1,0:T(8,128)} %get-tuple-element.13), channel_id=1, replica_groups=mesh['chan'=2,'sky'=16] {'chan'}, dimensions={0} | all-to-all | bytes 1048576 | tf_op jit(solution)/shard_map/all_to_all | solution.py:178
  32.1 0.9 %copy-done.2 = f32[4,128,128]{2,1,0:T(8,128)S(1)} copy-done((f32[4,128,128]{2,1,0:T(8,128)S(1)}, f32[4,128,128]{2,1,0:T(8,128)}, u32[]{:S(2)}) %copy-start.2) | copy-done | bytes 262168
  33.0 0.8 %divide_add_fusion = f32[4,128,128]{2,1,0:T(8,128)} fusion(f32[4,128,128]{2,1,0:T(8,128)S(1)} %copy-done.2, f32[4,128,128]{2,1,0:T(8,128)S(1)} %reduce_sum.27, f32[4]{0:T(128)S(1)} %multiply_reduce_fusion), kind=kLoop, calls=%fused_computation.2 | loop fusion | flops 131072 | bytes 786448 | tf_op jit(solution)/shard_map/add | solution.py:184
  (4 shorter events, 0.1 us)
Async XLA Ops:
  0.6 0.7 %copy-start.7 = (f32[4,4]{1,0:T(4,128)S(1)}, f32[4,4]{1,0:T(4,128)}, u32[]{:S(2)}) copy-start(f32[4,4]{1,0:T(4,128)} %spec_ref.1) | copy-start | bytes 196
  4.0 0.9 %copy-start = (bf16[2,256,128]{2,1,0:T(8,128)(2,1)S(1)}, bf16[2,256,128]{2,1,0:T(8,128)(2,1)}, u32[]{:S(2)}) copy-start(bf16[2,256,128]{2,1,0:T(8,128)(2,1)} %dirty_ref.1) | copy-start | bytes 393220
  5.2 0.7 %copy-start.1 = (bf16[2,256,128]{2,1,0:T(8,128)(2,1)}, bf16[2,256,128]{2,1,0:T(8,128)(2,1)S(1)}, u32[]{:S(2)}) copy-start(bf16[2,256,128]{2,1,0:T(8,128)(2,1)S(1)} %add_convert_fusion.xc_ref) | copy-start | bytes 393220
  5.2 6.7 %copy-start.5 = (f32[4,4,129]{2,1,0:T(4,128)S(1)}, f32[4,4,129]{2,1,0:T(4,128)}, u32[]{:S(2)}) copy-start(f32[4,4,129]{2,1,0:T(4,128)} %param.9) | copy-start | bytes 24772
  5.8 10.6 %collective-permute-start = (bf16[2,384,128]{2,1,0:T(8,128)(2,1)S(1)}, bf16[2,384,128]{2,1,0:T(8,128)(2,1)S(1)}, u32[]{:S(2)}, u32[]{:S(2)}) collective-permute-start(bf16[2,384,128]{2,1,0:T(8,128)(2,1)S(1)} %get-tuple-element.23), channel_id=1, source_target_pairs={{0,1},{1,2},{2,3},{3,4},{4,5},{5,6},{6,7},{7,8},{8,9},{9,10},{10,1... | collective-permute-start | bytes 589832 | tf_op jit(solution)/shard_map/ppermute | solution.py:18
  10.6 1.5 %copy-start.6 = (f32[4,4,129]{2,1,0:T(4,128)S(1)}, f32[4,4,129]{2,1,0:T(4,128)}, u32[]{:S(2)}) copy-start(f32[4,4,129]{2,1,0:T(4,128)} %param.10) | copy-start | bytes 24772
  10.6 10.6 %collective-permute-start.1 = (bf16[2,384,128]{2,1,0:T(8,128)(2,1)S(1)}, bf16[2,384,128]{2,1,0:T(8,128)(2,1)S(1)}, u32[]{:S(2)}, u32[]{:S(2)}) collective-permute-start(bf16[2,384,128]{2,1,0:T(8,128)(2,1)S(1)} %get-tuple-element.22), channel_id=1, source_target_pairs={{1,0},{2,1},{3,2},{4,3},{5,4},{6,5},{7,6},{8,7},{9,8},{10,9},{11,1... | collective-permute-start | bytes 589832 | tf_op jit(solution)/shard_map/ppermute | solution.py:18
  16.5 4.7 %copy-start.3 = (bf16[2,384,128]{2,1,0:T(8,128)(2,1)}, bf16[2,384,128]{2,1,0:T(8,128)(2,1)S(1)}, u32[]{:S(2)}) copy-start(bf16[2,384,128]{2,1,0:T(8,128)(2,1)S(1)} %collective-permute-done.left_ref) | copy-start | bytes 589828
  21.2 0.7 %copy-start.4 = (bf16[2,384,128]{2,1,0:T(8,128)(2,1)}, bf16[2,384,128]{2,1,0:T(8,128)(2,1)S(1)}, u32[]{:S(2)}) copy-start(bf16[2,384,128]{2,1,0:T(8,128)(2,1)S(1)} %collective-permute-done.1.right_ref) | copy-start | bytes 589828
  32.1 1.0 %copy-start.2 = (f32[4,128,128]{2,1,0:T(8,128)S(1)}, f32[4,128,128]{2,1,0:T(8,128)}, u32[]{:S(2)}) copy-start(f32[4,128,128]{2,1,0:T(8,128)} %param.7) | copy-start | bytes 786436

commit v10 on v9

--- a/solution.py
+++ b/solution.py
@@ -181,7 +181,8 @@
     gram_cols = jnp.einsum("crt,cst->crs", psf_cols, psf_cols, precision=lax.Precision.HIGHEST)
     energy = jnp.sum(gram_rows * gram_cols, axis=(1, 2))
     curvature = jnp.sum(spectral * spectral * energy[:, None], axis=0)
-    model_new = model + pieces.sum(0) / curvature[:, None, None]
+    own_rows = lax.dynamic_slice_in_dim(model_full, lax.axis_index("chan") * piece_rows, piece_rows, 1)
+    model_new = own_rows + pieces.sum(0) / curvature[:, None, None]
     return (residual, model_new)
 
 

time: 34.2 us -> 33.3 us (0.974)
  local copies, waits for them, and re-layouts: 4.04 us -> 3.12 us
    unnamed x16 -> x14, local copies, waits for them, and re-layouts: 3.68 us -> 2.76 us
  transfers between devices with their start and end apart: 2 -> 2, of which waited for: 1 -> 1; matrix products, arithmetic and copies ran while one was open for 3% -> 4% of each run, Pallas kernels for 10% -> 10%
where the time goes in v10:
time: 33.3 us; the launch traced here: 32.9 us
  Pallas kernels  8.37 us (25%)
  blocking collectives  7.7 us (23%)
  starting transfers between devices  6.06 us (18%)
  waiting for transfers between devices  4.71 us (14%)
  local copies, waits for them, and re-layouts  3.12 us (9%)
  other arithmetic  1.83 us (5%)
  between operations  0.73 us (2%)
  matrix products  0.42 us (1%)
    ppermute x2, starting transfers between devices, from_behind(): lax.ppermute(value, axis, [(source, source + steps) for source in range(f...  6.06 us
    all_to_all x1, blocking collectives, body(): pieces = lax.all_to_all(partial_value, 'chan', 0, 0, tiled=True)  5.23 us
    pallas_call x1, Pallas kernels, body(): pl.pallas_call(functools.partial(main_kernel, rank_count, local_chans, sk...  4.99 us
    ppermute x2, waiting for transfers between devices, from_behind(): lax.ppermute(value, axis, [(source, source + steps) for source in range(f...  4.71 us
    pallas_call x1, Pallas kernels, body(): pl.pallas_call(functools.partial(band_kernel, rank_count, local_chans, sl...  3.38 us
    unnamed x14, local copies, waits for them, and re-layouts  2.76 us
    all_gather x1, blocking collectives, body(): model_full = lax.all_gather(model, 'chan', axis=1, tiled=True)  2.47 us
    add x1, other arithmetic, body(): model_new = own_rows + pieces.sum(0) / curvature[:, None, None]  0.81 us
  transfers between devices with their start and end apart: 2, of which 1 were waited for; matrix products, arithmetic and copies ran while one was open for 4% of the time, Pallas kernels for 10%

profile of v10, /device:TPU:0, one launch (start us, length us, event | category | flops | bytes accessed | tf_op | source)
XLA Modules:
  0.0 32.9 jit_solution(17452744948924829536)
XLA Ops:
  0.6 0.0 copy-start.6
  0.6 0.7 %copy-done.6 = f32[4,4]{1,0:T(4,128)S(1)} copy-done((f32[4,4]{1,0:T(4,128)S(1)}, f32[4,4]{1,0:T(4,128)}, u32[]{:S(2)}) %copy-start.6) | copy-done | bytes 88
  1.3 0.2 slice_reduce_fusion.3
  1.5 2.5 %all_gather.3 = f32[4,256,128]{2,1,0:T(8,128)S(1)} all-gather(f32[4,128,128]{2,1,0:T(8,128)} %param.7), channel_id=1, replica_groups=mesh['chan'=2,'sky'=16] {'chan'}, dimensions={1}, use_global_device_ids=true | all-gather | bytes 786432 | tf_op jit(solution)/shard_map/all_gather | solution.py:136
  4.0 0.0 copy-start
  4.1 0.9 %copy-done = bf16[2,256,128]{2,1,0:T(8,128)(2,1)S(1)} copy-done((bf16[2,256,128]{2,1,0:T(8,128)(2,1)S(1)}, bf16[2,256,128]{2,1,0:T(8,128)(2,1)}, u32[]{:S(2)}) %copy-start) | copy-done | bytes 131096
  4.9 0.1 fusion.1
  5.0 0.1 add_convert_fusion.xc_ref
  5.2 0.0 copy-start.1
  5.2 0.0 copy-start.4
  5.2 0.1 pad_maximum_fusion
  5.3 0.5 %copy-done.1 = bf16[2,256,128]{2,1,0:T(8,128)(2,1)} copy-done((bf16[2,256,128]{2,1,0:T(8,128)(2,1)}, bf16[2,256,128]{2,1,0:T(8,128)(2,1)S(1)}, u32[]{:S(2)}) %copy-start.1) | copy-done | bytes 131096
  5.8 4.8 %collective-permute-start = (bf16[2,384,128]{2,1,0:T(8,128)(2,1)S(1)}, bf16[2,384,128]{2,1,0:T(8,128)(2,1)S(1)}, u32[]{:S(2)}, u32[]{:S(2)}) collective-permute-start(bf16[2,384,128]{2,1,0:T(8,128)(2,1)S(1)} %get-tuple-element.23), channel_id=1, source_target_pairs={{0,1},{1,2},{2,3},{3,4},{4,5},{5,6},{6,7},{7,8},{8,9},{9,10},{10,1... | collective-permute-start | bytes 589832 | tf_op jit(solution)/shard_map/ppermute | solution.py:18
  10.6 0.0 copy-start.5
  10.6 1.3 %collective-permute-start.1 = (bf16[2,384,128]{2,1,0:T(8,128)(2,1)S(1)}, bf16[2,384,128]{2,1,0:T(8,128)(2,1)S(1)}, u32[]{:S(2)}, u32[]{:S(2)}) collective-permute-start(bf16[2,384,128]{2,1,0:T(8,128)(2,1)S(1)} %get-tuple-element.22), channel_id=1, source_target_pairs={{1,0},{2,1},{3,2},{4,3},{5,4},{6,5},{7,6},{8,7},{9,8},{10,9},{11,1... | collective-permute-start | bytes 589832 | tf_op jit(solution)/shard_map/ppermute | solution.py:18
  11.9 0.0 copy-done.4
  11.9 0.2 fusion.2
  12.1 0.0 copy-done.5
  12.1 0.7 %select_maximum_fusion.taps_ref = f32[4,8,512]{2,1,0:T(8,128)} fusion(f32[4,4,129]{2,1,0:T(4,128)S(1)} %copy-done.5, f32[4,4,129]{2,1,0:T(4,128)S(1)} %copy-done.4), kind=kLoop, calls=%fused_computation.10 | loop fusion | flops 65536 | bytes 82048 | tf_op jit(solution)/shard_map/concatenate | solution.py:150
  12.7 3.4 %shard_map.68 = (bf16[2,256,512]{2,1,0:T(8,128)(2,1)}, bf16[2,4,256,256]{3,2,1,0:T(8,128)(2,1)}, bf16[2,256,512]{2,1,0:T(8,128)(2,1)}, bf16[2,4,256,256]{3,2,1,0:T(8,128)(2,1)}) custom-call(f32[4,8,512]{2,1,0:T(8,128)} %select_maximum_fusion.taps_ref), custom_call_target="tpu_custom_call" | custom-call | tf_op jit(solution)/shard_map/pallas_call | solution.py:158
  16.1 0.3 fusion
  16.4 0.1 multiply_reduce_fusion
  16.5 0.0 collective-permute-done.left_ref
  16.5 0.0 copy-start.2
  16.5 4.7 %collective-permute-done.1.right_ref = bf16[2,384,128]{2,1,0:T(8,128)(2,1)S(1)} collective-permute-done((bf16[2,384,128]{2,1,0:T(8,128)(2,1)S(1)}, bf16[2,384,128]{2,1,0:T(8,128)(2,1)S(1)}, u32[]{:S(2)}, u32[]{:S(2)}) %collective-permute-start.1) | collective-permute-done | bytes 196640 | tf_op jit(solution)/shard_map/ppermute | solution.py:18
  21.2 0.0 copy-start.3
  21.2 0.0 copy-done.2
  21.2 0.7 %copy-done.3 = bf16[2,384,128]{2,1,0:T(8,128)(2,1)} copy-done((bf16[2,384,128]{2,1,0:T(8,128)(2,1)}, bf16[2,384,128]{2,1,0:T(8,128)(2,1)S(1)}, u32[]{:S(2)}) %copy-start.3) | copy-done | bytes 196632
  21.9 5.0 %shard_map.69 = (bf16[2,256,128]{2,1,0:T(8,128)(2,1)}, f32[2,4,128,128]{3,2,1,0:T(8,128)}) custom-call(f32[4,4]{1,0:T(4,128)} %spec_ref.1, bf16[2,256,512]{2,1,0:T(8,128)(2,1)} %get-tuple-element.8.colf_ref, bf16[2,4,256,256]{3,2,1,0:T(8,128)(2,1)} %get-tuple-element.9.rowf_ref, bf16[2,256,512]{2,1,0:T(8,128)(2,1)} %get-tuple-element.10.cola_ref, ...), custom_call_target="tpu_custom_call" | custom-call | tf_op jit(solution)/shard_map/pallas_call | solution.py:164
  26.9 5.2 %all_to_all.5 = f32[2,4,128,128]{3,2,1,0:T(8,128)S(1)} all-to-all(f32[2,4,128,128]{3,2,1,0:T(8,128)} %get-tuple-element.13), channel_id=1, replica_groups=mesh['chan'=2,'sky'=16] {'chan'}, dimensions={0} | all-to-all | bytes 1048576 | tf_op jit(solution)/shard_map/all_to_all | solution.py:178
  32.1 0.8 %divide_add_fusion = f32[4,128,128]{2,1,0:T(8,128)} fusion(f32[4,128,128]{2,1,0:T(8,128)S(1)} %reduce_sum.27, f32[4,256,128]{2,1,0:T(8,128)S(1)} %all_gather.3, s32[]{:T(128)S(6)} %select_n.7, f32[4]{0:T(128)S(1)} %multiply_reduce_fusion), kind=kLoop, calls=%fused_computation.2 | loop fusion | flops 131072 | bytes 786452 | tf_op jit(solution)/shard_map/add | solution.py:185
  (3 shorter events, 0.1 us)
Async XLA Ops:
  0.6 0.7 %copy-start.6 = (f32[4,4]{1,0:T(4,128)S(1)}, f32[4,4]{1,0:T(4,128)}, u32[]{:S(2)}) copy-start(f32[4,4]{1,0:T(4,128)} %spec_ref.1) | copy-start | bytes 196
  4.0 0.9 %copy-start = (bf16[2,256,128]{2,1,0:T(8,128)(2,1)S(1)}, bf16[2,256,128]{2,1,0:T(8,128)(2,1)}, u32[]{:S(2)}) copy-start(bf16[2,256,128]{2,1,0:T(8,128)(2,1)} %dirty_ref.1) | copy-start | bytes 393220
  5.2 0.7 %copy-start.1 = (bf16[2,256,128]{2,1,0:T(8,128)(2,1)}, bf16[2,256,128]{2,1,0:T(8,128)(2,1)S(1)}, u32[]{:S(2)}) copy-start(bf16[2,256,128]{2,1,0:T(8,128)(2,1)S(1)} %add_convert_fusion.xc_ref) | copy-start | bytes 393220
  5.2 6.7 %copy-start.4 = (f32[4,4,129]{2,1,0:T(4,128)S(1)}, f32[4,4,129]{2,1,0:T(4,128)}, u32[]{:S(2)}) copy-start(f32[4,4,129]{2,1,0:T(4,128)} %param.9) | copy-start | bytes 24772
  5.8 10.6 %collective-permute-start = (bf16[2,384,128]{2,1,0:T(8,128)(2,1)S(1)}, bf16[2,384,128]{2,1,0:T(8,128)(2,1)S(1)}, u32[]{:S(2)}, u32[]{:S(2)}) collective-permute-start(bf16[2,384,128]{2,1,0:T(8,128)(2,1)S(1)} %get-tuple-element.23), channel_id=1, source_target_pairs={{0,1},{1,2},{2,3},{3,4},{4,5},{5,6},{6,7},{7,8},{8,9},{9,10},{10,1... | collective-permute-start | bytes 589832 | tf_op jit(solution)/shard_map/ppermute | solution.py:18
  10.6 1.5 %copy-start.5 = (f32[4,4,129]{2,1,0:T(4,128)S(1)}, f32[4,4,129]{2,1,0:T(4,128)}, u32[]{:S(2)}) copy-start(f32[4,4,129]{2,1,0:T(4,128)} %param.10) | copy-start | bytes 24772
  10.6 10.6 %collective-permute-start.1 = (bf16[2,384,128]{2,1,0:T(8,128)(2,1)S(1)}, bf16[2,384,128]{2,1,0:T(8,128)(2,1)S(1)}, u32[]{:S(2)}, u32[]{:S(2)}) collective-permute-start(bf16[2,384,128]{2,1,0:T(8,128)(2,1)S(1)} %get-tuple-element.22), channel_id=1, source_target_pairs={{1,0},{2,1},{3,2},{4,3},{5,4},{6,5},{7,6},{8,7},{9,8},{10,9},{11,1... | collective-permute-start | bytes 589832 | tf_op jit(solution)/shard_map/ppermute | solution.py:18
  16.5 4.7 %copy-start.2 = (bf16[2,384,128]{2,1,0:T(8,128)(2,1)}, bf16[2,384,128]{2,1,0:T(8,128)(2,1)S(1)}, u32[]{:S(2)}) copy-start(bf16[2,384,128]{2,1,0:T(8,128)(2,1)S(1)} %collective-permute-done.left_ref) | copy-start | bytes 589828
  21.2 0.7 %copy-start.3 = (bf16[2,384,128]{2,1,0:T(8,128)(2,1)}, bf16[2,384,128]{2,1,0:T(8,128)(2,1)S(1)}, u32[]{:S(2)}) copy-start(bf16[2,384,128]{2,1,0:T(8,128)(2,1)S(1)} %collective-permute-done.1.right_ref) | copy-start | bytes 589828

commit v11 on v10

--- a/solution.py
+++ b/solution.py
@@ -133,17 +133,20 @@
     chan_count = lax.axis_size("chan")
     sky_count = lax.axis_size("sky")
 
+    def packed(cols):
+        return jnp.concatenate([cols[:, : row_count // 2], cols[:, row_count // 2 :]], axis=2)
+
+    model, dirty_r, dirty_l = lax.optimization_barrier(
+        (model, packed(dirty[:, :, slot_width - HALF :]), packed(dirty[:, :, :HALF]))
+    )
     model_full = lax.all_gather(model, "chan", axis=1, tiled=True)
     spec_local = lax.dynamic_slice_in_dim(spectral, lax.axis_index("chan") * local_chans, local_chans, 0)
     image = spec_local[:, 0][:, None, None] * model_full[0][None]
     for basis_idx in range(1, basis):
         image = image + spec_local[:, basis_idx][:, None, None] * model_full[basis_idx][None]
     image = image.astype(jnp.bfloat16)
-    def with_dirty(cols):
-        return jnp.concatenate([image, jnp.concatenate([cols[:, : row_count // 2], cols[:, row_count // 2 :]], axis=2)], axis=1)
-
-    to_right = with_dirty(dirty[:, :, slot_width - HALF :])
-    to_left = with_dirty(dirty[:, :, :HALF])
+    to_right = jnp.concatenate([image, dirty_r], axis=1)
+    to_left = jnp.concatenate([image, dirty_l], axis=1)
     left = from_behind(to_right, "sky", 1)
     right = from_behind(to_left, "sky", -1)
 

time: 33.3 us -> 34.2 us (1.027)
  local copies, waits for them, and re-layouts: 3.12 us -> 4.09 us
    slice x1, local copies, waits for them, and re-layouts: 0.11 us -> 1.05 us  [packed(): cols[:, :row_count // 2]]
  transfers between devices with their start and end apart: 2 -> 2, of which waited for: 1 -> 1; matrix products, arithmetic and copies ran while one was open for 4% -> 3% of each run, Pallas kernels for 10% -> 10%
where the time goes in v11:
time: 34.2 us; the launch traced here: 33.8 us
  Pallas kernels  8.37 us (24%)
  blocking collectives  7.48 us (22%)
  starting transfers between devices  6.06 us (18%)
  waiting for transfers between devices  4.71 us (14%)
  local copies, waits for them, and re-layouts  4.09 us (12%)
  other arithmetic  1.88 us (5%)
  between operations  0.75 us (2%)
  matrix products  0.42 us (1%)
    ppermute x2, starting transfers between devices, from_behind(): lax.ppermute(value, axis, [(source, source + steps) for source in range(f...  6.06 us
    all_to_all x1, blocking collectives, body(): pieces = lax.all_to_all(partial_value, 'chan', 0, 0, tiled=True)  5.23 us
    pallas_call x1, Pallas kernels, body(): pl.pallas_call(functools.partial(main_kernel, rank_count, local_chans, sk...  4.99 us
    ppermute x2, waiting for transfers between devices, from_behind(): lax.ppermute(value, axis, [(source, source + steps) for source in range(f...  4.71 us
    pallas_call x1, Pallas kernels, body(): pl.pallas_call(functools.partial(band_kernel, rank_count, local_chans, sl...  3.38 us
    unnamed x14, local copies, waits for them, and re-layouts  2.79 us
    all_gather x1, blocking collectives, body(): model_full = lax.all_gather(model, 'chan', axis=1, tiled=True)  2.25 us
    slice x1, local copies, waits for them, and re-layouts, packed(): cols[:, :row_count // 2]  1.05 us
  transfers between devices with their start and end apart: 2, of which 1 were waited for; matrix products, arithmetic and copies ran while one was open for 3% of the time, Pallas kernels for 10%

profile of v11, /device:TPU:0, one launch (start us, length us, event | category | flops | bytes accessed | tf_op | source)
XLA Modules:
  0.0 33.8 jit_solution(16617387339253091492)
XLA Ops:
  0.6 1.0 %fusion.1 = (bf16[2,128,64]{2,1,0:T(8,128)(2,1)S(1)}, bf16[2,128,64]{2,1,0:T(8,128)(2,1)S(1)}, bf16[2,128,64]{2,1,0:T(8,128)(2,1)S(1)}, bf16[2,128,64]{2,1,0:T(8,128)(2,1)S(1)}) fusion(bf16[2,256,128]{2,1,0:T(8,128)(2,1)} %dirty_ref.1), kind=kLoop, calls=%fused_computation.20 | loop fusion | bytes 262144 | tf_op jit(solution)/shard_map/slice | solution.py:137
  1.7 0.0 copy-start.1
  1.7 0.1 pad_maximum_fusion.2
  1.8 0.8 %copy-done.1 = f32[4,128,128]{2,1,0:T(8,128)S(1)} copy-done((f32[4,128,128]{2,1,0:T(8,128)S(1)}, f32[4,128,128]{2,1,0:T(8,128)}, u32[]{:S(2)}) %copy-start.1) | copy-done | bytes 262168
  2.6 2.2 %all_gather.3 = f32[4,256,128]{2,1,0:T(8,128)S(1)} all-gather(f32[4,128,128]{2,1,0:T(8,128)S(1)} %copy-done.1), channel_id=1, replica_groups=mesh['chan'=2,'sky'=16] {'chan'}, dimensions={1}, use_global_device_ids=true | all-gather | bytes 786432 | tf_op jit(solution)/shard_map/all_gather | solution.py:142
  4.9 0.0 copy-start.6
  4.9 0.7 %copy-done.6 = f32[4,4]{1,0:T(4,128)S(1)} copy-done((f32[4,4]{1,0:T(4,128)S(1)}, f32[4,4]{1,0:T(4,128)}, u32[]{:S(2)}) %copy-start.6) | copy-done | bytes 88
  5.6 0.2 slice_reduce_fusion.3
  5.8 0.1 add_convert_fusion.xc_ref
  6.0 0.0 copy-start
  6.0 0.0 copy-start.4
  6.1 0.6 %copy-done = bf16[2,256,128]{2,1,0:T(8,128)(2,1)} copy-done((bf16[2,256,128]{2,1,0:T(8,128)(2,1)}, bf16[2,256,128]{2,1,0:T(8,128)(2,1)S(1)}, u32[]{:S(2)}) %copy-start) | copy-done | bytes 131096
  6.6 4.8 %collective-permute-start = (bf16[2,384,128]{2,1,0:T(8,128)(2,1)S(1)}, bf16[2,384,128]{2,1,0:T(8,128)(2,1)S(1)}, u32[]{:S(2)}, u32[]{:S(2)}) collective-permute-start(bf16[2,384,128]{2,1,0:T(8,128)(2,1)S(1)} %get-tuple-element.29), channel_id=1, source_target_pairs={{0,1},{1,2},{2,3},{3,4},{4,5},{5,6},{6,7},{7,8},{8,9},{9,10},{10,1... | collective-permute-start | bytes 589832 | tf_op jit(solution)/shard_map/ppermute | solution.py:18
  11.4 0.0 copy-start.5
  11.4 1.3 %collective-permute-start.1 = (bf16[2,384,128]{2,1,0:T(8,128)(2,1)S(1)}, bf16[2,384,128]{2,1,0:T(8,128)(2,1)S(1)}, u32[]{:S(2)}, u32[]{:S(2)}) collective-permute-start(bf16[2,384,128]{2,1,0:T(8,128)(2,1)S(1)} %get-tuple-element.28), channel_id=1, source_target_pairs={{1,0},{2,1},{3,2},{4,3},{5,4},{6,5},{7,6},{8,7},{9,8},{10,9},{11,1... | collective-permute-start | bytes 589832 | tf_op jit(solution)/shard_map/ppermute | solution.py:18
  12.7 0.0 copy-done.4
  12.7 0.2 fusion.2
  12.9 0.0 copy-done.5
  12.9 0.7 %select_maximum_fusion.taps_ref = f32[4,8,512]{2,1,0:T(8,128)} fusion(f32[4,4,129]{2,1,0:T(4,128)S(1)} %copy-done.5, f32[4,4,129]{2,1,0:T(4,128)S(1)} %copy-done.4), kind=kLoop, calls=%fused_computation.10 | loop fusion | flops 65536 | bytes 82048 | tf_op jit(solution)/shard_map/concatenate | solution.py:153
  13.5 3.4 %shard_map.68 = (bf16[2,256,512]{2,1,0:T(8,128)(2,1)}, bf16[2,4,256,256]{3,2,1,0:T(8,128)(2,1)}, bf16[2,256,512]{2,1,0:T(8,128)(2,1)}, bf16[2,4,256,256]{3,2,1,0:T(8,128)(2,1)}) custom-call(f32[4,8,512]{2,1,0:T(8,128)} %select_maximum_fusion.taps_ref), custom_call_target="tpu_custom_call" | custom-call | tf_op jit(solution)/shard_map/pallas_call | solution.py:161
  16.9 0.3 fusion
  17.2 0.1 multiply_reduce_fusion
  17.3 0.0 collective-permute-done.left_ref
  17.3 0.0 copy-start.2
  17.3 4.7 %collective-permute-done.1.right_ref = bf16[2,384,128]{2,1,0:T(8,128)(2,1)S(1)} collective-permute-done((bf16[2,384,128]{2,1,0:T(8,128)(2,1)S(1)}, bf16[2,384,128]{2,1,0:T(8,128)(2,1)S(1)}, u32[]{:S(2)}, u32[]{:S(2)}) %collective-permute-start.1) | collective-permute-done | bytes 196640 | tf_op jit(solution)/shard_map/ppermute | solution.py:18
  22.0 0.0 copy-start.3
  22.0 0.0 copy-done.2
  22.0 0.7 %copy-done.3 = bf16[2,384,128]{2,1,0:T(8,128)(2,1)} copy-done((bf16[2,384,128]{2,1,0:T(8,128)(2,1)}, bf16[2,384,128]{2,1,0:T(8,128)(2,1)S(1)}, u32[]{:S(2)}) %copy-start.3) | copy-done | bytes 196632
  22.7 5.0 %shard_map.69 = (bf16[2,256,128]{2,1,0:T(8,128)(2,1)}, f32[2,4,128,128]{3,2,1,0:T(8,128)}) custom-call(f32[4,4]{1,0:T(4,128)} %spec_ref.1, bf16[2,256,512]{2,1,0:T(8,128)(2,1)} %get-tuple-element.11.colf_ref, bf16[2,4,256,256]{3,2,1,0:T(8,128)(2,1)} %get-tuple-element.12.rowf_ref, bf16[2,256,512]{2,1,0:T(8,128)(2,1)} %get-tuple-element.13.cola_ref, ...), custom_call_target="tpu_custom_call" | custom-call | tf_op jit(solution)/shard_map/pallas_call | solution.py:167
  27.7 5.2 %all_to_all.5 = f32[2,4,128,128]{3,2,1,0:T(8,128)S(1)} all-to-all(f32[2,4,128,128]{3,2,1,0:T(8,128)} %get-tuple-element.19), channel_id=1, replica_groups=mesh['chan'=2,'sky'=16] {'chan'}, dimensions={0} | all-to-all | bytes 1048576 | tf_op jit(solution)/shard_map/all_to_all | solution.py:181
  32.9 0.8 %divide_add_fusion = f32[4,128,128]{2,1,0:T(8,128)} fusion(f32[4,128,128]{2,1,0:T(8,128)S(1)} %reduce_sum.27, f32[4,256,128]{2,1,0:T(8,128)S(1)} %all_gather.3, s32[]{:T(128)S(6)} %select_n.7, f32[4]{0:T(128)S(1)} %multiply_reduce_fusion), kind=kLoop, calls=%fused_computation.2 | loop fusion | flops 131072 | bytes 786452 | tf_op jit(solution)/shard_map/add | solution.py:188
  (4 shorter events, 0.1 us)
Async XLA Ops:
  1.7 1.0 %copy-start.1 = (f32[4,128,128]{2,1,0:T(8,128)S(1)}, f32[4,128,128]{2,1,0:T(8,128)}, u32[]{:S(2)}) copy-start(f32[4,128,128]{2,1,0:T(8,128)} %param.7) | copy-start | bytes 786436
  4.9 0.7 %copy-start.6 = (f32[4,4]{1,0:T(4,128)S(1)}, f32[4,4]{1,0:T(4,128)}, u32[]{:S(2)}) copy-start(f32[4,4]{1,0:T(4,128)} %spec_ref.1) | copy-start | bytes 196
  6.0 0.7 %copy-start = (bf16[2,256,128]{2,1,0:T(8,128)(2,1)}, bf16[2,256,128]{2,1,0:T(8,128)(2,1)S(1)}, u32[]{:S(2)}) copy-start(bf16[2,256,128]{2,1,0:T(8,128)(2,1)S(1)} %add_convert_fusion.xc_ref) | copy-start | bytes 393220
  6.0 6.7 %copy-start.4 = (f32[4,4,129]{2,1,0:T(4,128)S(1)}, f32[4,4,129]{2,1,0:T(4,128)}, u32[]{:S(2)}) copy-start(f32[4,4,129]{2,1,0:T(4,128)} %param.9) | copy-start | bytes 24772
  6.6 10.6 %collective-permute-start = (bf16[2,384,128]{2,1,0:T(8,128)(2,1)S(1)}, bf16[2,384,128]{2,1,0:T(8,128)(2,1)S(1)}, u32[]{:S(2)}, u32[]{:S(2)}) collective-permute-start(bf16[2,384,128]{2,1,0:T(8,128)(2,1)S(1)} %get-tuple-element.29), channel_id=1, source_target_pairs={{0,1},{1,2},{2,3},{3,4},{4,5},{5,6},{6,7},{7,8},{8,9},{9,10},{10,1... | collective-permute-start | bytes 589832 | tf_op jit(solution)/shard_map/ppermute | solution.py:18
  11.4 1.5 %copy-start.5 = (f32[4,4,129]{2,1,0:T(4,128)S(1)}, f32[4,4,129]{2,1,0:T(4,128)}, u32[]{:S(2)}) copy-start(f32[4,4,129]{2,1,0:T(4,128)} %param.10) | copy-start | bytes 24772
  11.4 10.6 %collective-permute-start.1 = (bf16[2,384,128]{2,1,0:T(8,128)(2,1)S(1)}, bf16[2,384,128]{2,1,0:T(8,128)(2,1)S(1)}, u32[]{:S(2)}, u32[]{:S(2)}) collective-permute-start(bf16[2,384,128]{2,1,0:T(8,128)(2,1)S(1)} %get-tuple-element.28), channel_id=1, source_target_pairs={{1,0},{2,1},{3,2},{4,3},{5,4},{6,5},{7,6},{8,7},{9,8},{10,9},{11,1... | collective-permute-start | bytes 589832 | tf_op jit(solution)/shard_map/ppermute | solution.py:18
  17.3 4.7 %copy-start.2 = (bf16[2,384,128]{2,1,0:T(8,128)(2,1)}, bf16[2,384,128]{2,1,0:T(8,128)(2,1)S(1)}, u32[]{:S(2)}) copy-start(bf16[2,384,128]{2,1,0:T(8,128)(2,1)S(1)} %collective-permute-done.left_ref) | copy-start | bytes 589828
  22.0 0.7 %copy-start.3 = (bf16[2,384,128]{2,1,0:T(8,128)(2,1)}, bf16[2,384,128]{2,1,0:T(8,128)(2,1)S(1)}, u32[]{:S(2)}) copy-start(bf16[2,384,128]{2,1,0:T(8,128)(2,1)S(1)} %collective-permute-done.1.right_ref) | copy-start | bytes 589828

commit v12 on v10

--- a/solution.py
+++ b/solution.py
@@ -65,14 +65,14 @@
     left_ref, xc_ref, right_ref, dirty_ref, res_ref, part_ref,
 ):
     slot = xc_ref.shape[-1]
-    rows = xc_ref.shape[0]
+    rows = dirty_ref.shape[0]
     pieces, basis, piece_rows, _ = part_ref.shape
     first_chan = lax.axis_index("chan") * local_chans
     sky_index = lax.axis_index("sky")
     lane = lax.broadcasted_iota(jnp.int32, (rows, slot), 1)
     step = pl.program_id(0)
     if True:
-        xl, xc, xr = left_ref[:rows], xc_ref[...], right_ref[:rows]
+        xl, xc, xr = left_ref[:rows], xc_ref[:rows], right_ref[:rows]
         stacked = jnp.concatenate(
             [jnp.concatenate([xl, xc], axis=1), jnp.concatenate([xc, xr], axis=1)], axis=0
         )
@@ -173,7 +173,7 @@
             per_chan(dirty.shape),
             pl.BlockSpec((chan_count, basis, piece_rows, slot_width), lambda c: (0, 0, 0, 0)),
         ],
-    )(spectral, *bands, left, image, right, dirty)
+    )(spectral, *bands, left, to_right, right, dirty)
 
     pieces = lax.all_to_all(partial_value, "chan", 0, 0, tiled=True)
 

time: 33.3 us -> 32.8 us (0.985)
  local copies, waits for them, and re-layouts: 3.12 us -> 2.6 us
    unnamed x14, local copies, waits for them, and re-layouts: 2.76 us -> 2.23 us
where the time goes in v12:
time: 32.8 us; the launch traced here: 32.4 us
  Pallas kernels  8.37 us (26%)
  blocking collectives  7.7 us (23%)
  starting transfers between devices  6.07 us (19%)
  waiting for transfers between devices  4.7 us (14%)
  local copies, waits for them, and re-layouts  2.6 us (8%)
  other arithmetic  1.83 us (6%)
  between operations  0.73 us (2%)
  matrix products  0.42 us (1%)
    ppermute x2, starting transfers between devices, from_behind(): lax.ppermute(value, axis, [(source, source + steps) for source in range(f...  6.07 us
    all_to_all x1, blocking collectives, body(): pieces = lax.all_to_all(partial_value, 'chan', 0, 0, tiled=True)  5.23 us
    pallas_call x1, Pallas kernels, body(): pl.pallas_call(functools.partial(main_kernel, rank_count, local_chans, sk...  4.99 us
    ppermute x2, waiting for transfers between devices, from_behind(): lax.ppermute(value, axis, [(source, source + steps) for source in range(f...  4.7 us
    pallas_call x1, Pallas kernels, body(): pl.pallas_call(functools.partial(band_kernel, rank_count, local_chans, sl...  3.38 us
    all_gather x1, blocking collectives, body(): model_full = lax.all_gather(model, 'chan', axis=1, tiled=True)  2.47 us
    unnamed x14, local copies, waits for them, and re-layouts  2.23 us
    add x1, other arithmetic, body(): model_new = own_rows + pieces.sum(0) / curvature[:, None, None]  0.81 us
  transfers between devices with their start and end apart: 2, of which 1 were waited for; matrix products, arithmetic and copies ran while one was open for 4% of the time, Pallas kernels for 10%

profile of v12, /device:TPU:0, one launch (start us, length us, event | category | flops | bytes accessed | tf_op | source)
XLA Modules:
  0.0 32.4 jit_solution(8493930299108881061)
XLA Ops:
  0.6 0.0 copy-start.6
  0.6 0.7 %copy-done.6 = f32[4,4]{1,0:T(4,128)S(1)} copy-done((f32[4,4]{1,0:T(4,128)S(1)}, f32[4,4]{1,0:T(4,128)}, u32[]{:S(2)}) %copy-start.6) | copy-done | bytes 88
  1.3 0.2 slice_reduce_fusion.3
  1.5 2.5 %all_gather.3 = f32[4,256,128]{2,1,0:T(8,128)S(1)} all-gather(f32[4,128,128]{2,1,0:T(8,128)} %param.7), channel_id=1, replica_groups=mesh['chan'=2,'sky'=16] {'chan'}, dimensions={1}, use_global_device_ids=true | all-gather | bytes 786432 | tf_op jit(solution)/shard_map/all_gather | solution.py:136
  4.0 0.0 copy-start
  4.1 0.9 %copy-done = bf16[2,256,128]{2,1,0:T(8,128)(2,1)S(1)} copy-done((bf16[2,256,128]{2,1,0:T(8,128)(2,1)S(1)}, bf16[2,256,128]{2,1,0:T(8,128)(2,1)}, u32[]{:S(2)}) %copy-start) | copy-done | bytes 131096
  4.9 0.1 fusion.1
  5.0 0.1 add_convert_fusion
  5.2 0.0 copy-start.4
  5.2 0.1 pad_maximum_fusion
  5.3 0.0 copy-start.1
  5.3 4.8 %collective-permute-start = (bf16[2,384,128]{2,1,0:T(8,128)(2,1)S(1)}, bf16[2,384,128]{2,1,0:T(8,128)(2,1)S(1)}, u32[]{:S(2)}, u32[]{:S(2)}) collective-permute-start(bf16[2,384,128]{2,1,0:T(8,128)(2,1)S(1)} %get-tuple-element.23.xc_ref), channel_id=1, source_target_pairs={{0,1},{1,2},{2,3},{3,4},{4,5},{5,6},{6,7},{7,8},{8,9},{9,10},{10,1... | collective-permute-start | bytes 589832 | tf_op jit(solution)/shard_map/ppermute | solution.py:18
  10.1 0.0 copy-start.5
  10.1 1.3 %collective-permute-start.1 = (bf16[2,384,128]{2,1,0:T(8,128)(2,1)S(1)}, bf16[2,384,128]{2,1,0:T(8,128)(2,1)S(1)}, u32[]{:S(2)}, u32[]{:S(2)}) collective-permute-start(bf16[2,384,128]{2,1,0:T(8,128)(2,1)S(1)} %get-tuple-element.22), channel_id=1, source_target_pairs={{1,0},{2,1},{3,2},{4,3},{5,4},{6,5},{7,6},{8,7},{9,8},{10,9},{11,1... | collective-permute-start | bytes 589832 | tf_op jit(solution)/shard_map/ppermute | solution.py:18
  11.4 0.0 copy-done.4
  11.4 0.2 fusion.2
  11.6 0.0 copy-done.5
  11.6 0.7 %select_maximum_fusion.taps_ref = f32[4,8,512]{2,1,0:T(8,128)} fusion(f32[4,4,129]{2,1,0:T(4,128)S(1)} %copy-done.5, f32[4,4,129]{2,1,0:T(4,128)S(1)} %copy-done.4), kind=kLoop, calls=%fused_computation.10 | loop fusion | flops 65536 | bytes 82048 | tf_op jit(solution)/shard_map/concatenate | solution.py:150
  12.2 3.4 %shard_map.68 = (bf16[2,256,512]{2,1,0:T(8,128)(2,1)}, bf16[2,4,256,256]{3,2,1,0:T(8,128)(2,1)}, bf16[2,256,512]{2,1,0:T(8,128)(2,1)}, bf16[2,4,256,256]{3,2,1,0:T(8,128)(2,1)}) custom-call(f32[4,8,512]{2,1,0:T(8,128)} %select_maximum_fusion.taps_ref), custom_call_target="tpu_custom_call" | custom-call | tf_op jit(solution)/shard_map/pallas_call | solution.py:158
  15.6 0.3 fusion
  15.9 0.1 multiply_reduce_fusion
  16.0 0.0 collective-permute-done.left_ref
  16.0 0.0 copy-start.2
  16.0 4.7 %collective-permute-done.1.right_ref = bf16[2,384,128]{2,1,0:T(8,128)(2,1)S(1)} collective-permute-done((bf16[2,384,128]{2,1,0:T(8,128)(2,1)S(1)}, bf16[2,384,128]{2,1,0:T(8,128)(2,1)S(1)}, u32[]{:S(2)}, u32[]{:S(2)}) %collective-permute-start.1) | collective-permute-done | bytes 196640 | tf_op jit(solution)/shard_map/ppermute | solution.py:18
  20.7 0.0 copy-start.3
  20.7 0.0 copy-done.1
  20.7 0.0 copy-done.2
  20.7 0.7 %copy-done.3 = bf16[2,384,128]{2,1,0:T(8,128)(2,1)} copy-done((bf16[2,384,128]{2,1,0:T(8,128)(2,1)}, bf16[2,384,128]{2,1,0:T(8,128)(2,1)S(1)}, u32[]{:S(2)}) %copy-start.3) | copy-done | bytes 196632
  21.4 5.0 %shard_map.69 = (bf16[2,256,128]{2,1,0:T(8,128)(2,1)}, f32[2,4,128,128]{3,2,1,0:T(8,128)}) custom-call(f32[4,4]{1,0:T(4,128)} %spec_ref.1, bf16[2,256,512]{2,1,0:T(8,128)(2,1)} %get-tuple-element.8.colf_ref, bf16[2,4,256,256]{3,2,1,0:T(8,128)(2,1)} %get-tuple-element.9.rowf_ref, bf16[2,256,512]{2,1,0:T(8,128)(2,1)} %get-tuple-element.10.cola_ref, ...), custom_call_target="tpu_custom_call" | custom-call | tf_op jit(solution)/shard_map/pallas_call | solution.py:164
  26.4 5.2 %all_to_all.5 = f32[2,4,128,128]{3,2,1,0:T(8,128)S(1)} all-to-all(f32[2,4,128,128]{3,2,1,0:T(8,128)} %get-tuple-element.13), channel_id=1, replica_groups=mesh['chan'=2,'sky'=16] {'chan'}, dimensions={0} | all-to-all | bytes 1048576 | tf_op jit(solution)/shard_map/all_to_all | solution.py:178
  31.6 0.8 %divide_add_fusion = f32[4,128,128]{2,1,0:T(8,128)} fusion(f32[4,128,128]{2,1,0:T(8,128)S(1)} %reduce_sum.27, f32[4,256,128]{2,1,0:T(8,128)S(1)} %all_gather.3, s32[]{:T(128)S(6)} %select_n.7, f32[4]{0:T(128)S(1)} %multiply_reduce_fusion), kind=kLoop, calls=%fused_computation.2 | loop fusion | flops 131072 | bytes 786452 | tf_op jit(solution)/shard_map/add | solution.py:185
  (3 shorter events, 0.1 us)
Async XLA Ops:
  0.6 0.7 %copy-start.6 = (f32[4,4]{1,0:T(4,128)S(1)}, f32[4,4]{1,0:T(4,128)}, u32[]{:S(2)}) copy-start(f32[4,4]{1,0:T(4,128)} %spec_ref.1) | copy-start | bytes 196
  4.0 0.9 %copy-start = (bf16[2,256,128]{2,1,0:T(8,128)(2,1)S(1)}, bf16[2,256,128]{2,1,0:T(8,128)(2,1)}, u32[]{:S(2)}) copy-start(bf16[2,256,128]{2,1,0:T(8,128)(2,1)} %dirty_ref.1) | copy-start | bytes 393220
  5.2 6.2 %copy-start.4 = (f32[4,4,129]{2,1,0:T(4,128)S(1)}, f32[4,4,129]{2,1,0:T(4,128)}, u32[]{:S(2)}) copy-start(f32[4,4,129]{2,1,0:T(4,128)} %param.9) | copy-start | bytes 24772
  5.3 15.4 %copy-start.1 = (bf16[2,384,128]{2,1,0:T(8,128)(2,1)}, bf16[2,384,128]{2,1,0:T(8,128)(2,1)S(1)}, u32[]{:S(2)}) copy-start(bf16[2,384,128]{2,1,0:T(8,128)(2,1)S(1)} %get-tuple-element.23.xc_ref) | copy-start | bytes 589828
  5.3 10.7 %collective-permute-start = (bf16[2,384,128]{2,1,0:T(8,128)(2,1)S(1)}, bf16[2,384,128]{2,1,0:T(8,128)(2,1)S(1)}, u32[]{:S(2)}, u32[]{:S(2)}) collective-permute-start(bf16[2,384,128]{2,1,0:T(8,128)(2,1)S(1)} %get-tuple-element.23.xc_ref), channel_id=1, source_target_pairs={{0,1},{1,2},{2,3},{3,4},{4,5},{5,6},{6,7},{7,8},{8,9},{9,10},{10,1... | collective-permute-start | bytes 589832 | tf_op jit(solution)/shard_map/ppermute | solution.py:18
  10.1 1.5 %copy-start.5 = (f32[4,4,129]{2,1,0:T(4,128)S(1)}, f32[4,4,129]{2,1,0:T(4,128)}, u32[]{:S(2)}) copy-start(f32[4,4,129]{2,1,0:T(4,128)} %param.10) | copy-start | bytes 24772
  10.1 10.6 %collective-permute-start.1 = (bf16[2,384,128]{2,1,0:T(8,128)(2,1)S(1)}, bf16[2,384,128]{2,1,0:T(8,128)(2,1)S(1)}, u32[]{:S(2)}, u32[]{:S(2)}) collective-permute-start(bf16[2,384,128]{2,1,0:T(8,128)(2,1)S(1)} %get-tuple-element.22), channel_id=1, source_target_pairs={{1,0},{2,1},{3,2},{4,3},{5,4},{6,5},{7,6},{8,7},{9,8},{10,9},{11,1... | collective-permute-start | bytes 589832 | tf_op jit(solution)/shard_map/ppermute | solution.py:18
  16.0 4.7 %copy-start.2 = (bf16[2,384,128]{2,1,0:T(8,128)(2,1)}, bf16[2,384,128]{2,1,0:T(8,128)(2,1)S(1)}, u32[]{:S(2)}) copy-start(bf16[2,384,128]{2,1,0:T(8,128)(2,1)S(1)} %collective-permute-done.left_ref) | copy-start | bytes 589828
  20.7 0.7 %copy-start.3 = (bf16[2,384,128]{2,1,0:T(8,128)(2,1)}, bf16[2,384,128]{2,1,0:T(8,128)(2,1)S(1)}, u32[]{:S(2)}) copy-start(bf16[2,384,128]{2,1,0:T(8,128)(2,1)S(1)} %collective-permute-done.1.right_ref) | copy-start | bytes 589828

commit v13 on v11

--- a/solution.py
+++ b/solution.py
@@ -65,14 +65,14 @@
     left_ref, xc_ref, right_ref, dirty_ref, res_ref, part_ref,
 ):
     slot = xc_ref.shape[-1]
-    rows = xc_ref.shape[0]
+    rows = dirty_ref.shape[0]
     pieces, basis, piece_rows, _ = part_ref.shape
     first_chan = lax.axis_index("chan") * local_chans
     sky_index = lax.axis_index("sky")
     lane = lax.broadcasted_iota(jnp.int32, (rows, slot), 1)
     step = pl.program_id(0)
     if True:
-        xl, xc, xr = left_ref[:rows], xc_ref[...], right_ref[:rows]
+        xl, xc, xr = left_ref[:rows], xc_ref[:rows], right_ref[:rows]
         stacked = jnp.concatenate(
             [jnp.concatenate([xl, xc], axis=1), jnp.concatenate([xc, xr], axis=1)], axis=0
         )
@@ -136,8 +136,8 @@
     def packed(cols):
         return jnp.concatenate([cols[:, : row_count // 2], cols[:, row_count // 2 :]], axis=2)
 
-    model, dirty_r, dirty_l = lax.optimization_barrier(
-        (model, packed(dirty[:, :, slot_width - HALF :]), packed(dirty[:, :, :HALF]))
+    spectral, dirty_r, dirty_l = lax.optimization_barrier(
+        (spectral, packed(dirty[:, :, slot_width - HALF :]), packed(dirty[:, :, :HALF]))
     )
     model_full = lax.all_gather(model, "chan", axis=1, tiled=True)
     spec_local = lax.dynamic_slice_in_dim(spectral, lax.axis_index("chan") * local_chans, local_chans, 0)
@@ -176,7 +176,7 @@
             per_chan(dirty.shape),
             pl.BlockSpec((chan_count, basis, piece_rows, slot_width), lambda c: (0, 0, 0, 0)),
         ],
-    )(spectral, *bands, left, image, right, dirty)
+    )(spectral, *bands, left, to_right, right, dirty)
 
     pieces = lax.all_to_all(partial_value, "chan", 0, 0, tiled=True)
 

time: 34.2 us -> 32.8 us (0.959)
  local copies, waits for them, and re-layouts: 4.09 us -> 2.67 us
    unnamed x14, local copies, waits for them, and re-layouts: 2.79 us -> 1.37 us
  transfers between devices with their start and end apart: 2 -> 2, of which waited for: 1 -> 1; matrix products, arithmetic and copies ran while one was open for 3% -> 4% of each run, Pallas kernels for 10% -> 10%
where the time goes in v13:
time: 32.8 us; the launch traced here: 32.4 us
  Pallas kernels  8.38 us (26%)
  blocking collectives  7.49 us (23%)
  starting transfers between devices  6.07 us (19%)
  waiting for transfers between devices  4.7 us (14%)
  local copies, waits for them, and re-layouts  2.67 us (8%)
  other arithmetic  1.88 us (6%)
  between operations  0.76 us (2%)
  matrix products  0.42 us (1%)
    ppermute x2, starting transfers between devices, from_behind(): lax.ppermute(value, axis, [(source, source + steps) for source in range(f...  6.07 us
    all_to_all x1, blocking collectives, body(): pieces = lax.all_to_all(partial_value, 'chan', 0, 0, tiled=True)  5.23 us
    pallas_call x1, Pallas kernels, body(): pl.pallas_call(functools.partial(main_kernel, rank_count, local_chans, sk...  4.99 us
    ppermute x2, waiting for transfers between devices, from_behind(): lax.ppermute(value, axis, [(source, source + steps) for source in range(f...  4.7 us
    pallas_call x1, Pallas kernels, body(): pl.pallas_call(functools.partial(band_kernel, rank_count, local_chans, sl...  3.38 us
    all_gather x1, blocking collectives, body(): model_full = lax.all_gather(model, 'chan', axis=1, tiled=True)  2.26 us
    unnamed x14, local copies, waits for them, and re-layouts  1.37 us
    slice x1, local copies, waits for them, and re-layouts, packed(): cols[:, :row_count // 2]  1.05 us
  transfers between devices with their start and end apart: 2, of which 1 were waited for; matrix products, arithmetic and copies ran while one was open for 4% of the time, Pallas kernels for 10%

profile of v13, /device:TPU:0, one launch (start us, length us, event | category | flops | bytes accessed | tf_op | source)
XLA Modules:
  0.0 32.4 jit_solution(3171508059215419977)
XLA Ops:
  0.6 1.0 %fusion.1 = (bf16[2,128,64]{2,1,0:T(8,128)(2,1)S(1)}, bf16[2,128,64]{2,1,0:T(8,128)(2,1)S(1)}, bf16[2,128,64]{2,1,0:T(8,128)(2,1)S(1)}, bf16[2,128,64]{2,1,0:T(8,128)(2,1)S(1)}) fusion(bf16[2,256,128]{2,1,0:T(8,128)(2,1)} %dirty_ref.1), kind=kLoop, calls=%fused_computation.20 | loop fusion | bytes 262144 | tf_op jit(solution)/shard_map/slice | solution.py:137
  1.7 0.0 copy-start.1
  1.7 0.1 pad_maximum_fusion.2
  1.8 0.0 copy-start.6
  1.8 0.7 %copy-done.6 = f32[4,4]{1,0:T(4,128)S(1)} copy-done((f32[4,4]{1,0:T(4,128)S(1)}, f32[4,4]{1,0:T(4,128)}, u32[]{:S(2)}) %copy-start.6) | copy-done | bytes 88
  2.5 0.2 slice_reduce_fusion.3
  2.7 0.0 copy-done.1
  2.7 2.3 %all_gather.3 = f32[4,256,128]{2,1,0:T(8,128)S(1)} all-gather(f32[4,128,128]{2,1,0:T(8,128)S(1)} %copy-done.1), channel_id=1, replica_groups=mesh['chan'=2,'sky'=16] {'chan'}, dimensions={1}, use_global_device_ids=true | all-gather | bytes 786432 | tf_op jit(solution)/shard_map/all_gather | solution.py:142
  5.0 0.1 add_convert_fusion
  5.2 0.0 copy-start.4
  5.2 0.0 copy-start
  5.3 4.8 %collective-permute-start = (bf16[2,384,128]{2,1,0:T(8,128)(2,1)S(1)}, bf16[2,384,128]{2,1,0:T(8,128)(2,1)S(1)}, u32[]{:S(2)}, u32[]{:S(2)}) collective-permute-start(bf16[2,384,128]{2,1,0:T(8,128)(2,1)S(1)} %get-tuple-element.29.xc_ref), channel_id=1, source_target_pairs={{0,1},{1,2},{2,3},{3,4},{4,5},{5,6},{6,7},{7,8},{8,9},{9,10},{10,1... | collective-permute-start | bytes 589832 | tf_op jit(solution)/shard_map/ppermute | solution.py:18
  10.0 0.0 copy-start.5
  10.0 1.3 %collective-permute-start.1 = (bf16[2,384,128]{2,1,0:T(8,128)(2,1)S(1)}, bf16[2,384,128]{2,1,0:T(8,128)(2,1)S(1)}, u32[]{:S(2)}, u32[]{:S(2)}) collective-permute-start(bf16[2,384,128]{2,1,0:T(8,128)(2,1)S(1)} %get-tuple-element.28), channel_id=1, source_target_pairs={{1,0},{2,1},{3,2},{4,3},{5,4},{6,5},{7,6},{8,7},{9,8},{10,9},{11,1... | collective-permute-start | bytes 589832 | tf_op jit(solution)/shard_map/ppermute | solution.py:18
  11.3 0.0 copy-done.4
  11.4 0.2 fusion.2
  11.5 0.0 copy-done.5
  11.5 0.7 %select_maximum_fusion.taps_ref = f32[4,8,512]{2,1,0:T(8,128)} fusion(f32[4,4,129]{2,1,0:T(4,128)S(1)} %copy-done.5, f32[4,4,129]{2,1,0:T(4,128)S(1)} %copy-done.4), kind=kLoop, calls=%fused_computation.10 | loop fusion | flops 65536 | bytes 82048 | tf_op jit(solution)/shard_map/concatenate | solution.py:153
  12.2 3.4 %shard_map.68 = (bf16[2,256,512]{2,1,0:T(8,128)(2,1)}, bf16[2,4,256,256]{3,2,1,0:T(8,128)(2,1)}, bf16[2,256,512]{2,1,0:T(8,128)(2,1)}, bf16[2,4,256,256]{3,2,1,0:T(8,128)(2,1)}) custom-call(f32[4,8,512]{2,1,0:T(8,128)} %select_maximum_fusion.taps_ref), custom_call_target="tpu_custom_call" | custom-call | tf_op jit(solution)/shard_map/pallas_call | solution.py:161
  15.6 0.3 fusion
  15.8 0.1 multiply_reduce_fusion
  15.9 0.0 collective-permute-done.left_ref
  15.9 0.0 copy-start.2
  15.9 4.7 %collective-permute-done.1.right_ref = bf16[2,384,128]{2,1,0:T(8,128)(2,1)S(1)} collective-permute-done((bf16[2,384,128]{2,1,0:T(8,128)(2,1)S(1)}, bf16[2,384,128]{2,1,0:T(8,128)(2,1)S(1)}, u32[]{:S(2)}, u32[]{:S(2)}) %collective-permute-start.1) | collective-permute-done | bytes 196640 | tf_op jit(solution)/shard_map/ppermute | solution.py:18
  20.6 0.0 copy-start.3
  20.6 0.0 copy-done
  20.6 0.0 copy-done.2
  20.6 0.7 %copy-done.3 = bf16[2,384,128]{2,1,0:T(8,128)(2,1)} copy-done((bf16[2,384,128]{2,1,0:T(8,128)(2,1)}, bf16[2,384,128]{2,1,0:T(8,128)(2,1)S(1)}, u32[]{:S(2)}) %copy-start.3) | copy-done | bytes 196632
  21.3 5.0 %shard_map.69 = (bf16[2,256,128]{2,1,0:T(8,128)(2,1)}, f32[2,4,128,128]{3,2,1,0:T(8,128)}) custom-call(f32[4,4]{1,0:T(4,128)} %spec_ref, bf16[2,256,512]{2,1,0:T(8,128)(2,1)} %get-tuple-element.12.colf_ref, bf16[2,4,256,256]{3,2,1,0:T(8,128)(2,1)} %get-tuple-element.13.rowf_ref, bf16[2,256,512]{2,1,0:T(8,128)(2,1)} %get-tuple-element.14.cola_ref, ...), custom_call_target="tpu_custom_call" | custom-call | tf_op jit(solution)/shard_map/pallas_call | solution.py:167
  26.3 5.2 %all_to_all.5 = f32[2,4,128,128]{3,2,1,0:T(8,128)S(1)} all-to-all(f32[2,4,128,128]{3,2,1,0:T(8,128)} %get-tuple-element.19), channel_id=1, replica_groups=mesh['chan'=2,'sky'=16] {'chan'}, dimensions={0} | all-to-all | bytes 1048576 | tf_op jit(solution)/shard_map/all_to_all | solution.py:181
  31.6 0.8 %divide_add_fusion = f32[4,128,128]{2,1,0:T(8,128)} fusion(f32[4,128,128]{2,1,0:T(8,128)S(1)} %reduce_sum.27, f32[4,256,128]{2,1,0:T(8,128)S(1)} %all_gather.3, s32[]{:T(128)S(6)} %select_n.7, f32[4]{0:T(128)S(1)} %multiply_reduce_fusion), kind=kLoop, calls=%fused_computation.2 | loop fusion | flops 131072 | bytes 786452 | tf_op jit(solution)/shard_map/add | solution.py:188
  (4 shorter events, 0.1 us)
Async XLA Ops:
  1.7 1.0 %copy-start.1 = (f32[4,128,128]{2,1,0:T(8,128)S(1)}, f32[4,128,128]{2,1,0:T(8,128)}, u32[]{:S(2)}) copy-start(f32[4,128,128]{2,1,0:T(8,128)} %param.7) | copy-start | bytes 786436
  1.8 0.7 %copy-start.6 = (f32[4,4]{1,0:T(4,128)S(1)}, f32[4,4]{1,0:T(4,128)}, u32[]{:S(2)}) copy-start(f32[4,4]{1,0:T(4,128)} %spec_ref) | copy-start | bytes 196
  5.2 6.2 %copy-start.4 = (f32[4,4,129]{2,1,0:T(4,128)S(1)}, f32[4,4,129]{2,1,0:T(4,128)}, u32[]{:S(2)}) copy-start(f32[4,4,129]{2,1,0:T(4,128)} %param.9) | copy-start | bytes 24772
  5.2 15.4 %copy-start = (bf16[2,384,128]{2,1,0:T(8,128)(2,1)}, bf16[2,384,128]{2,1,0:T(8,128)(2,1)S(1)}, u32[]{:S(2)}) copy-start(bf16[2,384,128]{2,1,0:T(8,128)(2,1)S(1)} %get-tuple-element.29.xc_ref) | copy-start | bytes 589828
  5.3 10.7 %collective-permute-start = (bf16[2,384,128]{2,1,0:T(8,128)(2,1)S(1)}, bf16[2,384,128]{2,1,0:T(8,128)(2,1)S(1)}, u32[]{:S(2)}, u32[]{:S(2)}) collective-permute-start(bf16[2,384,128]{2,1,0:T(8,128)(2,1)S(1)} %get-tuple-element.29.xc_ref), channel_id=1, source_target_pairs={{0,1},{1,2},{2,3},{3,4},{4,5},{5,6},{6,7},{7,8},{8,9},{9,10},{10,1... | collective-permute-start | bytes 589832 | tf_op jit(solution)/shard_map/ppermute | solution.py:18
  10.0 1.5 %copy-start.5 = (f32[4,4,129]{2,1,0:T(4,128)S(1)}, f32[4,4,129]{2,1,0:T(4,128)}, u32[]{:S(2)}) copy-start(f32[4,4,129]{2,1,0:T(4,128)} %param.10) | copy-start | bytes 24772
  10.0 10.6 %collective-permute-start.1 = (bf16[2,384,128]{2,1,0:T(8,128)(2,1)S(1)}, bf16[2,384,128]{2,1,0:T(8,128)(2,1)S(1)}, u32[]{:S(2)}, u32[]{:S(2)}) collective-permute-start(bf16[2,384,128]{2,1,0:T(8,128)(2,1)S(1)} %get-tuple-element.28), channel_id=1, source_target_pairs={{1,0},{2,1},{3,2},{4,3},{5,4},{6,5},{7,6},{8,7},{9,8},{10,9},{11,1... | collective-permute-start | bytes 589832 | tf_op jit(solution)/shard_map/ppermute | solution.py:18
  15.9 4.7 %copy-start.2 = (bf16[2,384,128]{2,1,0:T(8,128)(2,1)}, bf16[2,384,128]{2,1,0:T(8,128)(2,1)S(1)}, u32[]{:S(2)}) copy-start(bf16[2,384,128]{2,1,0:T(8,128)(2,1)S(1)} %collective-permute-done.left_ref) | copy-start | bytes 589828
  20.6 0.7 %copy-start.3 = (bf16[2,384,128]{2,1,0:T(8,128)(2,1)}, bf16[2,384,128]{2,1,0:T(8,128)(2,1)S(1)}, u32[]{:S(2)}) copy-start(bf16[2,384,128]{2,1,0:T(8,128)(2,1)S(1)} %collective-permute-done.1.right_ref) | copy-start | bytes 589828
